TPU v7x, 256 devices: a whole 4x4x8 slice. The times are simulated.
256 devices in a mesh: batch: 16 (over z, core), wx: 4 (over y), wy: 4 (over x).
Axes of the slice: x: 4, y: 4, z: 8, core: 2. Of those that a mesh axis runs over, the one named last changes fastest.
Arguments:
- tokens: bfloat16 [8192, 16384], P(('batch', 'wx'), 'wy'), may hold values from -6 to 6
- routes: int32 [8192, 1], P(('batch', 'wx')), may hold values from 0 to 15; in each aligned block of 128 rows (0 to 127, 128 to 255, ...) at most 16 rows name the same one
- gate_weight: bfloat16 [16384, 2048], P('wy', 'wx'), may hold values from -0.046875 to 0.046875
- up_weight: bfloat16 [16384, 2048], P('wy', 'wx'), may hold values from -0.046875 to 0.046875
Outputs:
- hidden: bfloat16 [16384, 2048], P(('batch', 'wy'), 'wx')
Inputs may be any that keep to these rules, and one draw needn't show every extreme that they name: `routes`: among the tokens of one device, at most 16 share a group.
All inputs are finite; a program needn't handle non-finite values.
Results may differ from a plain program's by a relative error of at most 0.001.
Values may be sent and summed in bfloat16 or wider, within the bound.
No kernel may reach another device: no remote copies, remote signals or barrier semaphores. Data moves between devices by JAX's collectives and lax.ppermute only.
A program may use at most 128 MiB of HBM per device.

v0:
```python
import jax
import jax.numpy as jnp
from jax import lax
from jax.sharding import PartitionSpec as P


def place_rows(source, group_of, slots, groups_total):
    onehot = (group_of[:, None] == jnp.arange(groups_total, dtype=jnp.int32)[None, :]).astype(
        jnp.int32
    )
    ordinal = jnp.sum((jnp.cumsum(onehot, axis=0) - onehot) * onehot, axis=1)
    target = group_of * slots + ordinal
    chooser = (
        target[:, None] == jnp.arange(groups_total * slots, dtype=jnp.int32)[None, :]
    ).astype(jnp.bfloat16)
    placed = lax.dot_general(
        chooser, source, (((0,), (0,)), ((), ())), preferred_element_type=jnp.float32
    )
    return placed.astype(jnp.bfloat16)


def per_device(tokens, routes, gate_weight, up_weight):
    row_count = tokens.shape[0]
    width = tokens.shape[1]
    groups_total = lax.axis_size("batch")
    wx_count = lax.axis_size("wx")
    slots = 2 * row_count // groups_total
    gathered, group_all = (
        lax.all_gather(tokens, "wx", axis=0, tiled=True),
        lax.all_gather(routes, "wx", axis=0, tiled=True),
    )
    placed = jax.vmap(lambda source, group_of: place_rows(source, group_of, slots, groups_total))(
        gathered.reshape(wx_count, row_count, width), group_all.reshape(wx_count, row_count)
    )
    placed = placed.reshape(wx_count, groups_total, slots, width)
    arrived = lax.all_to_all(placed, "batch", split_axis=1, concat_axis=1, tiled=True)
    group_tokens = arrived.reshape(wx_count * groups_total * slots, width)
    gate = jnp.dot(group_tokens, gate_weight, preferred_element_type=jnp.float32)
    up = jnp.dot(group_tokens, up_weight, preferred_element_type=jnp.float32)
    gate_sum, up_sum = (
        lax.psum_scatter(gate, "wy", scatter_dimension=0, tiled=True),
        lax.psum_scatter(up, "wy", scatter_dimension=0, tiled=True),
    )
    return (jax.nn.silu(gate_sum) * up_sum).astype(jnp.bfloat16)


def solution(mesh):
    placed = (P(("batch", "wx"), "wy"), P(("batch", "wx"), None), P("wy", "wx"), P("wy", "wx"))
    return jax.shard_map(
        per_device, mesh=mesh, in_specs=placed, out_specs=P(("batch", "wy"), "wx"), check_vma=False
    )
```

profile of v0, /device:TPU:1, one launch (start us, length us, event | category | flops | bytes accessed | tf_op | source)
XLA Modules:
  0.0 360.0 jit_solution(9742043317204767281)
XLA Ops:
  6.5 0.0 all-gather.2.cloned.1.call-start
  6.5 0.7 all-gather.2.cloned.1.call-update
  7.3 0.0 reduce-scatter.3.cloned.1.call-start
  7.3 8.9 %all_gather.6 = s32[512,1]{0,1:T(1,128)S(1)} all-gather(s32[128,1]{0,1:T(1,128)} %param.5), channel_id=1, replica_groups=mesh['batch'=16,'wx'=4,'wy'=4] {'wx'}, dimensions={0}, use_global_device_ids=true | all-gather | bytes 2560 | tf_op jit(solution)/shard_map/all_gather | solution.py:30
  16.3 0.1 fusion.1
  16.4 0.3 reduce_window_sum.11
  16.7 0.2 select_reduce_fusion
  16.9 46.7 %all-gather.2.cloned.1.call-done = bf16[512,4096]{1,0:T(8,128)(2,1)} async-done(((bf16[128,4096]{1,0:T(8,128)(2,1)}), bf16[512,4096]{1,0:T(8,128)(2,1)}) %all-gather.2.cloned.1.call-update) | async-done | bytes 4194320 | tf_op jit(solution)/shard_map/all_gather | solution.py:29
  63.6 7.7 %convolution_convert_fusion = bf16[4,256,4096]{2,1,0:T(8,128)(2,1)} fusion(bf16[4,128,4096]{2,1,0:T(8,128)(2,1)} %bitcast.10, s32[4,128]{1,0:T(4,128)S(1)} %multiply_add_fusion), kind=kOutput, calls=%fused_computation | convolution fusion | flops 1078067200 | bytes 12584960 | tf_op jit(solution)/shard_map/vmap()/dot_general | solution.py:16
  71.3 7.7 %copy.6 = bf16[4,16,16,4096]{3,2,0,1:T(8,128)(2,1)} copy(bf16[4,16,16,4096]{3,2,1,0:T(8,128)(2,1)} %bitcast.9) | data formatting | bytes 16777216 | tf_op jit(solution)/shard_map/reshape | solution.py:35
  79.0 193.7 %all_to_all.5 = bf16[4,16,16,4096]{3,2,0,1:T(8,128)(2,1)} all-to-all(bf16[4,16,16,4096]{3,2,0,1:T(8,128)(2,1)} %copy.6), channel_id=1, replica_groups=mesh['batch'=16,'wx'=4,'wy'=4] {'batch'}, dimensions={1} | all-to-all | bytes 16777216 | tf_op jit(solution)/shard_map/all_to_all | solution.py:36
  272.7 0.0 copy-start
  272.7 7.9 %copy.7 = bf16[4,16,16,4096]{3,2,1,0:T(8,128)(2,1)} copy(bf16[4,16,16,4096]{3,2,0,1:T(8,128)(2,1)} %all_to_all.5) | data formatting | bytes 16777216 | tf_op jit(solution)/shard_map/all_to_all | solution.py:36
  280.6 0.0 copy-done
  280.6 8.3 %fusion.2 = f32[1024,512]{1,0:T(8,128)} fusion(bf16[1024,4096]{1,0:T(8,128)(2,1)} %bitcast.11, bf16[4096,512]{1,0:T(8,128)(2,1)S(1)} %copy-done), kind=kOutput, calls=%fused_computation.8 | convolution fusion | flops 4294967296 | bytes 14680064 | tf_op jit(solution)/shard_map/dot_general | solution.py:38
  288.9 0.0 reduce-scatter.3.cloned.1.call-update
  288.9 0.0 reduce-scatter.5.cloned.1.call-start
  288.9 10.4 %fusion.3 = f32[1024,512]{1,0:T(8,128)} fusion(bf16[1024,4096]{1,0:T(8,128)(2,1)} %bitcast.12, bf16[4096,512]{1,0:T(8,128)(2,1)} %param.7), kind=kOutput, calls=%fused_computation.9 | convolution fusion | flops 4294967296 | bytes 14680064 | tf_op jit(solution)/shard_map/dot_general | solution.py:39
  299.3 0.0 reduce-scatter.5.cloned.1.call-update
  299.3 17.5 %reduce-scatter.3.cloned.1.call-done = f32[256,512]{1,0:T(8,128)} async-done(((f32[1024,512]{1,0:T(8,128)}), f32[256,512]{1,0:T(8,128)}) %reduce-scatter.3.cloned.1.call-update) | async-done | bytes 524304 | tf_op jit(solution)/shard_map/reduce_scatter | solution.py:41
  316.9 34.6 %reduce-scatter.5.cloned.1.call-done = f32[256,512]{1,0:T(8,128)} async-done(((f32[1024,512]{1,0:T(8,128)}), f32[256,512]{1,0:T(8,128)}) %reduce-scatter.5.cloned.1.call-update) | async-done | bytes 524304 | tf_op jit(solution)/shard_map/reduce_scatter | solution.py:42
  351.4 2.1 multiply_convert_fusion
  (1 shorter events, 0.0 us)
Async XLA Ops:
  6.5 57.0 %all-gather.2.cloned.1.call-start = ((), (), s32[]{:S(2)}) async-start(), calls=%async_computation.3 | async-start | bytes 5242880 | tf_op jit(solution)/shard_map/all_gather | solution.py:29
  7.3 309.6 %reduce-scatter.3.cloned.1.call-start = ((), (), s32[]{:S(2)}) async-start(), calls=%async_computation.4 | async-start | bytes 2621440 | tf_op jit(solution)/shard_map/reduce_scatter | solution.py:41
  272.7 7.9 %copy-start = (bf16[4096,512]{1,0:T(8,128)(2,1)S(1)}, bf16[4096,512]{1,0:T(8,128)(2,1)}, u32[]{:S(2)}) copy-start(bf16[4096,512]{1,0:T(8,128)(2,1)} %param.6) | copy-start | bytes 12582916
  288.9 62.5 %reduce-scatter.5.cloned.1.call-start = ((), (), s32[]{:S(2)}) async-start(), calls=%async_computation.5 | async-start | bytes 2621440 | tf_op jit(solution)/shard_map/reduce_scatter | solution.py:42
Sparse Core Ops, SparseCore 0:
  9.1 54.3 all-gather.1
  289.0 27.8 reduce-scatter.2
  319.4 31.9 reduce-scatter.4
where the time goes:
time: 360 us
  blocking collectives  203 us (56%)
  waiting for transfers between devices  99.5 us (28%)
  matrix products  26.4 us (7%)
  local copies, waits for them, and re-layouts  15.6 us (4%)
  between operations  13.1 us (4%)
    all_to_all x1, blocking collectives, per_device(): lax.all_to_all(placed, 'batch', split_axis=1, concat_axis=1, tiled=True)  194 us
    all_gather x1, waiting for transfers between devices, per_device(): lax.all_gather(tokens, 'wx', axis=0, tiled=True)  46.7 us
    reduce_scatter x1, waiting for transfers between devices, per_device(): lax.psum_scatter(up, 'wy', scatter_dimension=0, tiled=True)  34.6 us
    reduce_scatter x1, waiting for transfers between devices, per_device(): lax.psum_scatter(gate, 'wy', scatter_dimension=0, tiled=True)  17.5 us
    dot_general x1, matrix products, per_device(): up = jnp.dot(group_tokens, up_weight, preferred_element_type=jnp.float32)  10.4 us
    all_gather x1, blocking collectives, per_device(): lax.all_gather(routes, 'wx', axis=0, tiled=True)  8.95 us
    dot_general x1, matrix products, per_device(): jnp.dot(group_tokens, gate_weight, preferred_element_type=jnp.float32)  8.3 us
    all_to_all x1, local copies, waits for them, and re-layouts, per_device(): lax.all_to_all(placed, 'batch', split_axis=1, concat_axis=1, tiled=True)  7.86 us
  transfers between devices with their start and end apart: 3, of which 3 were waited for; matrix products, arithmetic and copies ran while one was open for 3% of the time, Pallas kernels for 0%

commit v1 on v0

v1 whole, which is shorter than its diff:
```python
import jax
import jax.numpy as jnp
from jax import lax
from jax.sharding import PartitionSpec as P


def place_rows(source, group_of, slots, groups_total):
    onehot = (group_of[:, None] == jnp.arange(groups_total, dtype=jnp.int32)[None, :]).astype(
        jnp.int32
    )
    ordinal = jnp.sum((jnp.cumsum(onehot, axis=0) - onehot) * onehot, axis=1)
    target = group_of * slots + ordinal
    chooser = (
        target[:, None] == jnp.arange(groups_total * slots, dtype=jnp.int32)[None, :]
    ).astype(jnp.bfloat16)
    placed = lax.dot_general(
        chooser, source, (((0,), (0,)), ((), ())), preferred_element_type=jnp.float32
    )
    return placed.astype(jnp.bfloat16)


def per_device(tokens, routes, gate_weight, up_weight):
    row_count = tokens.shape[0]
    hid = gate_weight.shape[1]
    groups_total = lax.axis_size("batch")
    wx_count = lax.axis_size("wx")
    slots = 2 * row_count // groups_total
    gathered = lax.all_gather(tokens, "wx", axis=0, tiled=True)
    group_all = lax.all_gather(routes, "wx", axis=0, tiled=True)
    gate = jnp.dot(gathered, gate_weight, preferred_element_type=jnp.float32)
    up = jnp.dot(gathered, up_weight, preferred_element_type=jnp.float32)
    both = jnp.concatenate([gate, up], axis=1)
    summed = lax.psum_scatter(both, "wy", scatter_dimension=0, tiled=True)
    gate_sum, up_sum = summed[:, :hid], summed[:, hid:]
    hidden = (jax.nn.silu(gate_sum) * up_sum).astype(jnp.bfloat16)
    own = lax.axis_index("wy")
    group_of = lax.dynamic_slice_in_dim(group_all.reshape(wx_count, row_count), own, 1, 0)[0]
    placed = place_rows(hidden, group_of, slots, groups_total)
    placed = placed.reshape(groups_total, slots, hid)
    arrived = lax.all_to_all(placed, "batch", split_axis=0, concat_axis=0, tiled=True)
    return arrived.reshape(groups_total * slots, hid)


def solution(mesh):
    placed = (P(("batch", "wx"), "wy"), P(("batch", "wx"), None), P("wy", "wx"), P("wy", "wx"))
    return jax.shard_map(
        per_device, mesh=mesh, in_specs=placed, out_specs=P(("batch", "wy"), "wx"), check_vma=False
    )
```

time: 360 us -> 135 us (0.38)
  blocking collectives: 203 us -> 24.9 us
  matrix products: 26.4 us -> 9.68 us
  waiting for transfers between devices: 99.5 us -> 83.6 us
  local copies, waits for them, and re-layouts: 15.6 us -> 0.72 us
    all_to_all x1, blocking collectives: 194 us -> 19.1 us  [per_device(): lax.all_to_all(placed, 'batch', split_axis=0, concat_axis=0, tiled=True)]
    reduce_scatter x2 -> x1, waiting for transfers between devices: 52.1 us -> 26.6 us  [per_device(): summed = lax.psum_scatter(both, 'wy', scatter_dimension=0, tiled=True)]
    dot_general x2, matrix products: 18.7 us -> 8.34 us  [the longest x1 5.97 us: per_device(): up = jnp.dot(gathered, up_weight, preferred_element_type=jnp.float32)]
    all_gather x1, waiting for transfers between devices: 46.7 us -> 56.3 us  [per_device(): gathered = lax.all_gather(tokens, 'wx', axis=0, tiled=True)]
    all_to_all x1 -> x0, local copies, waits for them, and re-layouts: 7.86 us -> none  [per_device(): lax.all_to_all(placed, 'batch', split_axis=1, concat_axis=1, tiled=True)]
    reshape x1 -> x0, local copies, waits for them, and re-layouts: 7.7 us -> none  [per_device(): placed = placed.reshape(wx_count, groups_total, slots, width)]
    dot_general x1, matrix products: 7.73 us -> 1.35 us  [place_rows(): lax.dot_general(chooser, source, (((0,), (0,)), ((), ())), preferred_elem...]
  transfers between devices with their start and end apart: 3 -> 2, of which waited for: 3 -> 2; matrix products, arithmetic and copies ran while one was open for 3% -> 0% of each run, Pallas kernels for 0% -> 0%
where the time goes in v1:
time: 135 us; the launch traced here: 134 us
  waiting for transfers between devices  83.6 us (62%)
  blocking collectives  24.9 us (18%)
  between operations  13.5 us (10%)
  matrix products  9.68 us (7%)
  other arithmetic  1.96 us (1%)
    all_gather x1, waiting for transfers between devices, per_device(): gathered = lax.all_gather(tokens, 'wx', axis=0, tiled=True)  56.3 us
    reduce_scatter x1, waiting for transfers between devices, per_device(): summed = lax.psum_scatter(both, 'wy', scatter_dimension=0, tiled=True)  26.6 us
    all_to_all x1, blocking collectives, per_device(): lax.all_to_all(placed, 'batch', split_axis=0, concat_axis=0, tiled=True)  19.1 us
    dot_general x1, matrix products, per_device(): up = jnp.dot(gathered, up_weight, preferred_element_type=jnp.float32)  5.97 us
    all_gather x1, blocking collectives, per_device(): group_all = lax.all_gather(routes, 'wx', axis=0, tiled=True)  5.78 us
  transfers between devices with their start and end apart: 2, of which 2 were waited for; matrix products, arithmetic and copies ran while one was open for 0% of the time, Pallas kernels for 0%

profile of v1, /device:TPU:1, one launch (start us, length us, event | category | flops | bytes accessed | tf_op | source)
XLA Modules:
  0.0 134.4 jit_solution(3706500899102372639)
XLA Ops:
  6.5 0.0 all-gather.2.cloned.1.call-start
  6.5 0.7 all-gather.2.cloned.1.call-update
  7.3 0.0 reduce-scatter.2.cloned.1.call-start
  7.3 56.3 %all-gather.2.cloned.1.call-done = bf16[512,4096]{1,0:T(8,128)(2,1)} async-done(((bf16[128,4096]{1,0:T(8,128)(2,1)}), bf16[512,4096]{1,0:T(8,128)(2,1)}) %all-gather.2.cloned.1.call-update) | async-done | bytes 4194320 | tf_op jit(solution)/shard_map/all_gather | solution.py:28
  63.6 0.0 copy-start.1
  63.6 0.0 copy-start.2
  63.6 6.0 %fusion.8 = f32[512,512]{0,1:T(8,128)S(1)} fusion(bf16[512,4096]{1,0:T(8,128)(2,1)} %all-gather.2.cloned.1.call-done, bf16[4096,512]{1,0:T(8,128)(2,1)} %param.7), kind=kOutput, calls=%fused_computation.14 | convolution fusion | flops 2147483648 | bytes 9437184 | tf_op jit(solution)/shard_map/dot_general | solution.py:31
  69.6 0.0 copy-done.1
  69.6 0.0 copy-done.2
  69.6 2.4 %fusion.7 = f32[512,512]{0,1:T(8,128)S(1)} fusion(bf16[512,4096]{1,0:T(8,128)(2,1)S(1)} %copy-done.2, bf16[4096,512]{1,0:T(8,128)(2,1)S(1)} %copy-done.1), kind=kOutput, calls=%fused_computation.13 | convolution fusion | flops 2147483648 | bytes 9437184 | tf_op jit(solution)/shard_map/dot_general | solution.py:30
  72.0 0.0 copy-start
  72.0 1.5 %pad_maximum_fusion = f32[512,1024]{0,1:T(8,128)} fusion(f32[512,512]{0,1:T(8,128)S(1)} %fusion.8, f32[512,512]{0,1:T(8,128)S(1)} %fusion.7), kind=kLoop, calls=%fused_computation | loop fusion | flops 524288 | bytes 4194304 | tf_op jit(solution)/shard_map/concatenate | solution.py:32
  73.5 0.0 reduce-scatter.2.cloned.1.call-update
  73.5 0.0 copy-done
  73.5 5.8 %all_gather.6 = s32[512,1]{0,1:T(1,128)S(1)} all-gather(s32[128,1]{0,1:T(1,128)S(1)} %copy-done), channel_id=1, replica_groups=mesh['batch'=16,'wx'=4,'wy'=4] {'wx'}, dimensions={0}, use_global_device_ids=true | all-gather | bytes 2560 | tf_op jit(solution)/shard_map/all_gather | solution.py:29
  79.3 0.1 fusion.5
  79.4 0.2 reduce_window_sum.11
  79.6 0.2 select_reduce_fusion
  79.8 26.6 %reduce-scatter.2.cloned.1.call-done = f32[128,1024]{0,1:T(8,128)} async-done(((f32[512,1024]{0,1:T(8,128)}), f32[128,1024]{0,1:T(8,128)}) %reduce-scatter.2.cloned.1.call-update) | async-done | bytes 524304 | tf_op jit(solution)/shard_map/reduce_scatter | solution.py:33
  106.3 1.3 %convolution_convert_fusion = bf16[256,512]{1,0:T(8,128)(2,1)S(1)} fusion(f32[128,1024]{0,1:T(8,128)} %reduce-scatter.2.cloned.1.call-done, s32[128]{0:T(128)S(1)} %multiply_add_fusion), kind=kOutput, calls=%fused_computation.1 | convolution fusion | flops 34144256 | bytes 786944 | tf_op jit(solution)/shard_map/dot_general | solution.py:16
  107.7 19.1 %all_to_all.5 = bf16[16,16,512]{2,1,0:T(8,128)(2,1)S(1)} all-to-all(bf16[16,16,512]{2,1,0:T(8,128)(2,1)S(1)} %bitcast.12), channel_id=1, replica_groups=mesh['batch'=16,'wx'=4,'wy'=4] {'batch'}, dimensions={0} | all-to-all | bytes 524288 | tf_op jit(solution)/shard_map/all_to_all | solution.py:40
  126.8 0.7 copy.6
  (2 shorter events, 0.0 us)
Async XLA Ops:
  6.5 57.0 %all-gather.2.cloned.1.call-start = ((), (), s32[]{:S(2)}) async-start(), calls=%async_computation.2 | async-start | bytes 5242880 | tf_op jit(solution)/shard_map/all_gather | solution.py:28
  7.3 99.1 %reduce-scatter.2.cloned.1.call-start = ((), (), s32[]{:S(2)}) async-start(), calls=%async_computation.3 | async-start | bytes 2621440 | tf_op jit(solution)/shard_map/reduce_scatter | solution.py:33
  63.6 6.0 %copy-start.1 = (bf16[4096,512]{1,0:T(8,128)(2,1)S(1)}, bf16[4096,512]{1,0:T(8,128)(2,1)}, u32[]{:S(2)}) copy-start(bf16[4096,512]{1,0:T(8,128)(2,1)} %param.6) | copy-start | bytes 12582916
  63.6 6.0 %copy-start.2 = (bf16[512,4096]{1,0:T(8,128)(2,1)S(1)}, bf16[512,4096]{1,0:T(8,128)(2,1)}, u32[]{:S(2)}) copy-start(bf16[512,4096]{1,0:T(8,128)(2,1)} %all-gather.2.cloned.1.call-done) | copy-start | bytes 12582916
  72.0 1.6 %copy-start = (s32[128,1]{0,1:T(1,128)S(1)}, s32[128,1]{0,1:T(1,128)}, u32[]{:S(2)}) copy-start(s32[128,1]{0,1:T(1,128)} %param.5) | copy-start | bytes 1540
Sparse Core Ops, SparseCore 0:
  9.1 54.3 all-gather.1
  73.6 32.6 reduce-scatter.1

commit v2 on v1

--- a/solution.py
+++ b/solution.py
@@ -19,22 +19,46 @@
     return placed.astype(jnp.bfloat16)
 
 
+def shift(value, axis, count, step):
+    return lax.ppermute(value, axis, [(i, (i + step) % count) for i in range(count)])
+
+
 def per_device(tokens, routes, gate_weight, up_weight):
     row_count = tokens.shape[0]
     hid = gate_weight.shape[1]
     groups_total = lax.axis_size("batch")
-    wx_count = lax.axis_size("wx")
+    nx = lax.axis_size("wx")
+    ny = lax.axis_size("wy")
+    assert nx == 4 and ny == 4
     slots = 2 * row_count // groups_total
-    gathered = lax.all_gather(tokens, "wx", axis=0, tiled=True)
-    group_all = lax.all_gather(routes, "wx", axis=0, tiled=True)
-    gate = jnp.dot(gathered, gate_weight, preferred_element_type=jnp.float32)
-    up = jnp.dot(gathered, up_weight, preferred_element_type=jnp.float32)
-    both = jnp.concatenate([gate, up], axis=1)
-    summed = lax.psum_scatter(both, "wy", scatter_dimension=0, tiled=True)
-    gate_sum, up_sum = summed[:, :hid], summed[:, hid:]
+    half = row_count // 2
+    x = lax.axis_index("wx")
+    y = lax.axis_index("wy")
+
+    pairs = [(w * ny + v, v * ny + w) for w in range(nx) for v in range(ny)]
+    group_of = lax.ppermute(routes, ("wx", "wy"), pairs)[:, 0]
+
+    def partial(rows):
+        gate = jnp.dot(rows, gate_weight, preferred_element_type=jnp.float32)
+        up = jnp.dot(rows, up_weight, preferred_element_type=jnp.float32)
+        return jnp.concatenate([gate, up], axis=1)
+
+    from_left = shift(tokens, "wx", nx, 1)
+    from_right = shift(tokens, "wx", nx, -1)
+    part_own = partial(tokens)
+    far_a = shift(from_left[:half], "wx", nx, 1)
+    far_b = shift(from_right[half:], "wx", nx, -1)
+    part_left = partial(from_left)
+    part_right = partial(from_right)
+    part_far = jnp.concatenate([partial(far_a), partial(far_b)], axis=0)
+    parts = jnp.stack([part_own, part_right, part_far, part_left])
+
+    total = lax.dynamic_index_in_dim(parts, (y - x) % nx, 0, keepdims=False)
+    for d in (1, 2, 3):
+        send = lax.dynamic_index_in_dim(parts, (y + d - x) % nx, 0, keepdims=False)
+        total = total + shift(send, "wy", ny, d)
+    gate_sum, up_sum = total[:, :hid], total[:, hid:]
     hidden = (jax.nn.silu(gate_sum) * up_sum).astype(jnp.bfloat16)
-    own = lax.axis_index("wy")
-    group_of = lax.dynamic_slice_in_dim(group_all.reshape(wx_count, row_count), own, 1, 0)[0]
     placed = place_rows(hidden, group_of, slots, groups_total)
     placed = placed.reshape(groups_total, slots, hid)
     arrived = lax.all_to_all(placed, "batch", split_axis=0, concat_axis=0, tiled=True)

time: 135 us -> 95.1 us (0.70)
  waiting for transfers between devices: 83.6 us -> 41.5 us
  starting transfers between devices: 0.04 us -> 15.1 us
  between operations: 13.5 us -> 0.19 us
  blocking collectives: 24.9 us -> 23 us
  local copies, waits for them, and re-layouts: 0.72 us -> 2.1 us
    all_gather x1 -> x0, waiting for transfers between devices: 56.3 us -> none  [per_device(): gathered = lax.all_gather(tokens, 'wx', axis=0, tiled=True)]
    ppermute x0 -> x8, waiting for transfers between devices: none -> 41.5 us  [the longest x7 41.5 us: shift(): lax.ppermute(value, axis, [(i, (i + step) % count) for i in range(count)])]
    reduce_scatter x1 -> x0, waiting for transfers between devices: 26.6 us -> none  [per_device(): summed = lax.psum_scatter(both, 'wy', scatter_dimension=0, tiled=True)]
    ppermute x0 -> x8, starting transfers between devices: none -> 15.1 us  [the longest x7 13.8 us: shift(): lax.ppermute(value, axis, [(i, (i + step) % count) for i in range(count)])]
    all_gather x1 -> x0, blocking collectives: 5.78 us -> none  [per_device(): group_all = lax.all_gather(routes, 'wx', axis=0, tiled=True)]
    all_to_all x1, blocking collectives: 19.1 us -> 23 us  [per_device(): lax.all_to_all(placed, 'batch', split_axis=0, concat_axis=0, tiled=True)]
    dot_general x2 -> x10, matrix products: 8.34 us -> 10.5 us  [the longest x5 6.57 us: partial(): up = jnp.dot(rows, up_weight, preferred_element_type=jnp.float32)]
    concatenate x1 -> x0, other arithmetic: 1.52 us -> none  [per_device(): both = jnp.concatenate([gate, up], axis=1)]
  transfers between devices with their start and end apart: 2 -> 8, of which waited for: 2 -> 4; matrix products, arithmetic and copies ran while one was open for 0% -> 13% of each run, Pallas kernels for 0% -> 0%
where the time goes in v2:
time: 95.1 us; the launch traced here: 95 us
  waiting for transfers between devices  41.5 us (44%)
  blocking collectives  23 us (24%)
  starting transfers between devices  15.1 us (16%)
  matrix products  10.9 us (11%)
  other arithmetic  2.23 us (2%)
  local copies, waits for them, and re-layouts  2.1 us (2%)
    ppermute x7, waiting for transfers between devices, shift(): lax.ppermute(value, axis, [(i, (i + step) % count) for i in range(count)])  41.5 us
    all_to_all x1, blocking collectives, per_device(): lax.all_to_all(placed, 'batch', split_axis=0, concat_axis=0, tiled=True)  23 us
    ppermute x7, starting transfers between devices, shift(): lax.ppermute(value, axis, [(i, (i + step) % count) for i in range(count)])  13.8 us
    dot_general x5, matrix products, partial(): up = jnp.dot(rows, up_weight, preferred_element_type=jnp.float32)  6.57 us
    dot_general x5, matrix products, partial(): gate = jnp.dot(rows, gate_weight, preferred_element_type=jnp.float32)  3.97 us
  transfers between devices with their start and end apart: 8, of which 4 were waited for; matrix products, arithmetic and copies ran while one was open for 13% of the time, Pallas kernels for 0%

profile of v2, /device:TPU:1, one launch (start us, length us, event | category | flops | bytes accessed | tf_op | source)
XLA Modules:
  0.0 95.0 jit_solution(12202384333544344961)
XLA Ops:
  0.0 2.1 %collective-permute-start.2 = (bf16[128,4096]{1,0:T(8,128)(2,1)}, bf16[128,4096]{1,0:T(8,128)(2,1)S(1)}, u32[]{:S(2)}, u32[]{:S(2)}) collective-permute-start(bf16[128,4096]{1,0:T(8,128)(2,1)} %param.4), channel_id=1, source_target_pairs={{0,4},{4,8},{8,12},{12,0},{1,5},{5,9},{9,13},{13,1},{2,6},{6,10},{... | collective-permute-start | bytes 3145736 | tf_op jit(solution)/shard_map/ppermute | solution.py:23
  2.1 1.5 %collective-permute-start.1 = (bf16[128,4096]{1,0:T(8,128)(2,1)}, bf16[128,4096]{1,0:T(8,128)(2,1)S(1)}, u32[]{:S(2)}, u32[]{:S(2)}) collective-permute-start(bf16[128,4096]{1,0:T(8,128)(2,1)} %param.4), channel_id=1, source_target_pairs={{0,12},{4,0},{8,4},{12,8},{1,13},{5,1},{9,5},{13,9},{2,14},{6,2},{... | collective-permute-start | bytes 3145736 | tf_op jit(solution)/shard_map/ppermute | solution.py:23
  3.6 1.3 %collective-permute-start = (s32[128,1]{0,1:T(1,128)}, s32[128,1]{0,1:T(1,128)S(1)}, u32[]{:S(2)}, u32[]{:S(2)}) collective-permute-start(s32[128,1]{0,1:T(1,128)} %param.5), channel_id=1, source_target_pairs={{0,0},{1,4},{2,8},{3,12},{4,1},{5,5},{6,9},{7,13},{8,2},{9,6},{10,... | collective-permute-start | bytes 1544 | tf_op jit(solution)/shard_map/ppermute | solution.py:39
  4.9 3.4 %fusion.9 = f32[128,512]{1,0:T(8,128)S(1)} fusion(bf16[128,4096]{1,0:T(8,128)(2,1)} %param.4, bf16[4096,512]{1,0:T(8,128)(2,1)} %param.7), kind=kOutput, calls=%fused_computation.23 | convolution fusion | flops 536870912 | bytes 5505024 | tf_op jit(solution)/shard_map/dot_general | solution.py:43
  8.7 0.8 fusion.8
  9.5 15.3 %collective-permute-done.2 = bf16[128,4096]{1,0:T(8,128)(2,1)S(1)} collective-permute-done((bf16[128,4096]{1,0:T(8,128)(2,1)}, bf16[128,4096]{1,0:T(8,128)(2,1)S(1)}, u32[]{:S(2)}, u32[]{:S(2)}) %collective-permute-start.2) | collective-permute-done | bytes 1048608 | tf_op jit(solution)/shard_map/ppermute | solution.py:23
  24.9 1.4 %collective-permute-start.3 = (bf16[64,4096]{1,0:T(8,128)(2,1)S(1)}, bf16[64,4096]{1,0:T(8,128)(2,1)S(1)}, u32[]{:S(2)}, u32[]{:S(2)}) collective-permute-start(bf16[64,4096]{1,0:T(8,128)(2,1)S(1)} %slice.16), channel_id=1, source_target_pairs={{0,4},{4,8},{8,12},{12,0},{1,5},{5,9},{9,13},{13,1},{2,6},{6,10},{... | collective-permute-start | bytes 1572872 | tf_op jit(solution)/shard_map/ppermute | solution.py:23
  26.3 1.7 %collective-permute-start.4 = (bf16[64,4096]{1,0:T(8,128)(2,1)S(1)}, bf16[64,4096]{1,0:T(8,128)(2,1)S(1)}, u32[]{:S(2)}, u32[]{:S(2)}) collective-permute-start(bf16[64,4096]{1,0:T(8,128)(2,1)S(1)} %slice.17), channel_id=1, source_target_pairs={{0,12},{4,0},{8,4},{12,8},{1,13},{5,1},{9,5},{13,9},{2,14},{6,2},{... | collective-permute-start | bytes 1572872 | tf_op jit(solution)/shard_map/ppermute | solution.py:23
  28.9 0.8 fusion.16
  29.6 0.8 fusion.11
  30.5 0.8 fusion.10
  31.3 5.9 %collective-permute-done.3 = bf16[64,4096]{1,0:T(8,128)(2,1)S(1)} collective-permute-done((bf16[64,4096]{1,0:T(8,128)(2,1)S(1)}, bf16[64,4096]{1,0:T(8,128)(2,1)S(1)}, u32[]{:S(2)}, u32[]{:S(2)}) %collective-permute-start.3) | collective-permute-done | bytes 524320 | tf_op jit(solution)/shard_map/ppermute | solution.py:23
  37.1 0.8 fusion.13
  38.0 0.8 fusion.12
  38.8 0.8 fusion.15
  39.7 0.8 fusion.14
  40.7 1.0 %dynamic-slice_bitcast_fusion.2 = (f32[128,1024]{1,0:T(8,128)}, f32[128,1024]{1,0:T(8,128)S(1)}, f32[128,1024]{1,0:T(8,128)S(1)}) fusion(f32[4,128,1024]{2,1,0:T(8,128)S(1)} %pad_maximum_fusion, s32[]{:T(128)S(6)} %select_n.35, s32[]{:T(128)S(6)} %select_n.39, s32[]{:T(128)S(6)} %select_n.37), kind=kLoop, calls=%fused_computation.11 | loop fusion | bytes 3145740 | tf_op jit(solution)/shard_map/jit(dynamic_index_in_dim)/squeeze | solution.py:58
  41.7 4.0 %collective-permute-start.5 = (f32[128,1024]{1,0:T(8,128)}, f32[128,1024]{1,0:T(8,128)}, u32[]{:S(2)}, u32[]{:S(2)}) collective-permute-start(f32[128,1024]{1,0:T(8,128)} %get-tuple-element.5), channel_id=1, source_target_pairs={{0,1},{1,2},{2,3},{3,0},{4,5},{5,6},{6,7},{7,4},{8,9},{9,10},{10,1... | collective-permute-start | bytes 1572872 | tf_op jit(solution)/shard_map/ppermute | solution.py:23
  45.7 1.3 %collective-permute-start.7 = (f32[128,1024]{1,0:T(8,128)S(1)}, f32[128,1024]{1,0:T(8,128)}, u32[]{:S(2)}, u32[]{:S(2)}) collective-permute-start(f32[128,1024]{1,0:T(8,128)S(1)} %get-tuple-element.6), channel_id=1, source_target_pairs={{0,3},{1,0},{2,1},{3,2},{4,7},{5,4},{6,5},{7,6},{8,11},{9,8},{10,9... | collective-permute-start | bytes 1572872 | tf_op jit(solution)/shard_map/ppermute | solution.py:23
  47.0 1.7 %collective-permute-start.6 = (f32[128,1024]{1,0:T(8,128)S(1)}, f32[128,1024]{1,0:T(8,128)}, u32[]{:S(2)}, u32[]{:S(2)}) collective-permute-start(f32[128,1024]{1,0:T(8,128)S(1)} %get-tuple-element.7), channel_id=1, source_target_pairs={{0,2},{1,3},{2,0},{3,1},{4,6},{5,7},{6,4},{7,5},{8,10},{9,11},{10,... | collective-permute-start | bytes 1572872 | tf_op jit(solution)/shard_map/ppermute | solution.py:23
  49.2 8.2 %collective-permute-done.5 = f32[128,1024]{1,0:T(8,128)} collective-permute-done((f32[128,1024]{1,0:T(8,128)}, f32[128,1024]{1,0:T(8,128)}, u32[]{:S(2)}, u32[]{:S(2)}) %collective-permute-start.5) | collective-permute-done | bytes 524320 | tf_op jit(solution)/shard_map/ppermute | solution.py:23
  57.3 12.1 %collective-permute-done.6 = f32[128,1024]{1,0:T(8,128)} collective-permute-done((f32[128,1024]{1,0:T(8,128)S(1)}, f32[128,1024]{1,0:T(8,128)}, u32[]{:S(2)}, u32[]{:S(2)}) %collective-permute-start.6) | collective-permute-done | bytes 524320 | tf_op jit(solution)/shard_map/ppermute | solution.py:23
  69.5 1.5 %fusion.1 = f32[128,1024]{1,0:T(8,128)S(1)} fusion(f32[128,1024]{1,0:T(8,128)} %collective-permute-done.7, f32[128,1024]{1,0:T(8,128)} %collective-permute-done.6, f32[128,1024]{1,0:T(8,128)} %collective-permute-done.5, f32[4,128,1024]{2,1,0:T(8,128)S(1)} %pad_maximum_fusion, s32[]{:T(128)S(6)} %select_n.33), kind=kLoop, calls=%fused_computation.8 | loop fusion | flops 393216 | bytes 2621444 | tf_op jit(solution)/shard_map/add | solution.py:59
  71.3 23.0 %all_to_all.5 = bf16[16,16,512]{2,1,0:T(8,128)(2,1)S(1)} all-to-all(bf16[16,16,512]{2,1,0:T(8,128)(2,1)S(1)} %bitcast.50), channel_id=1, replica_groups=mesh['batch'=16,'wx'=4,'wy'=4] {'batch'}, dimensions={0} | all-to-all | bytes 524288 | tf_op jit(solution)/shard_map/all_to_all | solution.py:64
  (24 shorter events, 3.0 us)
Async XLA Ops:
  0.0 8.3 %copy-start.2 = (bf16[128,4096]{1,0:T(8,128)(2,1)S(1)}, bf16[128,4096]{1,0:T(8,128)(2,1)}, u32[]{:S(2)}) copy-start(bf16[128,4096]{1,0:T(8,128)(2,1)} %param.4) | copy-start | bytes 3145732
  0.0 24.8 %collective-permute-start.2 = (bf16[128,4096]{1,0:T(8,128)(2,1)}, bf16[128,4096]{1,0:T(8,128)(2,1)S(1)}, u32[]{:S(2)}, u32[]{:S(2)}) collective-permute-start(bf16[128,4096]{1,0:T(8,128)(2,1)} %param.4), channel_id=1, source_target_pairs={{0,4},{4,8},{8,12},{12,0},{1,5},{5,9},{9,13},{13,1},{2,6},{6,10},{... | collective-permute-start | bytes 3145736 | tf_op jit(solution)/shard_map/ppermute | solution.py:23
  2.1 24.2 %collective-permute-start.1 = (bf16[128,4096]{1,0:T(8,128)(2,1)}, bf16[128,4096]{1,0:T(8,128)(2,1)S(1)}, u32[]{:S(2)}, u32[]{:S(2)}) collective-permute-start(bf16[128,4096]{1,0:T(8,128)(2,1)} %param.4), channel_id=1, source_target_pairs={{0,12},{4,0},{8,4},{12,8},{1,13},{5,1},{9,5},{13,9},{2,14},{6,2},{... | collective-permute-start | bytes 3145736 | tf_op jit(solution)/shard_map/ppermute | solution.py:23
  3.6 45.1 %collective-permute-start = (s32[128,1]{0,1:T(1,128)}, s32[128,1]{0,1:T(1,128)S(1)}, u32[]{:S(2)}, u32[]{:S(2)}) collective-permute-start(s32[128,1]{0,1:T(1,128)} %param.5), channel_id=1, source_target_pairs={{0,0},{1,4},{2,8},{3,12},{4,1},{5,5},{6,9},{7,13},{8,2},{9,6},{10,... | collective-permute-start | bytes 1544 | tf_op jit(solution)/shard_map/ppermute | solution.py:39
  4.9 3.7 %copy-start.1 = (bf16[4096,512]{1,0:T(8,128)(2,1)S(1)}, bf16[4096,512]{1,0:T(8,128)(2,1)}, u32[]{:S(2)}) copy-start(bf16[4096,512]{1,0:T(8,128)(2,1)} %param.6) | copy-start | bytes 12582916
  8.7 19.4 %copy-start = (bf16[4096,512]{1,0:T(8,128)(2,1)S(1)}, bf16[4096,512]{1,0:T(8,128)(2,1)}, u32[]{:S(2)}) copy-start(bf16[4096,512]{1,0:T(8,128)(2,1)} %param.7) | copy-start | bytes 12582916
  24.9 12.3 %collective-permute-start.3 = (bf16[64,4096]{1,0:T(8,128)(2,1)S(1)}, bf16[64,4096]{1,0:T(8,128)(2,1)S(1)}, u32[]{:S(2)}, u32[]{:S(2)}) collective-permute-start(bf16[64,4096]{1,0:T(8,128)(2,1)S(1)} %slice.16), channel_id=1, source_target_pairs={{0,4},{4,8},{8,12},{12,0},{1,5},{5,9},{9,13},{13,1},{2,6},{6,10},{... | collective-permute-start | bytes 1572872 | tf_op jit(solution)/shard_map/ppermute | solution.py:23
  26.3 12.5 %collective-permute-start.4 = (bf16[64,4096]{1,0:T(8,128)(2,1)S(1)}, bf16[64,4096]{1,0:T(8,128)(2,1)S(1)}, u32[]{:S(2)}, u32[]{:S(2)}) collective-permute-start(bf16[64,4096]{1,0:T(8,128)(2,1)S(1)} %slice.17), channel_id=1, source_target_pairs={{0,12},{4,0},{8,4},{12,8},{1,13},{5,1},{9,5},{13,9},{2,14},{6,2},{... | collective-permute-start | bytes 1572872 | tf_op jit(solution)/shard_map/ppermute | solution.py:23
  41.7 15.7 %collective-permute-start.5 = (f32[128,1024]{1,0:T(8,128)}, f32[128,1024]{1,0:T(8,128)}, u32[]{:S(2)}, u32[]{:S(2)}) collective-permute-start(f32[128,1024]{1,0:T(8,128)} %get-tuple-element.5), channel_id=1, source_target_pairs={{0,1},{1,2},{2,3},{3,0},{4,5},{5,6},{6,7},{7,4},{8,9},{9,10},{10,1... | collective-permute-start | bytes 1572872 | tf_op jit(solution)/shard_map/ppermute | solution.py:23
  45.7 11.6 %collective-permute-start.7 = (f32[128,1024]{1,0:T(8,128)S(1)}, f32[128,1024]{1,0:T(8,128)}, u32[]{:S(2)}, u32[]{:S(2)}) collective-permute-start(f32[128,1024]{1,0:T(8,128)S(1)} %get-tuple-element.6), channel_id=1, source_target_pairs={{0,3},{1,0},{2,1},{3,2},{4,7},{5,4},{6,5},{7,6},{8,11},{9,8},{10,9... | collective-permute-start | bytes 1572872 | tf_op jit(solution)/shard_map/ppermute | solution.py:23
  47.0 22.5 %collective-permute-start.6 = (f32[128,1024]{1,0:T(8,128)S(1)}, f32[128,1024]{1,0:T(8,128)}, u32[]{:S(2)}, u32[]{:S(2)}) collective-permute-start(f32[128,1024]{1,0:T(8,128)S(1)} %get-tuple-element.7), channel_id=1, source_target_pairs={{0,2},{1,3},{2,0},{3,1},{4,6},{5,7},{6,4},{7,5},{8,10},{9,11},{10,... | collective-permute-start | bytes 1572872 | tf_op jit(solution)/shard_map/ppermute | solution.py:23

commit v3 on v2

--- a/solution.py
+++ b/solution.py
@@ -32,34 +32,48 @@
     assert nx == 4 and ny == 4
     slots = 2 * row_count // groups_total
     half = row_count // 2
+    quarter = hid // ny
     x = lax.axis_index("wx")
     y = lax.axis_index("wy")
 
     pairs = [(w * ny + v, v * ny + w) for w in range(nx) for v in range(ny)]
     group_of = lax.ppermute(routes, ("wx", "wy"), pairs)[:, 0]
 
+    w_all = jnp.concatenate(
+        [m[:, j * quarter:(j + 1) * quarter] for j in range(ny) for m in (gate_weight, up_weight)],
+        axis=1,
+    )
+
     def partial(rows):
-        gate = jnp.dot(rows, gate_weight, preferred_element_type=jnp.float32)
-        up = jnp.dot(rows, up_weight, preferred_element_type=jnp.float32)
-        return jnp.concatenate([gate, up], axis=1)
+        out = jnp.dot(rows, w_all, preferred_element_type=jnp.float32)
+        return out.reshape(rows.shape[0], ny, 2 * quarter).transpose(1, 0, 2)
+
+    def reduce(parts):
+        total = lax.dynamic_index_in_dim(parts, y, 0, keepdims=False)
+        for d in range(1, ny):
+            send = lax.dynamic_index_in_dim(parts, (y + d) % ny, 0, keepdims=False)
+            total = total + shift(send, "wy", ny, d)
+        return total
 
     from_left = shift(tokens, "wx", nx, 1)
     from_right = shift(tokens, "wx", nx, -1)
-    part_own = partial(tokens)
+    sum_own = reduce(partial(tokens))
     far_a = shift(from_left[:half], "wx", nx, 1)
     far_b = shift(from_right[half:], "wx", nx, -1)
-    part_left = partial(from_left)
-    part_right = partial(from_right)
-    part_far = jnp.concatenate([partial(far_a), partial(far_b)], axis=0)
-    parts = jnp.stack([part_own, part_right, part_far, part_left])
+    sum_sides = reduce(jnp.concatenate([partial(from_left), partial(from_right)], axis=1))
+    sum_far = reduce(jnp.concatenate([partial(far_a), partial(far_b)], axis=1))
+    sums = jnp.stack([sum_own, sum_sides[row_count:], sum_far, sum_sides[:row_count]])
+    hidden = (jax.nn.silu(sums[..., :quarter]) * sums[..., quarter:]).astype(jnp.bfloat16)
 
-    total = lax.dynamic_index_in_dim(parts, (y - x) % nx, 0, keepdims=False)
-    for d in (1, 2, 3):
-        send = lax.dynamic_index_in_dim(parts, (y + d - x) % nx, 0, keepdims=False)
-        total = total + shift(send, "wy", ny, d)
-    gate_sum, up_sum = total[:, :hid], total[:, hid:]
-    hidden = (jax.nn.silu(gate_sum) * up_sum).astype(jnp.bfloat16)
-    placed = place_rows(hidden, group_of, slots, groups_total)
+    got = [lax.dynamic_index_in_dim(hidden, (y - x) % nx, 0, keepdims=False)]
+    for d in range(1, ny):
+        send = lax.dynamic_index_in_dim(hidden, (y + d - x) % nx, 0, keepdims=False)
+        got.append(shift(send, "wy", ny, d))
+    by_shift = jnp.stack(got)
+    quarters = jnp.take(by_shift, (y - jnp.arange(ny)) % ny, axis=0)
+    block = quarters.transpose(1, 0, 2).reshape(row_count, hid)
+
+    placed = place_rows(block, group_of, slots, groups_total)
     placed = placed.reshape(groups_total, slots, hid)
     arrived = lax.all_to_all(placed, "batch", split_axis=0, concat_axis=0, tiled=True)
     return arrived.reshape(groups_total * slots, hid)

time: 95.1 us -> 119 us (1.25)
  waiting for transfers between devices: 41.5 us -> 15.8 us
  local copies, waits for them, and re-layouts: 2.1 us -> 20.5 us
  matrix products: 10.9 us -> 28 us
  starting transfers between devices: 15.1 us -> 24.6 us
  blocking collectives: 23 us -> 27.7 us
    ppermute x7 -> x16, waiting for transfers between devices: 41.5 us -> 15.8 us  [shift(): lax.ppermute(value, axis, [(i, (i + step) % count) for i in range(count)])]
    dot_general x10 -> x5, matrix products: 10.5 us -> 27.7 us  [partial(): out = jnp.dot(rows, w_all, preferred_element_type=jnp.float32)]
    unnamed x7 -> x16, local copies, waits for them, and re-layouts: 1.07 us -> 14.5 us
    ppermute x7 -> x16, starting transfers between devices: 13.8 us -> 23.9 us  [shift(): lax.ppermute(value, axis, [(i, (i + step) % count) for i in range(count)])]
    all_to_all x1, blocking collectives: 23 us -> 27.7 us  [per_device(): lax.all_to_all(placed, 'batch', split_axis=0, concat_axis=0, tiled=True)]
    another operation x0 -> x6, local copies, waits for them, and re-layouts: none -> 2.41 us
    add x1, other arithmetic: 1.5 us -> 0.07 us  [reduce(): total = total + shift(send, 'wy', ny, d)]
    concatenate x0 -> x1, local copies, waits for them, and re-layouts: none -> 1.19 us  [per_device(): jnp.concatenate([m[:, j * quarter:(j + 1) * quarter] for j in range(ny) f...]
  transfers between devices with their start and end apart: 8 -> 17, of which waited for: 4 -> 7; matrix products, arithmetic and copies ran while one was open for 13% -> 36% of each run, Pallas kernels for 0% -> 0%
where the time goes in v3:
time: 119 us
  matrix products  28 us (24%)
  blocking collectives  27.7 us (23%)
  starting transfers between devices  24.6 us (21%)
  local copies, waits for them, and re-layouts  20.5 us (17%)
  waiting for transfers between devices  15.8 us (13%)
  other arithmetic  1.9 us (2%)
    dot_general x5, matrix products, partial(): out = jnp.dot(rows, w_all, preferred_element_type=jnp.float32)  27.7 us
    all_to_all x1, blocking collectives, per_device(): lax.all_to_all(placed, 'batch', split_axis=0, concat_axis=0, tiled=True)  27.7 us
    ppermute x16, starting transfers between devices, shift(): lax.ppermute(value, axis, [(i, (i + step) % count) for i in range(count)])  23.9 us
    ppermute x16, waiting for transfers between devices, shift(): lax.ppermute(value, axis, [(i, (i + step) % count) for i in range(count)])  15.8 us
    unnamed x16, local copies, waits for them, and re-layouts  14.5 us
    another operation x5, local copies, waits for them, and re-layouts  2.39 us
  transfers between devices with their start and end apart: 17, of which 7 were waited for; matrix products, arithmetic and copies ran while one was open for 36% of the time, Pallas kernels for 0%

profile of v3, /device:TPU:1, one launch (start us, length us, event | category | flops | bytes accessed | tf_op | source)
XLA Modules:
  0.0 118.9 jit_solution(2161178954393071383)
XLA Ops:
  0.0 2.1 %collective-permute-start.4 = (bf16[128,4096]{1,0:T(8,128)(2,1)}, bf16[128,4096]{1,0:T(8,128)(2,1)S(1)}, u32[]{:S(2)}, u32[]{:S(2)}) collective-permute-start(bf16[128,4096]{1,0:T(8,128)(2,1)} %param.4), channel_id=1, source_target_pairs={{0,4},{4,8},{8,12},{12,0},{1,5},{5,9},{9,13},{13,1},{2,6},{6,10},{... | collective-permute-start | bytes 3145736 | tf_op jit(solution)/shard_map/ppermute | solution.py:23
  2.1 1.4 %collective-permute-start.5 = (bf16[128,4096]{1,0:T(8,128)(2,1)}, bf16[128,4096]{1,0:T(8,128)(2,1)S(1)}, u32[]{:S(2)}, u32[]{:S(2)}) collective-permute-start(bf16[128,4096]{1,0:T(8,128)(2,1)} %param.4), channel_id=1, source_target_pairs={{0,12},{4,0},{8,4},{12,8},{1,13},{5,1},{9,5},{13,9},{2,14},{6,2},{... | collective-permute-start | bytes 3145736 | tf_op jit(solution)/shard_map/ppermute | solution.py:23
  3.6 2.5 %slice_dynamic-update-slice_fusion.7 = bf16[4096,1024]{1,0:T(8,128)(2,1)} fusion(bf16[4096,512]{1,0:T(8,128)(2,1)} %param.6), kind=kLoop, calls=%fused_computation.17 | loop fusion | bytes 2097152
  6.1 3.0 %slice_dynamic-update-slice_fusion.6 = bf16[4096,1024]{1,0:T(8,128)(2,1)} fusion(bf16[4096,1024]{1,0:T(8,128)(2,1)} %slice_dynamic-update-slice_fusion.7, bf16[4096,512]{1,0:T(8,128)(2,1)} %param.7), kind=kLoop, calls=%fused_computation.16 | loop fusion | bytes 2097152
  9.1 2.4 %slice_dynamic-update-slice_fusion.5 = bf16[4096,1024]{1,0:T(8,128)(2,1)} fusion(bf16[4096,1024]{1,0:T(8,128)(2,1)} %slice_dynamic-update-slice_fusion.6, bf16[4096,512]{1,0:T(8,128)(2,1)} %param.6), kind=kLoop, calls=%fused_computation.15 | loop fusion | bytes 2097152
  11.5 2.3 %slice_dynamic-update-slice_fusion.4 = bf16[4096,1024]{1,0:T(8,128)(2,1)} fusion(bf16[4096,1024]{1,0:T(8,128)(2,1)} %slice_dynamic-update-slice_fusion.5, bf16[4096,512]{1,0:T(8,128)(2,1)} %param.7), kind=kLoop, calls=%fused_computation.14 | loop fusion | bytes 2097152
  15.0 1.2 %slice_dynamic-update-slice_fusion.2 = bf16[4096,1024]{1,0:T(8,128)(2,1)} fusion(bf16[4096,1024]{1,0:T(8,128)(2,1)} %slice_dynamic-update-slice_fusion.3, bf16[4096,512]{1,0:T(8,128)(2,1)S(1)} %copy-done.1), kind=kLoop, calls=%fused_computation.12 | loop fusion | bytes 2097152
  18.5 6.0 %fusion.30 = f32[1024,128]{1,0:T(8,128)S(1)} fusion(bf16[4096,1024]{1,0:T(8,128)(2,1)} %slice_dynamic-update-slice_fusion, bf16[128,4096]{1,0:T(8,128)(2,1)} %param.4), kind=kOutput, calls=%fused_computation.87 | convolution fusion | flops 1073741824 | bytes 9961472 | tf_op jit(solution)/shard_map/dot_general | solution.py:48
  25.3 2.5 %collective-permute-start.3 = (f32[128,256]{1,0:T(8,128)}, f32[128,256]{1,0:T(8,128)S(1)}, u32[]{:S(2)}, u32[]{:S(2)}) collective-permute-start(f32[128,256]{1,0:T(8,128)} %bitcast.9), channel_id=1, source_target_pairs={{0,3},{1,0},{2,1},{3,2},{4,7},{5,4},{6,5},{7,6},{8,11},{9,8},{10,9... | collective-permute-start | bytes 393224 | tf_op jit(solution)/shard_map/ppermute | solution.py:23
  30.8 4.1 %collective-permute-start.1 = (f32[128,256]{1,0:T(8,128)}, f32[128,256]{1,0:T(8,128)}, u32[]{:S(2)}, u32[]{:S(2)}) collective-permute-start(f32[128,256]{1,0:T(8,128)} %bitcast.7), channel_id=1, source_target_pairs={{0,1},{1,2},{2,3},{3,0},{4,5},{5,6},{6,7},{7,4},{8,9},{9,10},{10,1... | collective-permute-start | bytes 393224 | tf_op jit(solution)/shard_map/ppermute | solution.py:23
  35.1 6.1 %fusion.31 = f32[1024,128]{1,0:T(8,128)S(1)} fusion(bf16[4096,1024]{1,0:T(8,128)(2,1)} %slice_dynamic-update-slice_fusion, bf16[128,4096]{1,0:T(8,128)(2,1)S(1)} %collective-permute-done.4), kind=kOutput, calls=%fused_computation.88 | convolution fusion | flops 1073741824 | bytes 9961472 | tf_op jit(solution)/shard_map/dot_general | solution.py:48
  41.3 5.7 %fusion.32 = f32[1024,128]{1,0:T(8,128)S(1)} fusion(bf16[4096,1024]{1,0:T(8,128)(2,1)} %slice_dynamic-update-slice_fusion, bf16[128,4096]{1,0:T(8,128)(2,1)S(1)} %collective-permute-done.5), kind=kOutput, calls=%fused_computation.89 | convolution fusion | flops 1073741824 | bytes 9961472 | tf_op jit(solution)/shard_map/dot_general | solution.py:48
  47.3 3.0 %collective-permute-start.8 = (f32[256,256]{1,0:T(8,128)S(1)}, f32[256,256]{1,0:T(8,128)S(1)}, u32[]{:S(2)}, u32[]{:S(2)}) collective-permute-start(f32[256,256]{1,0:T(8,128)S(1)} %bitcast.111), channel_id=1, source_target_pairs={{0,3},{1,0},{2,1},{3,2},{4,7},{5,4},{6,5},{7,6},{8,11},{9,8},{10,9... | collective-permute-start | bytes 786440 | tf_op jit(solution)/shard_map/ppermute | solution.py:23
  50.4 3.5 %collective-permute-start.7 = (f32[256,256]{1,0:T(8,128)S(1)}, f32[256,256]{1,0:T(8,128)S(1)}, u32[]{:S(2)}, u32[]{:S(2)}) collective-permute-start(f32[256,256]{1,0:T(8,128)S(1)} %bitcast.112), channel_id=1, source_target_pairs={{0,2},{1,3},{2,0},{3,1},{4,6},{5,7},{6,4},{7,5},{8,10},{9,11},{10,... | collective-permute-start | bytes 786440 | tf_op jit(solution)/shard_map/ppermute | solution.py:23
  56.8 1.4 %collective-permute-start.9 = (bf16[64,4096]{1,0:T(8,128)(2,1)S(1)}, bf16[64,4096]{1,0:T(8,128)(2,1)S(1)}, u32[]{:S(2)}, u32[]{:S(2)}) collective-permute-start(bf16[64,4096]{1,0:T(8,128)(2,1)S(1)} %slice.59), channel_id=1, source_target_pairs={{0,4},{4,8},{8,12},{12,0},{1,5},{5,9},{9,13},{13,1},{2,6},{6,10},{... | collective-permute-start | bytes 1572872 | tf_op jit(solution)/shard_map/ppermute | solution.py:23
  58.2 5.5 %collective-permute-done.6 = f32[256,256]{1,0:T(8,128)S(1)} collective-permute-done((f32[256,256]{1,0:T(8,128)S(1)}, f32[256,256]{1,0:T(8,128)S(1)}, u32[]{:S(2)}, u32[]{:S(2)}) %collective-permute-start.6) | collective-permute-done | bytes 262176 | tf_op jit(solution)/shard_map/ppermute | solution.py:23
  63.8 4.9 %fusion.34 = f32[1024,64]{0,1:T(8,128)S(1)} fusion(bf16[64,4096]{1,0:T(8,128)(2,1)S(1)} %collective-permute-done.10, bf16[4096,1024]{1,0:T(8,128)(2,1)} %slice_dynamic-update-slice_fusion), kind=kOutput, calls=%fused_computation.91 | convolution fusion | flops 536870912 | bytes 9175040 | tf_op jit(solution)/shard_map/dot_general | solution.py:48
  68.7 5.0 %fusion.33 = f32[1024,64]{0,1:T(8,128)S(1)} fusion(bf16[64,4096]{1,0:T(8,128)(2,1)S(1)} %collective-permute-done.9, bf16[4096,1024]{1,0:T(8,128)(2,1)} %slice_dynamic-update-slice_fusion), kind=kOutput, calls=%fused_computation.90 | convolution fusion | flops 536870912 | bytes 9175040 | tf_op jit(solution)/shard_map/dot_general | solution.py:48
  73.8 2.8 %collective-permute-start.13 = (f32[128,256]{1,0:T(8,128)S(1)}, f32[128,256]{1,0:T(8,128)S(1)}, u32[]{:S(2)}, u32[]{:S(2)}) collective-permute-start(f32[128,256]{1,0:T(8,128)S(1)} %get-tuple-element.15), channel_id=1, source_target_pairs={{0,3},{1,0},{2,1},{3,2},{4,7},{5,4},{6,5},{7,6},{8,11},{9,8},{10,9... | collective-permute-start | bytes 393224 | tf_op jit(solution)/shard_map/ppermute | solution.py:23
  77.3 2.6 %collective-permute-done.13 = f32[128,256]{1,0:T(8,128)S(1)} collective-permute-done((f32[128,256]{1,0:T(8,128)S(1)}, f32[128,256]{1,0:T(8,128)S(1)}, u32[]{:S(2)}, u32[]{:S(2)}) %collective-permute-start.13) | collective-permute-done | bytes 131104 | tf_op jit(solution)/shard_map/ppermute | solution.py:23
  79.9 2.1 %collective-permute-done.12 = f32[128,256]{1,0:T(8,128)S(1)} collective-permute-done((f32[128,256]{1,0:T(8,128)S(1)}, f32[128,256]{1,0:T(8,128)S(1)}, u32[]{:S(2)}, u32[]{:S(2)}) %collective-permute-start.12) | collective-permute-done | bytes 131104 | tf_op jit(solution)/shard_map/ppermute | solution.py:23
  84.8 1.3 %collective-permute-done.16 = bf16[128,128]{1,0:T(8,128)(2,1)S(1)} collective-permute-done((bf16[128,128]{1,0:T(8,128)(2,1)S(1)}, bf16[128,128]{1,0:T(8,128)(2,1)S(1)}, u32[]{:S(2)}, u32[]{:S(2)}) %collective-permute-start.16) | collective-permute-done | bytes 32800 | tf_op jit(solution)/shard_map/ppermute | solution.py:23
  86.1 2.5 %collective-permute-done.15 = bf16[128,128]{1,0:T(8,128)(2,1)S(1)} collective-permute-done((bf16[128,128]{1,0:T(8,128)(2,1)S(1)}, bf16[128,128]{1,0:T(8,128)(2,1)S(1)}, u32[]{:S(2)}, u32[]{:S(2)}) %collective-permute-start.15) | collective-permute-done | bytes 32800 | tf_op jit(solution)/shard_map/ppermute | solution.py:23
  90.5 27.7 %all_to_all.5 = bf16[16,16,512]{2,1,0:T(8,128)(2,1)S(1)} all-to-all(bf16[16,16,512]{2,1,0:T(8,128)(2,1)S(1)} %bitcast.105), channel_id=1, replica_groups=mesh['batch'=16,'wx'=4,'wy'=4] {'batch'}, dimensions={0} | all-to-all | bytes 524288 | tf_op jit(solution)/shard_map/all_to_all | solution.py:78
  (66 shorter events, 16.8 us)
Async XLA Ops:
  0.0 35.1 %collective-permute-start.4 = (bf16[128,4096]{1,0:T(8,128)(2,1)}, bf16[128,4096]{1,0:T(8,128)(2,1)S(1)}, u32[]{:S(2)}, u32[]{:S(2)}) collective-permute-start(bf16[128,4096]{1,0:T(8,128)(2,1)} %param.4), channel_id=1, source_target_pairs={{0,4},{4,8},{8,12},{12,0},{1,5},{5,9},{9,13},{13,1},{2,6},{6,10},{... | collective-permute-start | bytes 3145736 | tf_op jit(solution)/shard_map/ppermute | solution.py:23
  2.1 39.2 %collective-permute-start.5 = (bf16[128,4096]{1,0:T(8,128)(2,1)}, bf16[128,4096]{1,0:T(8,128)(2,1)S(1)}, u32[]{:S(2)}, u32[]{:S(2)}) collective-permute-start(bf16[128,4096]{1,0:T(8,128)(2,1)} %param.4), channel_id=1, source_target_pairs={{0,12},{4,0},{8,4},{12,8},{1,13},{5,1},{9,5},{13,9},{2,14},{6,2},{... | collective-permute-start | bytes 3145736 | tf_op jit(solution)/shard_map/ppermute | solution.py:23
  3.6 10.2 %copy-start = (bf16[4096,512]{1,0:T(8,128)(2,1)S(1)}, bf16[4096,512]{1,0:T(8,128)(2,1)}, u32[]{:S(2)}) copy-start(bf16[4096,512]{1,0:T(8,128)(2,1)} %param.6) | copy-start | bytes 12582916
  3.6 11.4 %copy-start.1 = (bf16[4096,512]{1,0:T(8,128)(2,1)S(1)}, bf16[4096,512]{1,0:T(8,128)(2,1)}, u32[]{:S(2)}) copy-start(bf16[4096,512]{1,0:T(8,128)(2,1)} %param.7) | copy-start | bytes 12582916
  16.2 12.9 %copy-start.3 = (s32[128,1]{0,1:T(1,128)S(1)}, s32[128,1]{0,1:T(1,128)}, u32[]{:S(2)}) copy-start(s32[128,1]{0,1:T(1,128)} %param.5) | copy-start | bytes 1540
  25.3 28.7 %collective-permute-start.3 = (f32[128,256]{1,0:T(8,128)}, f32[128,256]{1,0:T(8,128)S(1)}, u32[]{:S(2)}, u32[]{:S(2)}) collective-permute-start(f32[128,256]{1,0:T(8,128)} %bitcast.9), channel_id=1, source_target_pairs={{0,3},{1,0},{2,1},{3,2},{4,7},{5,4},{6,5},{7,6},{8,11},{9,8},{10,9... | collective-permute-start | bytes 393224 | tf_op jit(solution)/shard_map/ppermute | solution.py:23
  28.5 25.6 %collective-permute-start.2 = (f32[128,256]{1,0:T(8,128)}, f32[128,256]{1,0:T(8,128)}, u32[]{:S(2)}, u32[]{:S(2)}) collective-permute-start(f32[128,256]{1,0:T(8,128)} %bitcast.8), channel_id=1, source_target_pairs={{0,2},{1,3},{2,0},{3,1},{4,6},{5,7},{6,4},{7,5},{8,10},{9,11},{10,... | collective-permute-start | bytes 393224 | tf_op jit(solution)/shard_map/ppermute | solution.py:23
  29.1 1.7 %collective-permute-start = (s32[128,1]{0,1:T(1,128)S(1)}, s32[128,1]{0,1:T(1,128)S(1)}, u32[]{:S(2)}, u32[]{:S(2)}) collective-permute-start(s32[128,1]{0,1:T(1,128)S(1)} %copy-done.3), channel_id=1, source_target_pairs={{0,0},{1,4},{2,8},{3,12},{4,1},{5,5},{6,9},{7,13},{8,2},{9,6},{10,... | collective-permute-start | bytes 1544 | tf_op jit(solution)/shard_map/ppermute | solution.py:40
  30.8 23.9 %collective-permute-start.1 = (f32[128,256]{1,0:T(8,128)}, f32[128,256]{1,0:T(8,128)}, u32[]{:S(2)}, u32[]{:S(2)}) collective-permute-start(f32[128,256]{1,0:T(8,128)} %bitcast.7), channel_id=1, source_target_pairs={{0,1},{1,2},{2,3},{3,0},{4,5},{5,6},{6,7},{7,4},{8,9},{9,10},{10,1... | collective-permute-start | bytes 393224 | tf_op jit(solution)/shard_map/ppermute | solution.py:23
  35.1 11.9 %copy-start.2 = (bf16[128,4096]{1,0:T(8,128)(2,1)}, bf16[128,4096]{1,0:T(8,128)(2,1)S(1)}, u32[]{:S(2)}) copy-start(bf16[128,4096]{1,0:T(8,128)(2,1)S(1)} %collective-permute-done.4) | copy-start | bytes 3145732
  47.3 10.9 %collective-permute-start.8 = (f32[256,256]{1,0:T(8,128)S(1)}, f32[256,256]{1,0:T(8,128)S(1)}, u32[]{:S(2)}, u32[]{:S(2)}) collective-permute-start(f32[256,256]{1,0:T(8,128)S(1)} %bitcast.111), channel_id=1, source_target_pairs={{0,3},{1,0},{2,1},{3,2},{4,7},{5,4},{6,5},{7,6},{8,11},{9,8},{10,9... | collective-permute-start | bytes 786440 | tf_op jit(solution)/shard_map/ppermute | solution.py:23
  50.4 7.8 %collective-permute-start.7 = (f32[256,256]{1,0:T(8,128)S(1)}, f32[256,256]{1,0:T(8,128)S(1)}, u32[]{:S(2)}, u32[]{:S(2)}) collective-permute-start(f32[256,256]{1,0:T(8,128)S(1)} %bitcast.112), channel_id=1, source_target_pairs={{0,2},{1,3},{2,0},{3,1},{4,6},{5,7},{6,4},{7,5},{8,10},{9,11},{10,... | collective-permute-start | bytes 786440 | tf_op jit(solution)/shard_map/ppermute | solution.py:23
  54.1 9.6 %collective-permute-start.6 = (f32[256,256]{1,0:T(8,128)S(1)}, f32[256,256]{1,0:T(8,128)S(1)}, u32[]{:S(2)}, u32[]{:S(2)}) collective-permute-start(f32[256,256]{1,0:T(8,128)S(1)} %bitcast.113), channel_id=1, source_target_pairs={{0,1},{1,2},{2,3},{3,0},{4,5},{5,6},{6,7},{7,4},{8,9},{9,10},{10,1... | collective-permute-start | bytes 786440 | tf_op jit(solution)/shard_map/ppermute | solution.py:23
  54.2 9.6 %collective-permute-start.10 = (bf16[64,4096]{1,0:T(8,128)(2,1)S(1)}, bf16[64,4096]{1,0:T(8,128)(2,1)S(1)}, u32[]{:S(2)}, u32[]{:S(2)}) collective-permute-start(bf16[64,4096]{1,0:T(8,128)(2,1)S(1)} %slice.60), channel_id=1, source_target_pairs={{0,12},{4,0},{8,4},{12,8},{1,13},{5,1},{9,5},{13,9},{2,14},{6,2},{... | collective-permute-start | bytes 1572872 | tf_op jit(solution)/shard_map/ppermute | solution.py:23
  56.8 11.9 %collective-permute-start.9 = (bf16[64,4096]{1,0:T(8,128)(2,1)S(1)}, bf16[64,4096]{1,0:T(8,128)(2,1)S(1)}, u32[]{:S(2)}, u32[]{:S(2)}) collective-permute-start(bf16[64,4096]{1,0:T(8,128)(2,1)S(1)} %slice.59), channel_id=1, source_target_pairs={{0,4},{4,8},{8,12},{12,0},{1,5},{5,9},{9,13},{13,1},{2,6},{6,10},{... | collective-permute-start | bytes 1572872 | tf_op jit(solution)/shard_map/ppermute | solution.py:23
  73.8 6.1 %collective-permute-start.13 = (f32[128,256]{1,0:T(8,128)S(1)}, f32[128,256]{1,0:T(8,128)S(1)}, u32[]{:S(2)}, u32[]{:S(2)}) collective-permute-start(f32[128,256]{1,0:T(8,128)S(1)} %get-tuple-element.15), channel_id=1, source_target_pairs={{0,3},{1,0},{2,1},{3,2},{4,7},{5,4},{6,5},{7,6},{8,11},{9,8},{10,9... | collective-permute-start | bytes 393224 | tf_op jit(solution)/shard_map/ppermute | solution.py:23
  76.6 5.4 %collective-permute-start.12 = (f32[128,256]{1,0:T(8,128)S(1)}, f32[128,256]{1,0:T(8,128)S(1)}, u32[]{:S(2)}, u32[]{:S(2)}) collective-permute-start(f32[128,256]{1,0:T(8,128)S(1)} %get-tuple-element.14), channel_id=1, source_target_pairs={{0,2},{1,3},{2,0},{3,1},{4,6},{5,7},{6,4},{7,5},{8,10},{9,11},{10,... | collective-permute-start | bytes 393224 | tf_op jit(solution)/shard_map/ppermute | solution.py:23
  76.6 6.4 %collective-permute-start.11 = (f32[128,256]{1,0:T(8,128)S(1)}, f32[128,256]{1,0:T(8,128)S(1)}, u32[]{:S(2)}, u32[]{:S(2)}) collective-permute-start(f32[128,256]{1,0:T(8,128)S(1)} %get-tuple-element.13), channel_id=1, source_target_pairs={{0,1},{1,2},{2,3},{3,0},{4,5},{5,6},{6,7},{7,4},{8,9},{9,10},{10,1... | collective-permute-start | bytes 393224 | tf_op jit(solution)/shard_map/ppermute | solution.py:23
  83.3 2.8 %collective-permute-start.16 = (bf16[128,128]{1,0:T(8,128)(2,1)S(1)}, bf16[128,128]{1,0:T(8,128)(2,1)S(1)}, u32[]{:S(2)}, u32[]{:S(2)}) collective-permute-start(bf16[128,128]{1,0:T(8,128)(2,1)S(1)} %get-tuple-element.19), channel_id=1, source_target_pairs={{0,3},{1,0},{2,1},{3,2},{4,7},{5,4},{6,5},{7,6},{8,11},{9,8},{10,9... | collective-permute-start | bytes 98312 | tf_op jit(solution)/shard_map/ppermute | solution.py:23
  83.9 4.6 %collective-permute-start.15 = (bf16[128,128]{1,0:T(8,128)(2,1)S(1)}, bf16[128,128]{1,0:T(8,128)(2,1)S(1)}, u32[]{:S(2)}, u32[]{:S(2)}) collective-permute-start(bf16[128,128]{1,0:T(8,128)(2,1)S(1)} %get-tuple-element.20), channel_id=1, source_target_pairs={{0,2},{1,3},{2,0},{3,1},{4,6},{5,7},{6,4},{7,5},{8,10},{9,11},{10,... | collective-permute-start | bytes 98312 | tf_op jit(solution)/shard_map/ppermute | solution.py:23
  84.0 5.4 %collective-permute-start.14 = (bf16[128,128]{1,0:T(8,128)(2,1)S(1)}, bf16[128,128]{1,0:T(8,128)(2,1)S(1)}, u32[]{:S(2)}, u32[]{:S(2)}) collective-permute-start(bf16[128,128]{1,0:T(8,128)(2,1)S(1)} %get-tuple-element.21), channel_id=1, source_target_pairs={{0,1},{1,2},{2,3},{3,0},{4,5},{5,6},{6,7},{7,4},{8,9},{9,10},{10,1... | collective-permute-start | bytes 98312 | tf_op jit(solution)/shard_map/ppermute | solution.py:23

commit v4 on v2

--- a/solution.py
+++ b/solution.py
@@ -1,7 +1,7 @@
 import jax
 import jax.numpy as jnp
 from jax import lax
-from jax.sharding import PartitionSpec as P
+from jax.sharding import Mesh, PartitionSpec as P
 
 
 def place_rows(source, group_of, slots, groups_total):
@@ -26,7 +26,9 @@
 def per_device(tokens, routes, gate_weight, up_weight):
     row_count = tokens.shape[0]
     hid = gate_weight.shape[1]
-    groups_total = lax.axis_size("batch")
+    chips = lax.axis_size("bz")
+    cores = lax.axis_size("bc")
+    groups_total = chips * cores
     nx = lax.axis_size("wx")
     ny = lax.axis_size("wy")
     assert nx == 4 and ny == 4
@@ -60,13 +62,17 @@
     gate_sum, up_sum = total[:, :hid], total[:, hid:]
     hidden = (jax.nn.silu(gate_sum) * up_sum).astype(jnp.bfloat16)
     placed = place_rows(hidden, group_of, slots, groups_total)
-    placed = placed.reshape(groups_total, slots, hid)
-    arrived = lax.all_to_all(placed, "batch", split_axis=0, concat_axis=0, tiled=True)
+    placed = placed.reshape(chips, cores, slots, hid)
+    placed = lax.all_to_all(placed, "bc", split_axis=1, concat_axis=1, tiled=True)
+    arrived = lax.all_to_all(placed, "bz", split_axis=0, concat_axis=0, tiled=True)
     return arrived.reshape(groups_total * slots, hid)
 
 
 def solution(mesh):
-    placed = (P(("batch", "wx"), "wy"), P(("batch", "wx"), None), P("wy", "wx"), P("wy", "wx"))
+    n_batch, n_wx, n_wy = mesh.devices.shape
+    split = Mesh(mesh.devices.reshape(n_batch // 2, 2, n_wx, n_wy), ("bz", "bc", "wx", "wy"))
+    rows = ("bz", "bc", "wx")
+    placed = (P(rows, "wy"), P(rows, None), P("wy", "wx"), P("wy", "wx"))
     return jax.shard_map(
-        per_device, mesh=mesh, in_specs=placed, out_specs=P(("batch", "wy"), "wx"), check_vma=False
+        per_device, mesh=split, in_specs=placed, out_specs=P(("bz", "bc", "wy"), "wx"), check_vma=False
     )

time: 95.1 us -> 98.1 us (1.032)
  blocking collectives: 23 us -> 25.8 us
    all_to_all x1 -> x2, blocking collectives: 23 us -> 25.8 us  [the longest x1 19.1 us: per_device(): lax.all_to_all(placed, 'bz', split_axis=0, concat_axis=0, tiled=True)]
where the time goes in v4:
time: 98.1 us; the launch traced here: 97.9 us
  waiting for transfers between devices  41.5 us (42%)
  blocking collectives  25.8 us (26%)
  starting transfers between devices  15.1 us (15%)
  matrix products  10.9 us (11%)
  other arithmetic  2.23 us (2%)
  local copies, waits for them, and re-layouts  2.14 us (2%)
    ppermute x7, waiting for transfers between devices, shift(): lax.ppermute(value, axis, [(i, (i + step) % count) for i in range(count)])  41.5 us
    all_to_all x1, blocking collectives, per_device(): lax.all_to_all(placed, 'bz', split_axis=0, concat_axis=0, tiled=True)  19.1 us
    ppermute x7, starting transfers between devices, shift(): lax.ppermute(value, axis, [(i, (i + step) % count) for i in range(count)])  13.8 us
    all_to_all x1, blocking collectives, per_device(): lax.all_to_all(placed, 'bc', split_axis=1, concat_axis=1, tiled=True)  6.69 us
    dot_general x5, matrix products, partial(): up = jnp.dot(rows, up_weight, preferred_element_type=jnp.float32)  6.57 us
    dot_general x5, matrix products, partial(): gate = jnp.dot(rows, gate_weight, preferred_element_type=jnp.float32)  3.97 us
  transfers between devices with their start and end apart: 8, of which 4 were waited for; matrix products, arithmetic and copies ran while one was open for 13% of the time, Pallas kernels for 0%

profile of v4, /device:TPU:1, one launch (start us, length us, event | category | flops | bytes accessed | tf_op | source)
XLA Modules:
  0.0 97.9 jit_solution(83902284558098874)
XLA Ops:
  0.0 2.1 %collective-permute-start.2 = (bf16[128,4096]{1,0:T(8,128)(2,1)}, bf16[128,4096]{1,0:T(8,128)(2,1)S(1)}, u32[]{:S(2)}, u32[]{:S(2)}) collective-permute-start(bf16[128,4096]{1,0:T(8,128)(2,1)} %param.4), channel_id=1, source_target_pairs={{0,4},{4,8},{8,12},{12,0},{1,5},{5,9},{9,13},{13,1},{2,6},{6,10},{... | collective-permute-start | bytes 3145736 | tf_op jit(solution)/shard_map/ppermute | solution.py:23
  2.1 1.5 %collective-permute-start.1 = (bf16[128,4096]{1,0:T(8,128)(2,1)}, bf16[128,4096]{1,0:T(8,128)(2,1)S(1)}, u32[]{:S(2)}, u32[]{:S(2)}) collective-permute-start(bf16[128,4096]{1,0:T(8,128)(2,1)} %param.4), channel_id=1, source_target_pairs={{0,12},{4,0},{8,4},{12,8},{1,13},{5,1},{9,5},{13,9},{2,14},{6,2},{... | collective-permute-start | bytes 3145736 | tf_op jit(solution)/shard_map/ppermute | solution.py:23
  3.6 1.3 %collective-permute-start = (s32[128,1]{0,1:T(1,128)}, s32[128,1]{0,1:T(1,128)S(1)}, u32[]{:S(2)}, u32[]{:S(2)}) collective-permute-start(s32[128,1]{0,1:T(1,128)} %param.5), channel_id=1, source_target_pairs={{0,0},{1,4},{2,8},{3,12},{4,1},{5,5},{6,9},{7,13},{8,2},{9,6},{10,... | collective-permute-start | bytes 1544 | tf_op jit(solution)/shard_map/ppermute | solution.py:41
  4.9 3.4 %fusion.9 = f32[128,512]{1,0:T(8,128)S(1)} fusion(bf16[128,4096]{1,0:T(8,128)(2,1)} %param.4, bf16[4096,512]{1,0:T(8,128)(2,1)} %param.7), kind=kOutput, calls=%fused_computation.23 | convolution fusion | flops 536870912 | bytes 5505024 | tf_op jit(solution)/shard_map/dot_general | solution.py:45
  8.7 0.8 fusion.8
  9.5 15.3 %collective-permute-done.2 = bf16[128,4096]{1,0:T(8,128)(2,1)S(1)} collective-permute-done((bf16[128,4096]{1,0:T(8,128)(2,1)}, bf16[128,4096]{1,0:T(8,128)(2,1)S(1)}, u32[]{:S(2)}, u32[]{:S(2)}) %collective-permute-start.2) | collective-permute-done | bytes 1048608 | tf_op jit(solution)/shard_map/ppermute | solution.py:23
  24.9 1.4 %collective-permute-start.3 = (bf16[64,4096]{1,0:T(8,128)(2,1)S(1)}, bf16[64,4096]{1,0:T(8,128)(2,1)S(1)}, u32[]{:S(2)}, u32[]{:S(2)}) collective-permute-start(bf16[64,4096]{1,0:T(8,128)(2,1)S(1)} %slice.16), channel_id=1, source_target_pairs={{0,4},{4,8},{8,12},{12,0},{1,5},{5,9},{9,13},{13,1},{2,6},{6,10},{... | collective-permute-start | bytes 1572872 | tf_op jit(solution)/shard_map/ppermute | solution.py:23
  26.3 1.7 %collective-permute-start.4 = (bf16[64,4096]{1,0:T(8,128)(2,1)S(1)}, bf16[64,4096]{1,0:T(8,128)(2,1)S(1)}, u32[]{:S(2)}, u32[]{:S(2)}) collective-permute-start(bf16[64,4096]{1,0:T(8,128)(2,1)S(1)} %slice.17), channel_id=1, source_target_pairs={{0,12},{4,0},{8,4},{12,8},{1,13},{5,1},{9,5},{13,9},{2,14},{6,2},{... | collective-permute-start | bytes 1572872 | tf_op jit(solution)/shard_map/ppermute | solution.py:23
  28.9 0.8 fusion.16
  29.6 0.8 fusion.11
  31.3 5.9 %collective-permute-done.3 = bf16[64,4096]{1,0:T(8,128)(2,1)S(1)} collective-permute-done((bf16[64,4096]{1,0:T(8,128)(2,1)S(1)}, bf16[64,4096]{1,0:T(8,128)(2,1)S(1)}, u32[]{:S(2)}, u32[]{:S(2)}) %collective-permute-start.3) | collective-permute-done | bytes 524320 | tf_op jit(solution)/shard_map/ppermute | solution.py:23
  37.1 0.8 fusion.13
  38.0 0.8 fusion.12
  38.8 0.8 fusion.15
  39.7 0.8 fusion.14
  40.7 1.0 dynamic-slice_bitcast_fusion.2
  41.7 4.0 %collective-permute-start.5 = (f32[128,1024]{1,0:T(8,128)}, f32[128,1024]{1,0:T(8,128)}, u32[]{:S(2)}, u32[]{:S(2)}) collective-permute-start(f32[128,1024]{1,0:T(8,128)} %get-tuple-element.5), channel_id=1, source_target_pairs={{0,1},{1,2},{2,3},{3,0},{4,5},{5,6},{6,7},{7,4},{8,9},{9,10},{10,1... | collective-permute-start | bytes 1572872 | tf_op jit(solution)/shard_map/ppermute | solution.py:23
  45.7 1.3 %collective-permute-start.7 = (f32[128,1024]{1,0:T(8,128)S(1)}, f32[128,1024]{1,0:T(8,128)}, u32[]{:S(2)}, u32[]{:S(2)}) collective-permute-start(f32[128,1024]{1,0:T(8,128)S(1)} %get-tuple-element.6), channel_id=1, source_target_pairs={{0,3},{1,0},{2,1},{3,2},{4,7},{5,4},{6,5},{7,6},{8,11},{9,8},{10,9... | collective-permute-start | bytes 1572872 | tf_op jit(solution)/shard_map/ppermute | solution.py:23
  47.0 1.7 %collective-permute-start.6 = (f32[128,1024]{1,0:T(8,128)S(1)}, f32[128,1024]{1,0:T(8,128)}, u32[]{:S(2)}, u32[]{:S(2)}) collective-permute-start(f32[128,1024]{1,0:T(8,128)S(1)} %get-tuple-element.7), channel_id=1, source_target_pairs={{0,2},{1,3},{2,0},{3,1},{4,6},{5,7},{6,4},{7,5},{8,10},{9,11},{10,... | collective-permute-start | bytes 1572872 | tf_op jit(solution)/shard_map/ppermute | solution.py:23
  49.2 8.2 %collective-permute-done.5 = f32[128,1024]{1,0:T(8,128)} collective-permute-done((f32[128,1024]{1,0:T(8,128)}, f32[128,1024]{1,0:T(8,128)}, u32[]{:S(2)}, u32[]{:S(2)}) %collective-permute-start.5) | collective-permute-done | bytes 524320 | tf_op jit(solution)/shard_map/ppermute | solution.py:23
  57.3 12.1 %collective-permute-done.6 = f32[128,1024]{1,0:T(8,128)} collective-permute-done((f32[128,1024]{1,0:T(8,128)S(1)}, f32[128,1024]{1,0:T(8,128)}, u32[]{:S(2)}, u32[]{:S(2)}) %collective-permute-start.6) | collective-permute-done | bytes 524320 | tf_op jit(solution)/shard_map/ppermute | solution.py:23
  69.5 1.5 %fusion.1 = f32[128,1024]{1,0:T(8,128)S(1)} fusion(f32[128,1024]{1,0:T(8,128)} %collective-permute-done.7, f32[128,1024]{1,0:T(8,128)} %collective-permute-done.6, f32[128,1024]{1,0:T(8,128)} %collective-permute-done.5, f32[4,128,1024]{2,1,0:T(8,128)S(1)} %pad_maximum_fusion, s32[]{:T(128)S(6)} %select_n.33), kind=kLoop, calls=%fused_computation.8 | loop fusion | flops 393216 | bytes 2621444 | tf_op jit(solution)/shard_map/add | solution.py:61
  71.3 6.7 %all_to_all.10 = bf16[8,2,16,512]{3,2,0,1:T(8,128)(2,1)S(1)} all-to-all(bf16[8,2,16,512]{3,2,0,1:T(8,128)(2,1)S(1)} %copy.6), channel_id=1, replica_groups=mesh['bz'=8,'bc'=2,'wx'=4,'wy'=4] {'bc'}, dimensions={1} | all-to-all | bytes 524288 | tf_op jit(solution)/shard_map/all_to_all | solution.py:66
  78.1 19.1 %all_to_all.11 = bf16[8,2,16,512]{3,2,1,0:T(8,128)(2,1)S(1)} all-to-all(bf16[8,2,16,512]{3,2,1,0:T(8,128)(2,1)S(1)} %copy.7), channel_id=1, replica_groups=mesh['bz'=8,'bc'=2,'wx'=4,'wy'=4] {'bz'}, dimensions={0} | all-to-all | bytes 524288 | tf_op jit(solution)/shard_map/all_to_all | solution.py:67
  (27 shorter events, 3.8 us)
Async XLA Ops:
  0.0 8.3 %copy-start.2 = (bf16[128,4096]{1,0:T(8,128)(2,1)S(1)}, bf16[128,4096]{1,0:T(8,128)(2,1)}, u32[]{:S(2)}) copy-start(bf16[128,4096]{1,0:T(8,128)(2,1)} %param.4) | copy-start | bytes 3145732
  0.0 24.8 %collective-permute-start.2 = (bf16[128,4096]{1,0:T(8,128)(2,1)}, bf16[128,4096]{1,0:T(8,128)(2,1)S(1)}, u32[]{:S(2)}, u32[]{:S(2)}) collective-permute-start(bf16[128,4096]{1,0:T(8,128)(2,1)} %param.4), channel_id=1, source_target_pairs={{0,4},{4,8},{8,12},{12,0},{1,5},{5,9},{9,13},{13,1},{2,6},{6,10},{... | collective-permute-start | bytes 3145736 | tf_op jit(solution)/shard_map/ppermute | solution.py:23
  2.1 24.2 %collective-permute-start.1 = (bf16[128,4096]{1,0:T(8,128)(2,1)}, bf16[128,4096]{1,0:T(8,128)(2,1)S(1)}, u32[]{:S(2)}, u32[]{:S(2)}) collective-permute-start(bf16[128,4096]{1,0:T(8,128)(2,1)} %param.4), channel_id=1, source_target_pairs={{0,12},{4,0},{8,4},{12,8},{1,13},{5,1},{9,5},{13,9},{2,14},{6,2},{... | collective-permute-start | bytes 3145736 | tf_op jit(solution)/shard_map/ppermute | solution.py:23
  3.6 45.1 %collective-permute-start = (s32[128,1]{0,1:T(1,128)}, s32[128,1]{0,1:T(1,128)S(1)}, u32[]{:S(2)}, u32[]{:S(2)}) collective-permute-start(s32[128,1]{0,1:T(1,128)} %param.5), channel_id=1, source_target_pairs={{0,0},{1,4},{2,8},{3,12},{4,1},{5,5},{6,9},{7,13},{8,2},{9,6},{10,... | collective-permute-start | bytes 1544 | tf_op jit(solution)/shard_map/ppermute | solution.py:41
  4.9 3.7 %copy-start.1 = (bf16[4096,512]{1,0:T(8,128)(2,1)S(1)}, bf16[4096,512]{1,0:T(8,128)(2,1)}, u32[]{:S(2)}) copy-start(bf16[4096,512]{1,0:T(8,128)(2,1)} %param.6) | copy-start | bytes 12582916
  8.7 19.4 %copy-start = (bf16[4096,512]{1,0:T(8,128)(2,1)S(1)}, bf16[4096,512]{1,0:T(8,128)(2,1)}, u32[]{:S(2)}) copy-start(bf16[4096,512]{1,0:T(8,128)(2,1)} %param.7) | copy-start | bytes 12582916
  24.9 12.3 %collective-permute-start.3 = (bf16[64,4096]{1,0:T(8,128)(2,1)S(1)}, bf16[64,4096]{1,0:T(8,128)(2,1)S(1)}, u32[]{:S(2)}, u32[]{:S(2)}) collective-permute-start(bf16[64,4096]{1,0:T(8,128)(2,1)S(1)} %slice.16), channel_id=1, source_target_pairs={{0,4},{4,8},{8,12},{12,0},{1,5},{5,9},{9,13},{13,1},{2,6},{6,10},{... | collective-permute-start | bytes 1572872 | tf_op jit(solution)/shard_map/ppermute | solution.py:23
  26.3 12.5 %collective-permute-start.4 = (bf16[64,4096]{1,0:T(8,128)(2,1)S(1)}, bf16[64,4096]{1,0:T(8,128)(2,1)S(1)}, u32[]{:S(2)}, u32[]{:S(2)}) collective-permute-start(bf16[64,4096]{1,0:T(8,128)(2,1)S(1)} %slice.17), channel_id=1, source_target_pairs={{0,12},{4,0},{8,4},{12,8},{1,13},{5,1},{9,5},{13,9},{2,14},{6,2},{... | collective-permute-start | bytes 1572872 | tf_op jit(solution)/shard_map/ppermute | solution.py:23
  41.7 15.7 %collective-permute-start.5 = (f32[128,1024]{1,0:T(8,128)}, f32[128,1024]{1,0:T(8,128)}, u32[]{:S(2)}, u32[]{:S(2)}) collective-permute-start(f32[128,1024]{1,0:T(8,128)} %get-tuple-element.5), channel_id=1, source_target_pairs={{0,1},{1,2},{2,3},{3,0},{4,5},{5,6},{6,7},{7,4},{8,9},{9,10},{10,1... | collective-permute-start | bytes 1572872 | tf_op jit(solution)/shard_map/ppermute | solution.py:23
  45.7 11.6 %collective-permute-start.7 = (f32[128,1024]{1,0:T(8,128)S(1)}, f32[128,1024]{1,0:T(8,128)}, u32[]{:S(2)}, u32[]{:S(2)}) collective-permute-start(f32[128,1024]{1,0:T(8,128)S(1)} %get-tuple-element.6), channel_id=1, source_target_pairs={{0,3},{1,0},{2,1},{3,2},{4,7},{5,4},{6,5},{7,6},{8,11},{9,8},{10,9... | collective-permute-start | bytes 1572872 | tf_op jit(solution)/shard_map/ppermute | solution.py:23
  47.0 22.5 %collective-permute-start.6 = (f32[128,1024]{1,0:T(8,128)S(1)}, f32[128,1024]{1,0:T(8,128)}, u32[]{:S(2)}, u32[]{:S(2)}) collective-permute-start(f32[128,1024]{1,0:T(8,128)S(1)} %get-tuple-element.7), channel_id=1, source_target_pairs={{0,2},{1,3},{2,0},{3,1},{4,6},{5,7},{6,4},{7,5},{8,10},{9,11},{10,... | collective-permute-start | bytes 1572872 | tf_op jit(solution)/shard_map/ppermute | solution.py:23

commit v5 on v2

--- a/solution.py
+++ b/solution.py
@@ -53,10 +53,17 @@
     part_far = jnp.concatenate([partial(far_a), partial(far_b)], axis=0)
     parts = jnp.stack([part_own, part_right, part_far, part_left])
 
-    total = lax.dynamic_index_in_dim(parts, (y - x) % nx, 0, keepdims=False)
-    for d in (1, 2, 3):
-        send = lax.dynamic_index_in_dim(parts, (y + d - x) % nx, 0, keepdims=False)
-        total = total + shift(send, "wy", ny, d)
+    def block(w):
+        return lax.dynamic_index_in_dim(parts, (w - x) % nx, 0, keepdims=False)
+
+    far_part = block(y + 2)
+    via_right = shift(far_part[:half], "wy", ny, -1)
+    via_left = shift(far_part[half:], "wy", ny, 1)
+    to_left = block(y - 1)
+    to_left = jnp.concatenate([to_left[:half] + via_right, to_left[half:]], axis=0)
+    to_right = block(y + 1)
+    to_right = jnp.concatenate([to_right[:half], to_right[half:] + via_left], axis=0)
+    total = block(y) + shift(to_left, "wy", ny, -1) + shift(to_right, "wy", ny, 1)
     gate_sum, up_sum = total[:, :hid], total[:, hid:]
     hidden = (jax.nn.silu(gate_sum) * up_sum).astype(jnp.bfloat16)
     placed = place_rows(hidden, group_of, slots, groups_total)

time: 95.1 us -> 91.8 us (0.965)
  waiting for transfers between devices: 41.5 us -> 38.2 us
  starting transfers between devices: 15.1 us -> 12.8 us
  blocking collectives: 23 us -> 25 us
    ppermute x7 -> x8, waiting for transfers between devices: 41.5 us -> 38.2 us  [shift(): lax.ppermute(value, axis, [(i, (i + step) % count) for i in range(count)])]
    all_to_all x1, blocking collectives: 23 us -> 25 us  [per_device(): lax.all_to_all(placed, 'batch', split_axis=0, concat_axis=0, tiled=True)]
    concatenate x0 -> x2, other arithmetic: none -> 1.65 us  [the longest x1 0.84 us: per_device(): jnp.concatenate([to_right[:half], to_right[half:] + via_left], axis=0)]
    ppermute x7 -> x8, starting transfers between devices: 13.8 us -> 12.2 us  [shift(): lax.ppermute(value, axis, [(i, (i + step) % count) for i in range(count)])]
    add x1 -> x2, other arithmetic: 1.5 us -> 0.16 us  [the longest x1 0.09 us: per_device(): block(y) + shift(to_left, 'wy', ny, -1) + shift(to_right, 'wy', ny, 1)]
    squeeze x1 -> x0, local copies, waits for them, and re-layouts: 0.96 us -> none  [per_device(): send = lax.dynamic_index_in_dim(parts, (y + d - x) % nx, 0, keepdims=False)]
  transfers between devices with their start and end apart: 8 -> 9, of which waited for: 4 -> 6; matrix products, arithmetic and copies ran while one was open for 13% -> 12% of each run, Pallas kernels for 0% -> 0%
where the time goes in v5:
time: 91.8 us; the launch traced here: 91.6 us
  waiting for transfers between devices  38.2 us (42%)
  blocking collectives  25 us (27%)
  starting transfers between devices  12.8 us (14%)
  matrix products  10.9 us (12%)
  other arithmetic  2.54 us (3%)
  local copies, waits for them, and re-layouts  1.97 us (2%)
    ppermute x8, waiting for transfers between devices, shift(): lax.ppermute(value, axis, [(i, (i + step) % count) for i in range(count)])  38.2 us
    all_to_all x1, blocking collectives, per_device(): lax.all_to_all(placed, 'batch', split_axis=0, concat_axis=0, tiled=True)  25 us
    ppermute x8, starting transfers between devices, shift(): lax.ppermute(value, axis, [(i, (i + step) % count) for i in range(count)])  12.2 us
    dot_general x5, matrix products, partial(): up = jnp.dot(rows, up_weight, preferred_element_type=jnp.float32)  6.58 us
    dot_general x5, matrix products, partial(): gate = jnp.dot(rows, gate_weight, preferred_element_type=jnp.float32)  3.98 us
  transfers between devices with their start and end apart: 9, of which 6 were waited for; matrix products, arithmetic and copies ran while one was open for 12% of the time, Pallas kernels for 0%

profile of v5, /device:TPU:1, one launch (start us, length us, event | category | flops | bytes accessed | tf_op | source)
XLA Modules:
  0.0 91.6 jit_solution(1864369329400884856)
XLA Ops:
  0.0 3.6 %collective-permute-start.1 = (bf16[128,4096]{1,0:T(8,128)(2,1)}, bf16[128,4096]{1,0:T(8,128)(2,1)S(1)}, u32[]{:S(2)}, u32[]{:S(2)}) collective-permute-start(bf16[128,4096]{1,0:T(8,128)(2,1)} %param.4), channel_id=1, source_target_pairs={{0,12},{4,0},{8,4},{12,8},{1,13},{5,1},{9,5},{13,9},{2,14},{6,2},{... | collective-permute-start | bytes 3145736 | tf_op jit(solution)/shard_map/ppermute | solution.py:23
  3.6 3.4 %fusion.10 = f32[128,512]{1,0:T(8,128)S(1)} fusion(bf16[128,4096]{1,0:T(8,128)(2,1)} %param.4, bf16[4096,512]{1,0:T(8,128)(2,1)} %param.7), kind=kOutput, calls=%fused_computation.29 | convolution fusion | flops 536870912 | bytes 5505024 | tf_op jit(solution)/shard_map/dot_general | solution.py:43
  7.3 0.8 fusion.9
  8.1 17.6 %collective-permute-done.1 = bf16[128,4096]{1,0:T(8,128)(2,1)S(1)} collective-permute-done((bf16[128,4096]{1,0:T(8,128)(2,1)}, bf16[128,4096]{1,0:T(8,128)(2,1)S(1)}, u32[]{:S(2)}, u32[]{:S(2)}) %collective-permute-start.1) | collective-permute-done | bytes 1048608 | tf_op jit(solution)/shard_map/ppermute | solution.py:23
  25.8 3.4 %collective-permute-start.4 = (bf16[64,4096]{1,0:T(8,128)(2,1)S(1)}, bf16[64,4096]{1,0:T(8,128)(2,1)S(1)}, u32[]{:S(2)}, u32[]{:S(2)}) collective-permute-start(bf16[64,4096]{1,0:T(8,128)(2,1)S(1)} %slice.65), channel_id=1, source_target_pairs={{0,12},{4,0},{8,4},{12,8},{1,13},{5,1},{9,5},{13,9},{2,14},{6,2},{... | collective-permute-start | bytes 1572872 | tf_op jit(solution)/shard_map/ppermute | solution.py:23
  29.3 0.8 fusion.18
  30.1 0.8 fusion.17
  30.9 0.8 fusion.12
  31.7 0.8 fusion.11
  32.5 6.4 %collective-permute-done.4 = bf16[64,4096]{1,0:T(8,128)(2,1)S(1)} collective-permute-done((bf16[64,4096]{1,0:T(8,128)(2,1)S(1)}, bf16[64,4096]{1,0:T(8,128)(2,1)S(1)}, u32[]{:S(2)}, u32[]{:S(2)}) %collective-permute-start.4) | collective-permute-done | bytes 524320 | tf_op jit(solution)/shard_map/ppermute | solution.py:23
  38.9 0.8 fusion.16
  39.7 0.8 fusion.15
  40.6 1.6 %collective-permute-done.3 = bf16[64,4096]{1,0:T(8,128)(2,1)S(1)} collective-permute-done((bf16[64,4096]{1,0:T(8,128)(2,1)S(1)}, bf16[64,4096]{1,0:T(8,128)(2,1)S(1)}, u32[]{:S(2)}, u32[]{:S(2)}) %collective-permute-start.3) | collective-permute-done | bytes 524320 | tf_op jit(solution)/shard_map/ppermute | solution.py:23
  42.1 0.8 fusion.14
  43.0 0.8 fusion.13
  44.0 0.8 dynamic-slice_bitcast_fusion.4
  44.9 2.5 %collective-permute-start.5 = (f32[64,1024]{1,0:T(8,128)}, f32[64,1024]{1,0:T(8,128)S(1)}, u32[]{:S(2)}, u32[]{:S(2)}) collective-permute-start(f32[64,1024]{1,0:T(8,128)} %get-tuple-element.7), channel_id=1, source_target_pairs={{0,3},{1,0},{2,1},{3,2},{4,7},{5,4},{6,5},{7,6},{8,11},{9,8},{10,9... | collective-permute-start | bytes 786440 | tf_op jit(solution)/shard_map/ppermute | solution.py:23
  48.0 2.9 %collective-permute-done.5 = f32[64,1024]{1,0:T(8,128)S(1)} collective-permute-done((f32[64,1024]{1,0:T(8,128)}, f32[64,1024]{1,0:T(8,128)S(1)}, u32[]{:S(2)}, u32[]{:S(2)}) %collective-permute-start.5) | collective-permute-done | bytes 262176 | tf_op jit(solution)/shard_map/ppermute | solution.py:23
  51.0 2.8 %collective-permute-done.7 = f32[64,1024]{1,0:T(8,128)S(1)} collective-permute-done((f32[64,1024]{1,0:T(8,128)S(1)}, f32[64,1024]{1,0:T(8,128)S(1)}, u32[]{:S(2)}, u32[]{:S(2)}) %collective-permute-start.7) | collective-permute-done | bytes 262176 | tf_op jit(solution)/shard_map/ppermute | solution.py:23
  53.8 0.8 pad_maximum_fusion.2
  54.7 0.8 pad_maximum_fusion.1
  55.5 2.7 %collective-permute-start.6 = (f32[128,1024]{1,0:T(8,128)}, f32[128,1024]{1,0:T(8,128)S(1)}, u32[]{:S(2)}, u32[]{:S(2)}) collective-permute-start(f32[128,1024]{1,0:T(8,128)} %pad_maximum_fusion.1), channel_id=1, source_target_pairs={{0,3},{1,0},{2,1},{3,2},{4,7},{5,4},{6,5},{7,6},{8,11},{9,8},{10,9... | collective-permute-start | bytes 1572872 | tf_op jit(solution)/shard_map/ppermute | solution.py:23
  58.6 6.9 %collective-permute-done.8 = f32[128,1024]{1,0:T(8,128)S(1)} collective-permute-done((f32[128,1024]{1,0:T(8,128)}, f32[128,1024]{1,0:T(8,128)S(1)}, u32[]{:S(2)}, u32[]{:S(2)}) %collective-permute-start.8) | collective-permute-done | bytes 524320 | tf_op jit(solution)/shard_map/ppermute | solution.py:23
  65.9 25.0 %all_to_all.5 = bf16[16,16,512]{2,1,0:T(8,128)(2,1)S(1)} all-to-all(bf16[16,16,512]{2,1,0:T(8,128)(2,1)S(1)} %bitcast.58), channel_id=1, replica_groups=mesh['batch'=16,'wx'=4,'wy'=4] {'batch'}, dimensions={0} | all-to-all | bytes 524288 | tf_op jit(solution)/shard_map/all_to_all | solution.py:71
  (31 shorter events, 3.1 us)
Async XLA Ops:
  0.0 6.9 %copy-start.2 = (bf16[128,4096]{1,0:T(8,128)(2,1)S(1)}, bf16[128,4096]{1,0:T(8,128)(2,1)}, u32[]{:S(2)}) copy-start(bf16[128,4096]{1,0:T(8,128)(2,1)} %param.4) | copy-start | bytes 3145732
  0.0 25.7 %collective-permute-start.1 = (bf16[128,4096]{1,0:T(8,128)(2,1)}, bf16[128,4096]{1,0:T(8,128)(2,1)S(1)}, u32[]{:S(2)}, u32[]{:S(2)}) collective-permute-start(bf16[128,4096]{1,0:T(8,128)(2,1)} %param.4), channel_id=1, source_target_pairs={{0,12},{4,0},{8,4},{12,8},{1,13},{5,1},{9,5},{13,9},{2,14},{6,2},{... | collective-permute-start | bytes 3145736 | tf_op jit(solution)/shard_map/ppermute | solution.py:23
  3.6 25.6 %collective-permute-start.2 = (bf16[128,4096]{1,0:T(8,128)(2,1)}, bf16[128,4096]{1,0:T(8,128)(2,1)S(1)}, u32[]{:S(2)}, u32[]{:S(2)}) collective-permute-start(bf16[128,4096]{1,0:T(8,128)(2,1)} %param.4), channel_id=1, source_target_pairs={{0,4},{4,8},{8,12},{12,0},{1,5},{5,9},{9,13},{13,1},{2,6},{6,10},{... | collective-permute-start | bytes 3145736 | tf_op jit(solution)/shard_map/ppermute | solution.py:23
  3.6 3.7 %copy-start.1 = (bf16[4096,512]{1,0:T(8,128)(2,1)S(1)}, bf16[4096,512]{1,0:T(8,128)(2,1)}, u32[]{:S(2)}) copy-start(bf16[4096,512]{1,0:T(8,128)(2,1)} %param.6) | copy-start | bytes 12582916
  7.3 22.0 %copy-start = (bf16[4096,512]{1,0:T(8,128)(2,1)S(1)}, bf16[4096,512]{1,0:T(8,128)(2,1)}, u32[]{:S(2)}) copy-start(bf16[4096,512]{1,0:T(8,128)(2,1)} %param.7) | copy-start | bytes 12582916
  25.8 13.1 %collective-permute-start.4 = (bf16[64,4096]{1,0:T(8,128)(2,1)S(1)}, bf16[64,4096]{1,0:T(8,128)(2,1)S(1)}, u32[]{:S(2)}, u32[]{:S(2)}) collective-permute-start(bf16[64,4096]{1,0:T(8,128)(2,1)S(1)} %slice.65), channel_id=1, source_target_pairs={{0,12},{4,0},{8,4},{12,8},{1,13},{5,1},{9,5},{13,9},{2,14},{6,2},{... | collective-permute-start | bytes 1572872 | tf_op jit(solution)/shard_map/ppermute | solution.py:23
  29.2 13.0 %collective-permute-start.3 = (bf16[64,4096]{1,0:T(8,128)(2,1)S(1)}, bf16[64,4096]{1,0:T(8,128)(2,1)S(1)}, u32[]{:S(2)}, u32[]{:S(2)}) collective-permute-start(bf16[64,4096]{1,0:T(8,128)(2,1)S(1)} %slice.64), channel_id=1, source_target_pairs={{0,4},{4,8},{8,12},{12,0},{1,5},{5,9},{9,13},{13,1},{2,6},{6,10},{... | collective-permute-start | bytes 1572872 | tf_op jit(solution)/shard_map/ppermute | solution.py:23
  43.8 3.5 %copy-start.3 = (s32[128,1]{0,1:T(1,128)S(1)}, s32[128,1]{0,1:T(1,128)}, u32[]{:S(2)}) copy-start(s32[128,1]{0,1:T(1,128)} %param.5) | copy-start | bytes 1540
  44.9 6.1 %collective-permute-start.5 = (f32[64,1024]{1,0:T(8,128)}, f32[64,1024]{1,0:T(8,128)S(1)}, u32[]{:S(2)}, u32[]{:S(2)}) collective-permute-start(f32[64,1024]{1,0:T(8,128)} %get-tuple-element.7), channel_id=1, source_target_pairs={{0,3},{1,0},{2,1},{3,2},{4,7},{5,4},{6,5},{7,6},{8,11},{9,8},{10,9... | collective-permute-start | bytes 786440 | tf_op jit(solution)/shard_map/ppermute | solution.py:23
  47.3 6.4 %collective-permute-start.7 = (f32[64,1024]{1,0:T(8,128)S(1)}, f32[64,1024]{1,0:T(8,128)S(1)}, u32[]{:S(2)}, u32[]{:S(2)}) collective-permute-start(f32[64,1024]{1,0:T(8,128)S(1)} %get-tuple-element.9), channel_id=1, source_target_pairs={{0,1},{1,2},{2,3},{3,0},{4,5},{5,6},{6,7},{7,4},{8,9},{9,10},{10,1... | collective-permute-start | bytes 786440 | tf_op jit(solution)/shard_map/ppermute | solution.py:23
  47.3 10.8 %collective-permute-start = (s32[128,1]{0,1:T(1,128)S(1)}, s32[128,1]{0,1:T(1,128)S(1)}, u32[]{:S(2)}, u32[]{:S(2)}) collective-permute-start(s32[128,1]{0,1:T(1,128)S(1)} %copy-done.3), channel_id=1, source_target_pairs={{0,0},{1,4},{2,8},{3,12},{4,1},{5,5},{6,9},{7,13},{8,2},{9,6},{10,... | collective-permute-start | bytes 1544 | tf_op jit(solution)/shard_map/ppermute | solution.py:39
  54.7 10.8 %collective-permute-start.8 = (f32[128,1024]{1,0:T(8,128)}, f32[128,1024]{1,0:T(8,128)S(1)}, u32[]{:S(2)}, u32[]{:S(2)}) collective-permute-start(f32[128,1024]{1,0:T(8,128)} %pad_maximum_fusion.2), channel_id=1, source_target_pairs={{0,1},{1,2},{2,3},{3,0},{4,5},{5,6},{6,7},{7,4},{8,9},{9,10},{10,1... | collective-permute-start | bytes 1572872 | tf_op jit(solution)/shard_map/ppermute | solution.py:23
  55.5 10.0 %collective-permute-start.6 = (f32[128,1024]{1,0:T(8,128)}, f32[128,1024]{1,0:T(8,128)S(1)}, u32[]{:S(2)}, u32[]{:S(2)}) collective-permute-start(f32[128,1024]{1,0:T(8,128)} %pad_maximum_fusion.1), channel_id=1, source_target_pairs={{0,3},{1,0},{2,1},{3,2},{4,7},{5,4},{6,5},{7,6},{8,11},{9,8},{10,9... | collective-permute-start | bytes 1572872 | tf_op jit(solution)/shard_map/ppermute | solution.py:23

commit v6 on v2

--- a/solution.py
+++ b/solution.py
@@ -43,20 +43,38 @@
         up = jnp.dot(rows, up_weight, preferred_element_type=jnp.float32)
         return jnp.concatenate([gate, up], axis=1)
 
-    from_left = shift(tokens, "wx", nx, 1)
-    from_right = shift(tokens, "wx", nx, -1)
-    part_own = partial(tokens)
-    far_a = shift(from_left[:half], "wx", nx, 1)
-    far_b = shift(from_right[half:], "wx", nx, -1)
-    part_left = partial(from_left)
-    part_right = partial(from_right)
-    part_far = jnp.concatenate([partial(far_a), partial(far_b)], axis=0)
-    parts = jnp.stack([part_own, part_right, part_far, part_left])
+    def gather(own):
+        cut = own.shape[0] // 2
+        from_left = shift(own, "wx", nx, 1)
+        from_right = shift(own, "wx", nx, -1)
+        far_a = shift(from_left[:cut], "wx", nx, 1)
+        far_b = shift(from_right[cut:], "wx", nx, -1)
+        return from_left, from_right, far_a, far_b
 
-    total = lax.dynamic_index_in_dim(parts, (y - x) % nx, 0, keepdims=False)
-    for d in (1, 2, 3):
-        send = lax.dynamic_index_in_dim(parts, (y + d - x) % nx, 0, keepdims=False)
-        total = total + shift(send, "wy", ny, d)
+    def feature_sum(own, from_left, from_right, far_a, far_b):
+        far = jnp.concatenate([partial(far_a), partial(far_b)], axis=0)
+        parts = jnp.stack([partial(own), partial(from_right), far, partial(from_left)])
+        cut = own.shape[0] // 2
+
+        def block(w):
+            return lax.dynamic_index_in_dim(parts, (w - x) % nx, 0, keepdims=False)
+
+        far_part = block(y + 2)
+        via_right = shift(far_part[:cut], "wy", ny, -1)
+        via_left = shift(far_part[cut:], "wy", ny, 1)
+        to_left = block(y - 1)
+        to_left = jnp.concatenate([to_left[:cut] + via_right, to_left[cut:]], axis=0)
+        to_right = block(y + 1)
+        to_right = jnp.concatenate([to_right[:cut], to_right[cut:] + via_left], axis=0)
+        return block(y) + shift(to_left, "wy", ny, -1) + shift(to_right, "wy", ny, 1)
+
+    first, second = tokens[:half], tokens[half:]
+    got_first = gather(first)
+    second, _ = lax.optimization_barrier((second, got_first[:2]))
+    got_second = gather(second)
+    total = jnp.concatenate(
+        [feature_sum(first, *got_first), feature_sum(second, *got_second)], axis=0
+    )
     gate_sum, up_sum = total[:, :hid], total[:, hid:]
     hidden = (jax.nn.silu(gate_sum) * up_sum).astype(jnp.bfloat16)
     placed = place_rows(hidden, group_of, slots, groups_total)

time: 95.1 us -> 98.1 us (1.032)
  waiting for transfers between devices: 41.5 us -> 22.8 us
  matrix products: 10.9 us -> 21.4 us
  starting transfers between devices: 15.1 us -> 24.4 us
  blocking collectives: 23 us -> 25.6 us
  other arithmetic: 2.23 us -> 1.05 us
    ppermute x7 -> x16, waiting for transfers between devices: 41.5 us -> 22.8 us  [shift(): lax.ppermute(value, axis, [(i, (i + step) % count) for i in range(count)])]
    ppermute x7 -> x16, starting transfers between devices: 13.8 us -> 23.1 us  [shift(): lax.ppermute(value, axis, [(i, (i + step) % count) for i in range(count)])]
    dot_general x5 -> x10, matrix products: 6.57 us -> 12.8 us  [partial(): up = jnp.dot(rows, up_weight, preferred_element_type=jnp.float32)]
    dot_general x5 -> x10, matrix products: 3.97 us -> 8.27 us  [partial(): gate = jnp.dot(rows, gate_weight, preferred_element_type=jnp.float32)]
    all_to_all x1, blocking collectives: 23 us -> 25.6 us  [per_device(): lax.all_to_all(placed, 'batch', split_axis=0, concat_axis=0, tiled=True)]
    slice x2 -> x7, local copies, waits for them, and re-layouts: 0.07 us -> 1.59 us  [the longest x1 1.42 us: per_device(): first, second = (tokens[:half], tokens[half:])]
    add x1 -> x4, other arithmetic: 1.5 us -> 0.2 us  [the longest x2 0.13 us: feature_sum(): block(y) + shift(to_left, 'wy', ny, -1) + shift(to_right, 'wy', ny, 1)]
  transfers between devices with their start and end apart: 8 -> 17, of which waited for: 4 -> 9; matrix products, arithmetic and copies ran while one was open for 13% -> 21% of each run, Pallas kernels for 0% -> 0%
where the time goes in v6:
time: 98.1 us; the launch traced here: 98 us
  blocking collectives  25.6 us (26%)
  starting transfers between devices  24.4 us (25%)
  waiting for transfers between devices  22.8 us (23%)
  matrix products  21.4 us (22%)
  local copies, waits for them, and re-layouts  2.31 us (2%)
  other arithmetic  1.05 us (1%)
    all_to_all x1, blocking collectives, per_device(): lax.all_to_all(placed, 'batch', split_axis=0, concat_axis=0, tiled=True)  25.6 us
    ppermute x16, starting transfers between devices, shift(): lax.ppermute(value, axis, [(i, (i + step) % count) for i in range(count)])  23.1 us
    ppermute x16, waiting for transfers between devices, shift(): lax.ppermute(value, axis, [(i, (i + step) % count) for i in range(count)])  22.8 us
    dot_general x10, matrix products, partial(): up = jnp.dot(rows, up_weight, preferred_element_type=jnp.float32)  12.8 us
    dot_general x10, matrix products, partial(): gate = jnp.dot(rows, gate_weight, preferred_element_type=jnp.float32)  8.27 us
  transfers between devices with their start and end apart: 17, of which 9 were waited for; matrix products, arithmetic and copies ran while one was open for 21% of the time, Pallas kernels for 0%

profile of v6, /device:TPU:1, one launch (start us, length us, event | category | flops | bytes accessed | tf_op | source)
XLA Modules:
  0.0 98.0 jit_solution(6493003763542326456)
XLA Ops:
  0.0 1.4 %fusion.19 = (bf16[64,4096]{1,0:T(8,128)(2,1)S(1)}, bf16[64,4096]{1,0:T(8,128)(2,1)S(1)}) fusion(bf16[128,4096]{1,0:T(8,128)(2,1)} %param.4), kind=kLoop, calls=%fused_computation.54 | loop fusion | bytes 2097152 | tf_op jit(solution)/shard_map/slice | solution.py:71
  1.4 2.2 %collective-permute-start.2 = (bf16[64,4096]{1,0:T(8,128)(2,1)S(1)}, bf16[64,4096]{1,0:T(8,128)(2,1)S(1)}, u32[]{:S(2)}, u32[]{:S(2)}) collective-permute-start(bf16[64,4096]{1,0:T(8,128)(2,1)S(1)} %get-tuple-element.19), channel_id=1, source_target_pairs={{0,4},{4,8},{8,12},{12,0},{1,5},{5,9},{9,13},{13,1},{2,6},{6,10},{... | collective-permute-start | bytes 1572872 | tf_op jit(solution)/shard_map/ppermute | solution.py:23
  3.6 1.5 %collective-permute-start.1 = (bf16[64,4096]{1,0:T(8,128)(2,1)S(1)}, bf16[64,4096]{1,0:T(8,128)(2,1)S(1)}, u32[]{:S(2)}, u32[]{:S(2)}) collective-permute-start(bf16[64,4096]{1,0:T(8,128)(2,1)S(1)} %get-tuple-element.19), channel_id=1, source_target_pairs={{0,12},{4,0},{8,4},{12,8},{1,13},{5,1},{9,5},{13,9},{2,14},{6,2},{... | collective-permute-start | bytes 1572872 | tf_op jit(solution)/shard_map/ppermute | solution.py:23
  5.1 1.3 %collective-permute-start = (s32[128,1]{0,1:T(1,128)}, s32[128,1]{0,1:T(1,128)S(1)}, u32[]{:S(2)}, u32[]{:S(2)}) collective-permute-start(s32[128,1]{0,1:T(1,128)} %param.5), channel_id=1, source_target_pairs={{0,0},{1,4},{2,8},{3,12},{4,1},{5,5},{6,9},{7,13},{8,2},{9,6},{10,... | collective-permute-start | bytes 1544 | tf_op jit(solution)/shard_map/ppermute | solution.py:39
  6.5 3.2 %fusion.15 = f32[64,512]{1,0:T(8,128)S(1)} fusion(bf16[4096,512]{1,0:T(8,128)(2,1)} %param.7, bf16[128,4096]{1,0:T(8,128)(2,1)} %param.4), kind=kOutput, calls=%fused_computation.50 | convolution fusion | flops 268435456 | bytes 4849664 | tf_op jit(solution)/shard_map/dot_general | solution.py:43
  11.1 3.7 %collective-permute-done.2 = bf16[64,4096]{1,0:T(8,128)(2,1)S(1)} collective-permute-done((bf16[64,4096]{1,0:T(8,128)(2,1)S(1)}, bf16[64,4096]{1,0:T(8,128)(2,1)S(1)}, u32[]{:S(2)}, u32[]{:S(2)}) %collective-permute-start.2) | collective-permute-done | bytes 524320 | tf_op jit(solution)/shard_map/ppermute | solution.py:23
  14.8 1.2 %collective-permute-done.1 = bf16[64,4096]{1,0:T(8,128)(2,1)S(1)} collective-permute-done((bf16[64,4096]{1,0:T(8,128)(2,1)S(1)}, bf16[64,4096]{1,0:T(8,128)(2,1)S(1)}, u32[]{:S(2)}, u32[]{:S(2)}) %collective-permute-start.1) | collective-permute-done | bytes 524320 | tf_op jit(solution)/shard_map/ppermute | solution.py:23
  15.9 1.5 %collective-permute-start.10 = (bf16[64,4096]{1,0:T(8,128)(2,1)S(1)}, bf16[64,4096]{1,0:T(8,128)(2,1)S(1)}, u32[]{:S(2)}, u32[]{:S(2)}) collective-permute-start(bf16[64,4096]{1,0:T(8,128)(2,1)S(1)} %get-tuple-element.6), channel_id=1, source_target_pairs={{0,4},{4,8},{8,12},{12,0},{1,5},{5,9},{9,13},{13,1},{2,6},{6,10},{... | collective-permute-start | bytes 1572872 | tf_op jit(solution)/shard_map/ppermute | solution.py:23
  17.4 1.2 %collective-permute-start.9 = (bf16[64,4096]{1,0:T(8,128)(2,1)S(1)}, bf16[64,4096]{1,0:T(8,128)(2,1)S(1)}, u32[]{:S(2)}, u32[]{:S(2)}) collective-permute-start(bf16[64,4096]{1,0:T(8,128)(2,1)S(1)} %get-tuple-element.6), channel_id=1, source_target_pairs={{0,12},{4,0},{8,4},{12,8},{1,13},{5,1},{9,5},{13,9},{2,14},{6,2},{... | collective-permute-start | bytes 1572872 | tf_op jit(solution)/shard_map/ppermute | solution.py:23
  19.0 2.4 %collective-permute-start.4 = (bf16[32,4096]{1,0:T(8,128)(2,1)S(1)}, bf16[32,4096]{1,0:T(8,128)(2,1)S(1)}, u32[]{:S(2)}, u32[]{:S(2)}) collective-permute-start(bf16[32,4096]{1,0:T(8,128)(2,1)S(1)} %slice.129), channel_id=1, source_target_pairs={{0,12},{4,0},{8,4},{12,8},{1,13},{5,1},{9,5},{13,9},{2,14},{6,2},{... | collective-permute-start | bytes 786440 | tf_op jit(solution)/shard_map/ppermute | solution.py:23
  21.5 3.0 %fusion.27 = f32[64,512]{1,0:T(8,128)S(1)} fusion(bf16[64,4096]{1,0:T(8,128)(2,1)S(1)} %collective-permute-done.2, bf16[4096,512]{1,0:T(8,128)(2,1)} %param.7), kind=kOutput, calls=%fused_computation.62 | convolution fusion | flops 268435456 | bytes 4849664 | tf_op jit(solution)/shard_map/dot_general | solution.py:43
  26.2 0.8 fusion.20
  27.9 6.3 %collective-permute-done.3 = bf16[32,4096]{1,0:T(8,128)(2,1)S(1)} collective-permute-done((bf16[32,4096]{1,0:T(8,128)(2,1)S(1)}, bf16[32,4096]{1,0:T(8,128)(2,1)S(1)}, u32[]{:S(2)}, u32[]{:S(2)}) %collective-permute-start.3) | collective-permute-done | bytes 262176 | tf_op jit(solution)/shard_map/ppermute | solution.py:23
  37.7 3.7 %collective-permute-start.5 = (f32[32,1024]{1,0:T(8,128)S(1)}, f32[32,1024]{1,0:T(8,128)S(1)}, u32[]{:S(2)}, u32[]{:S(2)}) collective-permute-start(f32[32,1024]{1,0:T(8,128)S(1)} %get-tuple-element.9), channel_id=1, source_target_pairs={{0,3},{1,0},{2,1},{3,2},{4,7},{5,4},{6,5},{7,6},{8,11},{9,8},{10,9... | collective-permute-start | bytes 393224 | tf_op jit(solution)/shard_map/ppermute | solution.py:23
  42.2 1.1 %collective-permute-done.5 = f32[32,1024]{1,0:T(8,128)S(1)} collective-permute-done((f32[32,1024]{1,0:T(8,128)S(1)}, f32[32,1024]{1,0:T(8,128)S(1)}, u32[]{:S(2)}, u32[]{:S(2)}) %collective-permute-start.5) | collective-permute-done | bytes 131104 | tf_op jit(solution)/shard_map/ppermute | solution.py:23
  43.3 3.1 %collective-permute-done.7 = f32[32,1024]{1,0:T(8,128)S(1)} collective-permute-done((f32[32,1024]{1,0:T(8,128)S(1)}, f32[32,1024]{1,0:T(8,128)S(1)}, u32[]{:S(2)}, u32[]{:S(2)}) %collective-permute-start.7) | collective-permute-done | bytes 131104 | tf_op jit(solution)/shard_map/ppermute | solution.py:23
  46.8 2.7 %collective-permute-start.12 = (bf16[32,4096]{1,0:T(8,128)(2,1)S(1)}, bf16[32,4096]{1,0:T(8,128)(2,1)S(1)}, u32[]{:S(2)}, u32[]{:S(2)}) collective-permute-start(bf16[32,4096]{1,0:T(8,128)(2,1)S(1)} %slice.131), channel_id=1, source_target_pairs={{0,12},{4,0},{8,4},{12,8},{1,13},{5,1},{9,5},{13,9},{2,14},{6,2},{... | collective-permute-start | bytes 786440 | tf_op jit(solution)/shard_map/ppermute | solution.py:23
  51.2 0.8 fusion.31
  56.7 1.5 %collective-permute-start.15 = (f32[32,1024]{1,0:T(8,128)S(1)}, f32[32,1024]{1,0:T(8,128)S(1)}, u32[]{:S(2)}, u32[]{:S(2)}) collective-permute-start(f32[32,1024]{1,0:T(8,128)S(1)} %get-tuple-element.17), channel_id=1, source_target_pairs={{0,1},{1,2},{2,3},{3,0},{4,5},{5,6},{6,7},{7,4},{8,9},{9,10},{10,1... | collective-permute-start | bytes 393224 | tf_op jit(solution)/shard_map/ppermute | solution.py:23
  58.3 2.7 %collective-permute-start.6 = (f32[64,1024]{1,0:T(8,128)S(1)}, f32[64,1024]{1,0:T(8,128)S(1)}, u32[]{:S(2)}, u32[]{:S(2)}) collective-permute-start(f32[64,1024]{1,0:T(8,128)S(1)} %pad_maximum_fusion.3), channel_id=1, source_target_pairs={{0,3},{1,0},{2,1},{3,2},{4,7},{5,4},{6,5},{7,6},{8,11},{9,8},{10,9... | collective-permute-start | bytes 786440 | tf_op jit(solution)/shard_map/ppermute | solution.py:23
  62.1 2.6 %collective-permute-start.14 = (f32[64,1024]{1,0:T(8,128)S(1)}, f32[64,1024]{1,0:T(8,128)S(1)}, u32[]{:S(2)}, u32[]{:S(2)}) collective-permute-start(f32[64,1024]{1,0:T(8,128)S(1)} %pad_maximum_fusion.5), channel_id=1, source_target_pairs={{0,3},{1,0},{2,1},{3,2},{4,7},{5,4},{6,5},{7,6},{8,11},{9,8},{10,9... | collective-permute-start | bytes 786440 | tf_op jit(solution)/shard_map/ppermute | solution.py:23
  64.7 1.0 %collective-permute-done.6 = f32[64,1024]{1,0:T(8,128)S(1)} collective-permute-done((f32[64,1024]{1,0:T(8,128)S(1)}, f32[64,1024]{1,0:T(8,128)S(1)}, u32[]{:S(2)}, u32[]{:S(2)}) %collective-permute-start.6) | collective-permute-done | bytes 262176 | tf_op jit(solution)/shard_map/ppermute | solution.py:23
  65.8 5.5 %collective-permute-done.16 = f32[64,1024]{1,0:T(8,128)S(1)} collective-permute-done((f32[64,1024]{1,0:T(8,128)S(1)}, f32[64,1024]{1,0:T(8,128)S(1)}, u32[]{:S(2)}, u32[]{:S(2)}) %collective-permute-start.16) | collective-permute-done | bytes 262176 | tf_op jit(solution)/shard_map/ppermute | solution.py:23
  71.7 25.6 %all_to_all.5 = bf16[16,16,512]{2,1,0:T(8,128)(2,1)S(1)} all-to-all(bf16[16,16,512]{2,1,0:T(8,128)(2,1)S(1)} %bitcast.104), channel_id=1, replica_groups=mesh['batch'=16,'wx'=4,'wy'=4] {'batch'}, dimensions={0} | all-to-all | bytes 524288 | tf_op jit(solution)/shard_map/all_to_all | solution.py:82
  (70 shorter events, 17.6 us)
Async XLA Ops:
  0.0 9.6 %copy-start.3 = (bf16[128,4096]{1,0:T(8,128)(2,1)S(1)}, bf16[128,4096]{1,0:T(8,128)(2,1)}, u32[]{:S(2)}) copy-start(bf16[128,4096]{1,0:T(8,128)(2,1)} %param.4) | copy-start | bytes 3145732
  0.0 9.7 %copy-start.1 = (bf16[4096,512]{1,0:T(8,128)(2,1)S(1)}, bf16[4096,512]{1,0:T(8,128)(2,1)}, u32[]{:S(2)}) copy-start(bf16[4096,512]{1,0:T(8,128)(2,1)} %param.6) | copy-start | bytes 12582916
  1.4 13.3 %collective-permute-start.2 = (bf16[64,4096]{1,0:T(8,128)(2,1)S(1)}, bf16[64,4096]{1,0:T(8,128)(2,1)S(1)}, u32[]{:S(2)}, u32[]{:S(2)}) collective-permute-start(bf16[64,4096]{1,0:T(8,128)(2,1)S(1)} %get-tuple-element.19), channel_id=1, source_target_pairs={{0,4},{4,8},{8,12},{12,0},{1,5},{5,9},{9,13},{13,1},{2,6},{6,10},{... | collective-permute-start | bytes 1572872 | tf_op jit(solution)/shard_map/ppermute | solution.py:23
  3.6 12.3 %collective-permute-start.1 = (bf16[64,4096]{1,0:T(8,128)(2,1)S(1)}, bf16[64,4096]{1,0:T(8,128)(2,1)S(1)}, u32[]{:S(2)}, u32[]{:S(2)}) collective-permute-start(bf16[64,4096]{1,0:T(8,128)(2,1)S(1)} %get-tuple-element.19), channel_id=1, source_target_pairs={{0,12},{4,0},{8,4},{12,8},{1,13},{5,1},{9,5},{13,9},{2,14},{6,2},{... | collective-permute-start | bytes 1572872 | tf_op jit(solution)/shard_map/ppermute | solution.py:23
  5.1 5.5 %collective-permute-start = (s32[128,1]{0,1:T(1,128)}, s32[128,1]{0,1:T(1,128)S(1)}, u32[]{:S(2)}, u32[]{:S(2)}) collective-permute-start(s32[128,1]{0,1:T(1,128)} %param.5), channel_id=1, source_target_pairs={{0,0},{1,4},{2,8},{3,12},{4,1},{5,5},{6,9},{7,13},{8,2},{9,6},{10,... | collective-permute-start | bytes 1544 | tf_op jit(solution)/shard_map/ppermute | solution.py:39
  10.9 13.6 %copy-start.2 = (bf16[4096,512]{1,0:T(8,128)(2,1)S(1)}, bf16[4096,512]{1,0:T(8,128)(2,1)}, u32[]{:S(2)}) copy-start(bf16[4096,512]{1,0:T(8,128)(2,1)} %param.6) | copy-start | bytes 12582916
  15.9 30.5 %collective-permute-start.10 = (bf16[64,4096]{1,0:T(8,128)(2,1)S(1)}, bf16[64,4096]{1,0:T(8,128)(2,1)S(1)}, u32[]{:S(2)}, u32[]{:S(2)}) collective-permute-start(bf16[64,4096]{1,0:T(8,128)(2,1)S(1)} %get-tuple-element.6), channel_id=1, source_target_pairs={{0,4},{4,8},{8,12},{12,0},{1,5},{5,9},{9,13},{13,1},{2,6},{6,10},{... | collective-permute-start | bytes 1572872 | tf_op jit(solution)/shard_map/ppermute | solution.py:23
  17.4 29.3 %collective-permute-start.9 = (bf16[64,4096]{1,0:T(8,128)(2,1)S(1)}, bf16[64,4096]{1,0:T(8,128)(2,1)S(1)}, u32[]{:S(2)}, u32[]{:S(2)}) collective-permute-start(bf16[64,4096]{1,0:T(8,128)(2,1)S(1)} %get-tuple-element.6), channel_id=1, source_target_pairs={{0,12},{4,0},{8,4},{12,8},{1,13},{5,1},{9,5},{13,9},{2,14},{6,2},{... | collective-permute-start | bytes 1572872 | tf_op jit(solution)/shard_map/ppermute | solution.py:23
  18.6 15.6 %collective-permute-start.3 = (bf16[32,4096]{1,0:T(8,128)(2,1)S(1)}, bf16[32,4096]{1,0:T(8,128)(2,1)S(1)}, u32[]{:S(2)}, u32[]{:S(2)}) collective-permute-start(bf16[32,4096]{1,0:T(8,128)(2,1)S(1)} %slice.128), channel_id=1, source_target_pairs={{0,4},{4,8},{8,12},{12,0},{1,5},{5,9},{9,13},{13,1},{2,6},{6,10},{... | collective-permute-start | bytes 786440 | tf_op jit(solution)/shard_map/ppermute | solution.py:23
  19.0 6.4 %copy-start = (bf16[4096,512]{1,0:T(8,128)(2,1)S(1)}, bf16[4096,512]{1,0:T(8,128)(2,1)}, u32[]{:S(2)}) copy-start(bf16[4096,512]{1,0:T(8,128)(2,1)} %param.7) | copy-start | bytes 12582916
  19.0 16.8 %collective-permute-start.4 = (bf16[32,4096]{1,0:T(8,128)(2,1)S(1)}, bf16[32,4096]{1,0:T(8,128)(2,1)S(1)}, u32[]{:S(2)}, u32[]{:S(2)}) collective-permute-start(bf16[32,4096]{1,0:T(8,128)(2,1)S(1)} %slice.129), channel_id=1, source_target_pairs={{0,12},{4,0},{8,4},{12,8},{1,13},{5,1},{9,5},{13,9},{2,14},{6,2},{... | collective-permute-start | bytes 786440 | tf_op jit(solution)/shard_map/ppermute | solution.py:23
  37.7 5.6 %collective-permute-start.5 = (f32[32,1024]{1,0:T(8,128)S(1)}, f32[32,1024]{1,0:T(8,128)S(1)}, u32[]{:S(2)}, u32[]{:S(2)}) collective-permute-start(f32[32,1024]{1,0:T(8,128)S(1)} %get-tuple-element.9), channel_id=1, source_target_pairs={{0,3},{1,0},{2,1},{3,2},{4,7},{5,4},{6,5},{7,6},{8,11},{9,8},{10,9... | collective-permute-start | bytes 393224 | tf_op jit(solution)/shard_map/ppermute | solution.py:23
  41.4 5.0 %collective-permute-start.7 = (f32[32,1024]{1,0:T(8,128)S(1)}, f32[32,1024]{1,0:T(8,128)S(1)}, u32[]{:S(2)}, u32[]{:S(2)}) collective-permute-start(f32[32,1024]{1,0:T(8,128)S(1)} %get-tuple-element.11), channel_id=1, source_target_pairs={{0,1},{1,2},{2,3},{3,0},{4,5},{5,6},{6,7},{7,4},{8,9},{9,10},{10,1... | collective-permute-start | bytes 393224 | tf_op jit(solution)/shard_map/ppermute | solution.py:23
  46.5 6.7 %collective-permute-start.11 = (bf16[32,4096]{1,0:T(8,128)(2,1)S(1)}, bf16[32,4096]{1,0:T(8,128)(2,1)S(1)}, u32[]{:S(2)}, u32[]{:S(2)}) collective-permute-start(bf16[32,4096]{1,0:T(8,128)(2,1)S(1)} %slice.130), channel_id=1, source_target_pairs={{0,4},{4,8},{8,12},{12,0},{1,5},{5,9},{9,13},{13,1},{2,6},{6,10},{... | collective-permute-start | bytes 786440 | tf_op jit(solution)/shard_map/ppermute | solution.py:23
  46.8 8.0 %collective-permute-start.12 = (bf16[32,4096]{1,0:T(8,128)(2,1)S(1)}, bf16[32,4096]{1,0:T(8,128)(2,1)S(1)}, u32[]{:S(2)}, u32[]{:S(2)}) collective-permute-start(bf16[32,4096]{1,0:T(8,128)(2,1)S(1)} %slice.131), channel_id=1, source_target_pairs={{0,12},{4,0},{8,4},{12,8},{1,13},{5,1},{9,5},{13,9},{2,14},{6,2},{... | collective-permute-start | bytes 786440 | tf_op jit(solution)/shard_map/ppermute | solution.py:23
  56.6 4.4 %collective-permute-start.13 = (f32[32,1024]{1,0:T(8,128)S(1)}, f32[32,1024]{1,0:T(8,128)S(1)}, u32[]{:S(2)}, u32[]{:S(2)}) collective-permute-start(f32[32,1024]{1,0:T(8,128)S(1)} %get-tuple-element.15), channel_id=1, source_target_pairs={{0,3},{1,0},{2,1},{3,2},{4,7},{5,4},{6,5},{7,6},{8,11},{9,8},{10,9... | collective-permute-start | bytes 393224 | tf_op jit(solution)/shard_map/ppermute | solution.py:23
  56.7 5.1 %collective-permute-start.15 = (f32[32,1024]{1,0:T(8,128)S(1)}, f32[32,1024]{1,0:T(8,128)S(1)}, u32[]{:S(2)}, u32[]{:S(2)}) collective-permute-start(f32[32,1024]{1,0:T(8,128)S(1)} %get-tuple-element.17), channel_id=1, source_target_pairs={{0,1},{1,2},{2,3},{3,0},{4,5},{5,6},{6,7},{7,4},{8,9},{9,10},{10,1... | collective-permute-start | bytes 393224 | tf_op jit(solution)/shard_map/ppermute | solution.py:23
  58.2 6.6 %collective-permute-start.8 = (f32[64,1024]{1,0:T(8,128)S(1)}, f32[64,1024]{1,0:T(8,128)S(1)}, u32[]{:S(2)}, u32[]{:S(2)}) collective-permute-start(f32[64,1024]{1,0:T(8,128)S(1)} %pad_maximum_fusion.4), channel_id=1, source_target_pairs={{0,1},{1,2},{2,3},{3,0},{4,5},{5,6},{6,7},{7,4},{8,9},{9,10},{10,1... | collective-permute-start | bytes 786440 | tf_op jit(solution)/shard_map/ppermute | solution.py:23
  58.3 7.5 %collective-permute-start.6 = (f32[64,1024]{1,0:T(8,128)S(1)}, f32[64,1024]{1,0:T(8,128)S(1)}, u32[]{:S(2)}, u32[]{:S(2)}) collective-permute-start(f32[64,1024]{1,0:T(8,128)S(1)} %pad_maximum_fusion.3), channel_id=1, source_target_pairs={{0,3},{1,0},{2,1},{3,2},{4,7},{5,4},{6,5},{7,6},{8,11},{9,8},{10,9... | collective-permute-start | bytes 786440 | tf_op jit(solution)/shard_map/ppermute | solution.py:23
  61.9 9.4 %collective-permute-start.16 = (f32[64,1024]{1,0:T(8,128)S(1)}, f32[64,1024]{1,0:T(8,128)S(1)}, u32[]{:S(2)}, u32[]{:S(2)}) collective-permute-start(f32[64,1024]{1,0:T(8,128)S(1)} %pad_maximum_fusion.6), channel_id=1, source_target_pairs={{0,1},{1,2},{2,3},{3,0},{4,5},{5,6},{6,7},{7,4},{8,9},{9,10},{10,1... | collective-permute-start | bytes 786440 | tf_op jit(solution)/shard_map/ppermute | solution.py:23
  62.1 9.1 %collective-permute-start.14 = (f32[64,1024]{1,0:T(8,128)S(1)}, f32[64,1024]{1,0:T(8,128)S(1)}, u32[]{:S(2)}, u32[]{:S(2)}) collective-permute-start(f32[64,1024]{1,0:T(8,128)S(1)} %pad_maximum_fusion.5), channel_id=1, source_target_pairs={{0,3},{1,0},{2,1},{3,2},{4,7},{5,4},{6,5},{7,6},{8,11},{9,8},{10,9... | collective-permute-start | bytes 786440 | tf_op jit(solution)/shard_map/ppermute | solution.py:23

commit v7 on v2

--- a/solution.py
+++ b/solution.py
@@ -50,13 +50,24 @@
     far_b = shift(from_right[half:], "wx", nx, -1)
     part_left = partial(from_left)
     part_right = partial(from_right)
+
+    near = jnp.stack([part_own, part_right, part_own, part_left])
+    total = jnp.zeros_like(part_own)
+    for d in range(1, ny):
+        route = [
+            (w * ny + v, w * ny + (v + d) % ny)
+            for w in range(nx)
+            for v in range(ny)
+            if (v + d) % ny != (w + 2) % ny
+        ]
+        send = lax.dynamic_index_in_dim(near, (y + d - x) % nx, 0, keepdims=False)
+        total = total + lax.ppermute(send, ("wx", "wy"), route)
     part_far = jnp.concatenate([partial(far_a), partial(far_b)], axis=0)
+    for d in range(1, ny):
+        route = [(w * ny + (w + 2 - d) % ny, w * ny + (w + 2) % ny) for w in range(nx)]
+        total = total + lax.ppermute(part_far, ("wx", "wy"), route)
     parts = jnp.stack([part_own, part_right, part_far, part_left])
-
-    total = lax.dynamic_index_in_dim(parts, (y - x) % nx, 0, keepdims=False)
-    for d in (1, 2, 3):
-        send = lax.dynamic_index_in_dim(parts, (y + d - x) % nx, 0, keepdims=False)
-        total = total + shift(send, "wy", ny, d)
+    total = total + lax.dynamic_index_in_dim(parts, (y - x) % nx, 0, keepdims=False)
     gate_sum, up_sum = total[:, :hid], total[:, hid:]
     hidden = (jax.nn.silu(gate_sum) * up_sum).astype(jnp.bfloat16)
     placed = place_rows(hidden, group_of, slots, groups_total)

time: 95.1 us -> 101 us (1.062)
  the two profiles are of different devices: /device:TPU:1 before, /device:TPU:17 now
where the time goes in v7:
time: 101 us
  waiting for transfers between devices  38.5 us (38%)
  starting transfers between devices  24.6 us (24%)
  blocking collectives  20.4 us (20%)
  matrix products  10.9 us (11%)
  other arithmetic  3.79 us (4%)
  local copies, waits for them, and re-layouts  2.27 us (2%)
    all_to_all x1, blocking collectives, per_device(): lax.all_to_all(placed, 'batch', split_axis=0, concat_axis=0, tiled=True)  20.4 us
    ppermute x3, waiting for transfers between devices, per_device(): total = total + lax.ppermute(part_far, ('wx', 'wy'), route)  19.1 us
    ppermute x4, waiting for transfers between devices, shift(): lax.ppermute(value, axis, [(i, (i + step) % count) for i in range(count)])  12.8 us
    ppermute x3, starting transfers between devices, per_device(): total = total + lax.ppermute(send, ('wx', 'wy'), route)  11.1 us
    ppermute x3, waiting for transfers between devices, per_device(): total = total + lax.ppermute(send, ('wx', 'wy'), route)  6.6 us
    dot_general x5, matrix products, partial(): up = jnp.dot(rows, up_weight, preferred_element_type=jnp.float32)  6.57 us
    ppermute x1, starting transfers between devices, per_device(): group_of = lax.ppermute(routes, ('wx', 'wy'), pairs)[:, 0]  5.68 us
    dot_general x5, matrix products, partial(): gate = jnp.dot(rows, gate_weight, preferred_element_type=jnp.float32)  3.99 us
  transfers between devices with their start and end apart: 11, of which 6 were waited for; matrix products, arithmetic and copies ran while one was open for 13% of the time, Pallas kernels for 0%

profile of v7, /device:TPU:17, one launch (start us, length us, event | category | flops | bytes accessed | tf_op | source)
XLA Modules:
  0.0 100.7 jit_solution(3480793456874201137)
XLA Ops:
  0.2 1.3 %collective-permute-start.2 = (bf16[128,4096]{1,0:T(8,128)(2,1)}, bf16[128,4096]{1,0:T(8,128)(2,1)S(1)}, u32[]{:S(2)}, u32[]{:S(2)}) collective-permute-start(bf16[128,4096]{1,0:T(8,128)(2,1)} %param.4), channel_id=1, source_target_pairs={{0,4},{4,8},{8,12},{12,0},{1,5},{5,9},{9,13},{13,1},{2,6},{6,10},{... | collective-permute-start | bytes 3145736 | tf_op jit(solution)/shard_map/ppermute | solution.py:23
  1.5 5.7 %collective-permute-start = (s32[128,1]{0,1:T(1,128)}, s32[128,1]{0,1:T(1,128)S(1)}, u32[]{:S(2)}, u32[]{:S(2)}) collective-permute-start(s32[128,1]{0,1:T(1,128)} %param.5), channel_id=1, source_target_pairs={{0,0},{1,4},{2,8},{3,12},{4,1},{5,5},{6,9},{7,13},{8,2},{9,6},{10,... | collective-permute-start | bytes 1544 | tf_op jit(solution)/shard_map/ppermute | solution.py:39
  7.2 3.4 %fusion.14 = f32[128,512]{1,0:T(8,128)S(1)} fusion(bf16[128,4096]{1,0:T(8,128)(2,1)} %param.4, bf16[4096,512]{1,0:T(8,128)(2,1)} %param.7), kind=kOutput, calls=%fused_computation.32 | convolution fusion | flops 536870912 | bytes 5505024 | tf_op jit(solution)/shard_map/dot_general | solution.py:43
  11.8 12.4 %collective-permute-done.1 = bf16[128,4096]{1,0:T(8,128)(2,1)S(1)} collective-permute-done((bf16[128,4096]{1,0:T(8,128)(2,1)}, bf16[128,4096]{1,0:T(8,128)(2,1)S(1)}, u32[]{:S(2)}, u32[]{:S(2)}) %collective-permute-start.1) | collective-permute-done | bytes 1048608 | tf_op jit(solution)/shard_map/ppermute | solution.py:23
  24.6 2.2 %collective-permute-start.6 = (bf16[64,4096]{1,0:T(8,128)(2,1)S(1)}, bf16[64,4096]{1,0:T(8,128)(2,1)S(1)}, u32[]{:S(2)}, u32[]{:S(2)}) collective-permute-start(bf16[64,4096]{1,0:T(8,128)(2,1)S(1)} %slice.16), channel_id=1, source_target_pairs={{0,4},{4,8},{8,12},{12,0},{1,5},{5,9},{9,13},{13,1},{2,6},{6,10},{... | collective-permute-start | bytes 1572872 | tf_op jit(solution)/shard_map/ppermute | solution.py:23
  28.3 0.8 fusion.18
  29.1 0.8 fusion.17
  30.2 1.1 %dynamic-slice_bitcast_fusion.1 = (f32[128,1024]{1,0:T(8,128)}, f32[128,1024]{1,0:T(8,128)S(1)}, f32[128,1024]{1,0:T(8,128)}) fusion(f32[4,128,1024]{2,1,0:T(8,128)S(1)} %pad_maximum_fusion, s32[]{:T(128)S(6)} %select_n.35, s32[]{:T(128)S(6)} %select_n.37, s32[]{:T(128)S(6)} %select_n.33), kind=kLoop, calls=%fused_computation.18 | loop fusion | bytes 3145740 | tf_op jit(solution)/shard_map/jit(dynamic_index_in_dim)/squeeze | solution.py:63
  31.3 4.4 %collective-permute-start.5 = (f32[128,1024]{1,0:T(8,128)S(1)}, f32[128,1024]{1,0:T(8,128)S(1)}, u32[]{:S(2)}, u32[]{:S(2)}) collective-permute-start(f32[128,1024]{1,0:T(8,128)S(1)} %get-tuple-element.6), channel_id=1, source_target_pairs={{0,3},{1,0},{2,1},{5,4},{6,5},{7,6},{8,11},{10,9},{11,10},{12,15},... | collective-permute-start | bytes 1572872 | tf_op jit(solution)/shard_map/ppermute | solution.py:64
  35.7 1.3 %collective-permute-start.3 = (f32[128,1024]{1,0:T(8,128)}, f32[128,1024]{1,0:T(8,128)S(1)}, u32[]{:S(2)}, u32[]{:S(2)}) collective-permute-start(f32[128,1024]{1,0:T(8,128)} %get-tuple-element.7), channel_id=1, source_target_pairs={{0,1},{2,3},{3,0},{4,5},{5,6},{7,4},{8,9},{9,10},{10,11},{13,14},{... | collective-permute-start | bytes 1572872 | tf_op jit(solution)/shard_map/ppermute | solution.py:64
  37.4 5.4 %collective-permute-start.4 = (f32[128,1024]{1,0:T(8,128)}, f32[128,1024]{1,0:T(8,128)}, u32[]{:S(2)}, u32[]{:S(2)}) collective-permute-start(f32[128,1024]{1,0:T(8,128)} %get-tuple-element.5), channel_id=1, source_target_pairs={{1,3},{2,0},{3,1},{4,6},{6,4},{7,5},{8,10},{9,11},{11,9},{12,14},{... | collective-permute-start | bytes 1572872 | tf_op jit(solution)/shard_map/ppermute | solution.py:64
  42.8 0.8 fusion.22
  43.6 0.8 fusion.21
  44.5 0.8 fusion.20
  45.3 0.8 fusion.19
  46.2 0.9 maximum_maximum_fusion
  47.1 1.3 %collective-permute-start.10 = (f32[128,1024]{1,0:T(8,128)}, f32[128,1024]{1,0:T(8,128)}, u32[]{:S(2)}, u32[]{:S(2)}) collective-permute-start(f32[128,1024]{1,0:T(8,128)} %get-tuple-element.8), channel_id=1, source_target_pairs={{3,2},{4,7},{9,8},{14,13},{19,18},{20,23},{25,24},{30,29},{35,34},... | collective-permute-start | bytes 1572872 | tf_op jit(solution)/shard_map/ppermute | solution.py:68
  48.4 1.3 %collective-permute-start.9 = (f32[128,1024]{1,0:T(8,128)}, f32[128,1024]{1,0:T(8,128)}, u32[]{:S(2)}, u32[]{:S(2)}) collective-permute-start(f32[128,1024]{1,0:T(8,128)} %get-tuple-element.8), channel_id=1, source_target_pairs={{0,2},{5,7},{10,8},{15,13},{16,18},{21,23},{26,24},{31,29},{32,34}... | collective-permute-start | bytes 1572872 | tf_op jit(solution)/shard_map/ppermute | solution.py:68
  49.7 6.1 %collective-permute-done.5 = f32[128,1024]{1,0:T(8,128)S(1)} collective-permute-done((f32[128,1024]{1,0:T(8,128)S(1)}, f32[128,1024]{1,0:T(8,128)S(1)}, u32[]{:S(2)}, u32[]{:S(2)}) %collective-permute-start.5) | collective-permute-done | bytes 524320 | tf_op jit(solution)/shard_map/ppermute | solution.py:64
  55.8 1.3 %collective-permute-start.8 = (f32[128,1024]{1,0:T(8,128)}, f32[128,1024]{1,0:T(8,128)}, u32[]{:S(2)}, u32[]{:S(2)}) collective-permute-start(f32[128,1024]{1,0:T(8,128)} %get-tuple-element.8), channel_id=1, source_target_pairs={{1,2},{6,7},{11,8},{12,13},{17,18},{22,23},{27,24},{28,29},{33,34}... | collective-permute-start | bytes 1572872 | tf_op jit(solution)/shard_map/ppermute | solution.py:68
  58.0 5.8 %collective-permute-done.10 = f32[128,1024]{1,0:T(8,128)} collective-permute-done((f32[128,1024]{1,0:T(8,128)}, f32[128,1024]{1,0:T(8,128)}, u32[]{:S(2)}, u32[]{:S(2)}) %collective-permute-start.10) | collective-permute-done | bytes 524320 | tf_op jit(solution)/shard_map/ppermute | solution.py:68
  63.9 13.3 %collective-permute-done.8 = f32[128,1024]{1,0:T(8,128)} collective-permute-done((f32[128,1024]{1,0:T(8,128)}, f32[128,1024]{1,0:T(8,128)}, u32[]{:S(2)}, u32[]{:S(2)}) %collective-permute-start.8) | collective-permute-done | bytes 524320 | tf_op jit(solution)/shard_map/ppermute | solution.py:68
  77.2 2.1 %fusion.4 = f32[128,1024]{1,0:T(8,128)S(1)} fusion(s32[]{:T(128)S(6)} %select_n.39, f32[1,128,1024]{2,1,0:T(8,128)S(1)} %get-tuple-element.9, f32[1,128,1024]{2,1,0:T(8,128)S(1)} %maximum_bitcast_fusion, f32[1,128,1024]{2,1,0:T(8,128)S(1)} %maximum_bitcast_fusion.1, f32[1,128,1024]{2,1,0:T(8,128)S(1)} %maximum_bitcast_fusion.2, ...), kind=kLoop, calls=%fused_computation.11 | loop fusion | flops 1179648 | bytes 5767172 | tf_op jit(solution)/shard_map/add | solution.py:70
  79.6 20.4 %all_to_all.5 = bf16[16,16,512]{2,1,0:T(8,128)(2,1)S(1)} all-to-all(bf16[16,16,512]{2,1,0:T(8,128)(2,1)S(1)} %bitcast.48), channel_id=1, replica_groups=mesh['batch'=16,'wx'=4,'wy'=4] {'batch'}, dimensions={0} | all-to-all | bytes 524288 | tf_op jit(solution)/shard_map/all_to_all | solution.py:75
  (30 shorter events, 5.8 us)
Async XLA Ops:
  0.0 10.6 %copy-start.2 = (bf16[128,4096]{1,0:T(8,128)(2,1)S(1)}, bf16[128,4096]{1,0:T(8,128)(2,1)}, u32[]{:S(2)}) copy-start(bf16[128,4096]{1,0:T(8,128)(2,1)} %param.4) | copy-start | bytes 3145732
  0.0 24.3 %collective-permute-start.1 = (bf16[128,4096]{1,0:T(8,128)(2,1)}, bf16[128,4096]{1,0:T(8,128)(2,1)S(1)}, u32[]{:S(2)}, u32[]{:S(2)}) collective-permute-start(bf16[128,4096]{1,0:T(8,128)(2,1)} %param.4), channel_id=1, source_target_pairs={{0,12},{4,0},{8,4},{12,8},{1,13},{5,1},{9,5},{13,9},{2,14},{6,2},{... | collective-permute-start | bytes 3145736 | tf_op jit(solution)/shard_map/ppermute | solution.py:23
  0.2 24.4 %collective-permute-start.2 = (bf16[128,4096]{1,0:T(8,128)(2,1)}, bf16[128,4096]{1,0:T(8,128)(2,1)S(1)}, u32[]{:S(2)}, u32[]{:S(2)}) collective-permute-start(bf16[128,4096]{1,0:T(8,128)(2,1)} %param.4), channel_id=1, source_target_pairs={{0,4},{4,8},{8,12},{12,0},{1,5},{5,9},{9,13},{13,1},{2,6},{6,10},{... | collective-permute-start | bytes 3145736 | tf_op jit(solution)/shard_map/ppermute | solution.py:23
  1.5 46.9 %collective-permute-start = (s32[128,1]{0,1:T(1,128)}, s32[128,1]{0,1:T(1,128)S(1)}, u32[]{:S(2)}, u32[]{:S(2)}) collective-permute-start(s32[128,1]{0,1:T(1,128)} %param.5), channel_id=1, source_target_pairs={{0,0},{1,4},{2,8},{3,12},{4,1},{5,5},{6,9},{7,13},{8,2},{9,6},{10,... | collective-permute-start | bytes 1544 | tf_op jit(solution)/shard_map/ppermute | solution.py:39
  7.2 3.7 %copy-start.1 = (bf16[4096,512]{1,0:T(8,128)(2,1)S(1)}, bf16[4096,512]{1,0:T(8,128)(2,1)}, u32[]{:S(2)}) copy-start(bf16[4096,512]{1,0:T(8,128)(2,1)} %param.6) | copy-start | bytes 12582916
  11.0 15.8 %copy-start = (bf16[4096,512]{1,0:T(8,128)(2,1)S(1)}, bf16[4096,512]{1,0:T(8,128)(2,1)}, u32[]{:S(2)}) copy-start(bf16[4096,512]{1,0:T(8,128)(2,1)} %param.7) | copy-start | bytes 12582916
  24.3 13.1 %collective-permute-start.7 = (bf16[64,4096]{1,0:T(8,128)(2,1)S(1)}, bf16[64,4096]{1,0:T(8,128)(2,1)S(1)}, u32[]{:S(2)}, u32[]{:S(2)}) collective-permute-start(bf16[64,4096]{1,0:T(8,128)(2,1)S(1)} %slice.17), channel_id=1, source_target_pairs={{0,12},{4,0},{8,4},{12,8},{1,13},{5,1},{9,5},{13,9},{2,14},{6,2},{... | collective-permute-start | bytes 1572872 | tf_op jit(solution)/shard_map/ppermute | solution.py:23
  24.6 19.9 %collective-permute-start.6 = (bf16[64,4096]{1,0:T(8,128)(2,1)S(1)}, bf16[64,4096]{1,0:T(8,128)(2,1)S(1)}, u32[]{:S(2)}, u32[]{:S(2)}) collective-permute-start(bf16[64,4096]{1,0:T(8,128)(2,1)S(1)} %slice.16), channel_id=1, source_target_pairs={{0,4},{4,8},{8,12},{12,0},{1,5},{5,9},{9,13},{13,1},{2,6},{6,10},{... | collective-permute-start | bytes 1572872 | tf_op jit(solution)/shard_map/ppermute | solution.py:23
  31.3 24.4 %collective-permute-start.5 = (f32[128,1024]{1,0:T(8,128)S(1)}, f32[128,1024]{1,0:T(8,128)S(1)}, u32[]{:S(2)}, u32[]{:S(2)}) collective-permute-start(f32[128,1024]{1,0:T(8,128)S(1)} %get-tuple-element.6), channel_id=1, source_target_pairs={{0,3},{1,0},{2,1},{5,4},{6,5},{7,6},{8,11},{10,9},{11,10},{12,15},... | collective-permute-start | bytes 1572872 | tf_op jit(solution)/shard_map/ppermute | solution.py:64
  35.7 21.8 %collective-permute-start.3 = (f32[128,1024]{1,0:T(8,128)}, f32[128,1024]{1,0:T(8,128)S(1)}, u32[]{:S(2)}, u32[]{:S(2)}) collective-permute-start(f32[128,1024]{1,0:T(8,128)} %get-tuple-element.7), channel_id=1, source_target_pairs={{0,1},{2,3},{3,0},{4,5},{5,6},{7,4},{8,9},{9,10},{10,11},{13,14},{... | collective-permute-start | bytes 1572872 | tf_op jit(solution)/shard_map/ppermute | solution.py:64
  37.4 20.7 %collective-permute-start.4 = (f32[128,1024]{1,0:T(8,128)}, f32[128,1024]{1,0:T(8,128)}, u32[]{:S(2)}, u32[]{:S(2)}) collective-permute-start(f32[128,1024]{1,0:T(8,128)} %get-tuple-element.5), channel_id=1, source_target_pairs={{1,3},{2,0},{3,1},{4,6},{6,4},{7,5},{8,10},{9,11},{11,9},{12,14},{... | collective-permute-start | bytes 1572872 | tf_op jit(solution)/shard_map/ppermute | solution.py:64
  47.1 16.8 %collective-permute-start.10 = (f32[128,1024]{1,0:T(8,128)}, f32[128,1024]{1,0:T(8,128)}, u32[]{:S(2)}, u32[]{:S(2)}) collective-permute-start(f32[128,1024]{1,0:T(8,128)} %get-tuple-element.8), channel_id=1, source_target_pairs={{3,2},{4,7},{9,8},{14,13},{19,18},{20,23},{25,24},{30,29},{35,34},... | collective-permute-start | bytes 1572872 | tf_op jit(solution)/shard_map/ppermute | solution.py:68
  48.4 15.5 %collective-permute-start.9 = (f32[128,1024]{1,0:T(8,128)}, f32[128,1024]{1,0:T(8,128)}, u32[]{:S(2)}, u32[]{:S(2)}) collective-permute-start(f32[128,1024]{1,0:T(8,128)} %get-tuple-element.8), channel_id=1, source_target_pairs={{0,2},{5,7},{10,8},{15,13},{16,18},{21,23},{26,24},{31,29},{32,34}... | collective-permute-start | bytes 1572872 | tf_op jit(solution)/shard_map/ppermute | solution.py:68
  55.8 21.4 %collective-permute-start.8 = (f32[128,1024]{1,0:T(8,128)}, f32[128,1024]{1,0:T(8,128)}, u32[]{:S(2)}, u32[]{:S(2)}) collective-permute-start(f32[128,1024]{1,0:T(8,128)} %get-tuple-element.8), channel_id=1, source_target_pairs={{1,2},{6,7},{11,8},{12,13},{17,18},{22,23},{27,24},{28,29},{33,34}... | collective-permute-start | bytes 1572872 | tf_op jit(solution)/shard_map/ppermute | solution.py:68

commit v8 on v5

--- a/solution.py
+++ b/solution.py
@@ -50,7 +50,7 @@
     far_b = shift(from_right[half:], "wx", nx, -1)
     part_left = partial(from_left)
     part_right = partial(from_right)
-    part_far = jnp.concatenate([partial(far_a), partial(far_b)], axis=0)
+    part_far = partial(jnp.concatenate([far_a, far_b], axis=0))
     parts = jnp.stack([part_own, part_right, part_far, part_left])
 
     def block(w):
@@ -59,10 +59,8 @@
     far_part = block(y + 2)
     via_right = shift(far_part[:half], "wy", ny, -1)
     via_left = shift(far_part[half:], "wy", ny, 1)
-    to_left = block(y - 1)
-    to_left = jnp.concatenate([to_left[:half] + via_right, to_left[half:]], axis=0)
-    to_right = block(y + 1)
-    to_right = jnp.concatenate([to_right[:half], to_right[half:] + via_left], axis=0)
+    to_left = block(y - 1).at[:half].add(via_right)
+    to_right = block(y + 1).at[half:].add(via_left)
     total = block(y) + shift(to_left, "wy", ny, -1) + shift(to_right, "wy", ny, 1)
     gate_sum, up_sum = total[:, :hid], total[:, hid:]
     hidden = (jax.nn.silu(gate_sum) * up_sum).astype(jnp.bfloat16)

time: 91.8 us -> 90 us (0.980)
  matrix products: 10.9 us -> 9 us
    concatenate x2 -> x0, other arithmetic: 1.65 us -> none  [the longest x1 0.84 us: per_device(): jnp.concatenate([to_right[:half], to_right[half:] + via_left], axis=0)]
    squeeze x0 -> x1, local copies, waits for them, and re-layouts: none -> 1.05 us  [block(): return lax.dynamic_index_in_dim(parts, (w - x) % nx, 0, keepdims=False)]
    dot_general x5 -> x4, matrix products: 3.98 us -> 3.03 us  [partial(): gate = jnp.dot(rows, gate_weight, preferred_element_type=jnp.float32)]
    dot_general x5 -> x4, matrix products: 6.58 us -> 5.63 us  [partial(): up = jnp.dot(rows, up_weight, preferred_element_type=jnp.float32)]
  transfers between devices with their start and end apart: 9 -> 9, of which waited for: 6 -> 7; matrix products, arithmetic and copies ran while one was open for 12% -> 11% of each run, Pallas kernels for 0% -> 0%
where the time goes in v8:
time: 90 us; the launch traced here: 89.8 us
  waiting for transfers between devices  39 us (43%)
  blocking collectives  24.1 us (27%)
  starting transfers between devices  13.5 us (15%)
  matrix products  9 us (10%)
  local copies, waits for them, and re-layouts  2.32 us (3%)
  other arithmetic  1.67 us (2%)
    ppermute x8, waiting for transfers between devices, shift(): lax.ppermute(value, axis, [(i, (i + step) % count) for i in range(count)])  39 us
    all_to_all x1, blocking collectives, per_device(): lax.all_to_all(placed, 'batch', split_axis=0, concat_axis=0, tiled=True)  24.1 us
    ppermute x8, starting transfers between devices, shift(): lax.ppermute(value, axis, [(i, (i + step) % count) for i in range(count)])  12.9 us
    dot_general x4, matrix products, partial(): up = jnp.dot(rows, up_weight, preferred_element_type=jnp.float32)  5.63 us
    dot_general x4, matrix products, partial(): gate = jnp.dot(rows, gate_weight, preferred_element_type=jnp.float32)  3.03 us
  transfers between devices with their start and end apart: 9, of which 7 were waited for; matrix products, arithmetic and copies ran while one was open for 11% of the time, Pallas kernels for 0%

profile of v8, /device:TPU:1, one launch (start us, length us, event | category | flops | bytes accessed | tf_op | source)
XLA Modules:
  0.0 89.8 jit_solution(17370441795860826302)
XLA Ops:
  0.0 2.1 %collective-permute-start.2 = (bf16[128,4096]{1,0:T(8,128)(2,1)}, bf16[128,4096]{1,0:T(8,128)(2,1)S(1)}, u32[]{:S(2)}, u32[]{:S(2)}) collective-permute-start(bf16[128,4096]{1,0:T(8,128)(2,1)} %param.8), channel_id=1, source_target_pairs={{0,4},{4,8},{8,12},{12,0},{1,5},{5,9},{9,13},{13,1},{2,6},{6,10},{... | collective-permute-start | bytes 3145736 | tf_op jit(solution)/shard_map/ppermute | solution.py:23
  2.1 1.5 %collective-permute-start.1 = (bf16[128,4096]{1,0:T(8,128)(2,1)}, bf16[128,4096]{1,0:T(8,128)(2,1)S(1)}, u32[]{:S(2)}, u32[]{:S(2)}) collective-permute-start(bf16[128,4096]{1,0:T(8,128)(2,1)} %param.8), channel_id=1, source_target_pairs={{0,12},{4,0},{8,4},{12,8},{1,13},{5,1},{9,5},{13,9},{2,14},{6,2},{... | collective-permute-start | bytes 3145736 | tf_op jit(solution)/shard_map/ppermute | solution.py:23
  3.6 3.4 %fusion.10 = f32[128,512]{1,0:T(8,128)S(1)} fusion(bf16[128,4096]{1,0:T(8,128)(2,1)} %param.8, bf16[4096,512]{1,0:T(8,128)(2,1)} %param.11), kind=kOutput, calls=%fused_computation.29 | convolution fusion | flops 536870912 | bytes 5505024 | tf_op jit(solution)/shard_map/dot_general | solution.py:43
  7.4 0.8 fusion.9
  8.2 16.6 %collective-permute-done.2 = bf16[128,4096]{1,0:T(8,128)(2,1)S(1)} collective-permute-done((bf16[128,4096]{1,0:T(8,128)(2,1)}, bf16[128,4096]{1,0:T(8,128)(2,1)S(1)}, u32[]{:S(2)}, u32[]{:S(2)}) %collective-permute-start.2) | collective-permute-done | bytes 1048608 | tf_op jit(solution)/shard_map/ppermute | solution.py:23
  24.9 1.4 %collective-permute-start.3 = (bf16[64,4096]{1,0:T(8,128)(2,1)S(1)}, bf16[64,4096]{1,0:T(8,128)(2,1)S(1)}, u32[]{:S(2)}, u32[]{:S(2)}) collective-permute-start(bf16[64,4096]{1,0:T(8,128)(2,1)S(1)} %slice.64), channel_id=1, source_target_pairs={{0,4},{4,8},{8,12},{12,0},{1,5},{5,9},{9,13},{13,1},{2,6},{6,10},{... | collective-permute-start | bytes 1572872 | tf_op jit(solution)/shard_map/ppermute | solution.py:23
  26.3 1.7 %collective-permute-start.4 = (bf16[64,4096]{1,0:T(8,128)(2,1)S(1)}, bf16[64,4096]{1,0:T(8,128)(2,1)S(1)}, u32[]{:S(2)}, u32[]{:S(2)}) collective-permute-start(bf16[64,4096]{1,0:T(8,128)(2,1)S(1)} %slice.65), channel_id=1, source_target_pairs={{0,12},{4,0},{8,4},{12,8},{1,13},{5,1},{9,5},{13,9},{2,14},{6,2},{... | collective-permute-start | bytes 1572872 | tf_op jit(solution)/shard_map/ppermute | solution.py:23
  28.1 0.8 fusion.16
  28.9 0.8 fusion.15
  29.6 0.8 fusion.12
  30.5 0.8 fusion.11
  31.3 5.9 %collective-permute-done.3 = bf16[64,4096]{1,0:T(8,128)(2,1)S(1)} collective-permute-done((bf16[64,4096]{1,0:T(8,128)(2,1)S(1)}, bf16[64,4096]{1,0:T(8,128)(2,1)S(1)}, u32[]{:S(2)}, u32[]{:S(2)}) %collective-permute-start.3) | collective-permute-done | bytes 524320 | tf_op jit(solution)/shard_map/ppermute | solution.py:23
  37.2 0.8 collective-permute-done.4
  38.0 0.7 fusion.14
  38.7 0.7 fusion.13
  39.7 4.6 %collective-permute-start.5 = (f32[64,1024]{1,0:T(8,128)S(1)}, f32[64,1024]{1,0:T(8,128)S(1)}, u32[]{:S(2)}, u32[]{:S(2)}) collective-permute-start(f32[64,1024]{1,0:T(8,128)S(1)} %get-tuple-element.31), channel_id=1, source_target_pairs={{0,3},{1,0},{2,1},{3,2},{4,7},{5,4},{6,5},{7,6},{8,11},{9,8},{10,9... | collective-permute-start | bytes 786440 | tf_op jit(solution)/shard_map/ppermute | solution.py:23
  45.1 1.1 %dynamic-slice_bitcast_fusion.1 = (f32[128,1024]{1,0:T(8,128)}, f32[128,1024]{1,0:T(8,128)}) fusion(f32[4,128,1024]{2,1,0:T(8,128)S(1)} %pad_maximum_fusion, s32[]{:T(128)S(6)} %select_n.39, s32[]{:T(128)S(6)} %select_n.44), kind=kLoop, calls=%fused_computation.9 | loop fusion | bytes 2097160 | tf_op jit(solution)/shard_map/jit(dynamic_index_in_dim)/squeeze | solution.py:57
  46.1 1.5 %collective-permute-done.5 = f32[64,1024]{1,0:T(8,128)S(1)} collective-permute-done((f32[64,1024]{1,0:T(8,128)S(1)}, f32[64,1024]{1,0:T(8,128)S(1)}, u32[]{:S(2)}, u32[]{:S(2)}) %collective-permute-start.5) | collective-permute-done | bytes 262176 | tf_op jit(solution)/shard_map/ppermute | solution.py:23
  47.6 3.1 %collective-permute-done.7 = f32[64,1024]{1,0:T(8,128)S(1)} collective-permute-done((f32[64,1024]{1,0:T(8,128)S(1)}, f32[64,1024]{1,0:T(8,128)S(1)}, u32[]{:S(2)}, u32[]{:S(2)}) %collective-permute-start.7) | collective-permute-done | bytes 262176 | tf_op jit(solution)/shard_map/ppermute | solution.py:23
  50.8 0.9 fusion.3
  51.6 1.5 %collective-permute-start.6 = (f32[128,1024]{1,0:T(8,128)}, f32[128,1024]{1,0:T(8,128)S(1)}, u32[]{:S(2)}, u32[]{:S(2)}) collective-permute-start(f32[128,1024]{1,0:T(8,128)} %get-tuple-element.29), channel_id=1, source_target_pairs={{0,3},{1,0},{2,1},{3,2},{4,7},{5,4},{6,5},{7,6},{8,11},{9,8},{10,9... | collective-permute-start | bytes 1572872 | tf_op jit(solution)/shard_map/ppermute | solution.py:23
  53.5 8.1 %collective-permute-done.6 = f32[128,1024]{1,0:T(8,128)S(1)} collective-permute-done((f32[128,1024]{1,0:T(8,128)}, f32[128,1024]{1,0:T(8,128)S(1)}, u32[]{:S(2)}, u32[]{:S(2)}) %collective-permute-start.6) | collective-permute-done | bytes 524320 | tf_op jit(solution)/shard_map/ppermute | solution.py:23
  61.6 3.0 %collective-permute-done.8 = f32[128,1024]{1,0:T(8,128)S(1)} collective-permute-done((f32[128,1024]{1,0:T(8,128)}, f32[128,1024]{1,0:T(8,128)S(1)}, u32[]{:S(2)}, u32[]{:S(2)}) %collective-permute-start.8) | collective-permute-done | bytes 524320 | tf_op jit(solution)/shard_map/ppermute | solution.py:23
  65.1 24.1 %all_to_all.5 = bf16[16,16,512]{2,1,0:T(8,128)(2,1)S(1)} all-to-all(bf16[16,16,512]{2,1,0:T(8,128)(2,1)S(1)} %bitcast.54), channel_id=1, replica_groups=mesh['batch'=16,'wx'=4,'wy'=4] {'batch'}, dimensions={0} | all-to-all | bytes 524288 | tf_op jit(solution)/shard_map/all_to_all | solution.py:69
  (30 shorter events, 3.1 us)
Async XLA Ops:
  0.0 7.0 %copy-start.2 = (bf16[128,4096]{1,0:T(8,128)(2,1)S(1)}, bf16[128,4096]{1,0:T(8,128)(2,1)}, u32[]{:S(2)}) copy-start(bf16[128,4096]{1,0:T(8,128)(2,1)} %param.8) | copy-start | bytes 3145732
  0.0 24.8 %collective-permute-start.2 = (bf16[128,4096]{1,0:T(8,128)(2,1)}, bf16[128,4096]{1,0:T(8,128)(2,1)S(1)}, u32[]{:S(2)}, u32[]{:S(2)}) collective-permute-start(bf16[128,4096]{1,0:T(8,128)(2,1)} %param.8), channel_id=1, source_target_pairs={{0,4},{4,8},{8,12},{12,0},{1,5},{5,9},{9,13},{13,1},{2,6},{6,10},{... | collective-permute-start | bytes 3145736 | tf_op jit(solution)/shard_map/ppermute | solution.py:23
  2.1 24.2 %collective-permute-start.1 = (bf16[128,4096]{1,0:T(8,128)(2,1)}, bf16[128,4096]{1,0:T(8,128)(2,1)S(1)}, u32[]{:S(2)}, u32[]{:S(2)}) collective-permute-start(bf16[128,4096]{1,0:T(8,128)(2,1)} %param.8), channel_id=1, source_target_pairs={{0,12},{4,0},{8,4},{12,8},{1,13},{5,1},{9,5},{13,9},{2,14},{6,2},{... | collective-permute-start | bytes 3145736 | tf_op jit(solution)/shard_map/ppermute | solution.py:23
  3.6 3.7 %copy-start.1 = (bf16[4096,512]{1,0:T(8,128)(2,1)S(1)}, bf16[4096,512]{1,0:T(8,128)(2,1)}, u32[]{:S(2)}) copy-start(bf16[4096,512]{1,0:T(8,128)(2,1)} %param.10) | copy-start | bytes 12582916
  7.4 20.7 %copy-start = (bf16[4096,512]{1,0:T(8,128)(2,1)S(1)}, bf16[4096,512]{1,0:T(8,128)(2,1)}, u32[]{:S(2)}) copy-start(bf16[4096,512]{1,0:T(8,128)(2,1)} %param.11) | copy-start | bytes 12582916
  24.9 12.3 %collective-permute-start.3 = (bf16[64,4096]{1,0:T(8,128)(2,1)S(1)}, bf16[64,4096]{1,0:T(8,128)(2,1)S(1)}, u32[]{:S(2)}, u32[]{:S(2)}) collective-permute-start(bf16[64,4096]{1,0:T(8,128)(2,1)S(1)} %slice.64), channel_id=1, source_target_pairs={{0,4},{4,8},{8,12},{12,0},{1,5},{5,9},{9,13},{13,1},{2,6},{6,10},{... | collective-permute-start | bytes 1572872 | tf_op jit(solution)/shard_map/ppermute | solution.py:23
  26.3 11.6 %collective-permute-start.4 = (bf16[64,4096]{1,0:T(8,128)(2,1)S(1)}, bf16[64,4096]{1,0:T(8,128)(2,1)S(1)}, u32[]{:S(2)}, u32[]{:S(2)}) collective-permute-start(bf16[64,4096]{1,0:T(8,128)(2,1)S(1)} %slice.65), channel_id=1, source_target_pairs={{0,12},{4,0},{8,4},{12,8},{1,13},{5,1},{9,5},{13,9},{2,14},{6,2},{... | collective-permute-start | bytes 1572872 | tf_op jit(solution)/shard_map/ppermute | solution.py:23
  39.4 4.9 %copy-start.3 = (s32[128,1]{0,1:T(1,128)S(1)}, s32[128,1]{0,1:T(1,128)}, u32[]{:S(2)}) copy-start(s32[128,1]{0,1:T(1,128)} %param.9) | copy-start | bytes 1540
  39.7 7.9 %collective-permute-start.5 = (f32[64,1024]{1,0:T(8,128)S(1)}, f32[64,1024]{1,0:T(8,128)S(1)}, u32[]{:S(2)}, u32[]{:S(2)}) collective-permute-start(f32[64,1024]{1,0:T(8,128)S(1)} %get-tuple-element.31), channel_id=1, source_target_pairs={{0,3},{1,0},{2,1},{3,2},{4,7},{5,4},{6,5},{7,6},{8,11},{9,8},{10,9... | collective-permute-start | bytes 786440 | tf_op jit(solution)/shard_map/ppermute | solution.py:23
  44.3 6.4 %collective-permute-start.7 = (f32[64,1024]{1,0:T(8,128)S(1)}, f32[64,1024]{1,0:T(8,128)S(1)}, u32[]{:S(2)}, u32[]{:S(2)}) collective-permute-start(f32[64,1024]{1,0:T(8,128)S(1)} %get-tuple-element.32), channel_id=1, source_target_pairs={{0,1},{1,2},{2,3},{3,0},{4,5},{5,6},{6,7},{7,4},{8,9},{9,10},{10,1... | collective-permute-start | bytes 786440 | tf_op jit(solution)/shard_map/ppermute | solution.py:23
  44.3 8.8 %collective-permute-start = (s32[128,1]{0,1:T(1,128)S(1)}, s32[128,1]{0,1:T(1,128)S(1)}, u32[]{:S(2)}, u32[]{:S(2)}) collective-permute-start(s32[128,1]{0,1:T(1,128)S(1)} %copy-done.3), channel_id=1, source_target_pairs={{0,0},{1,4},{2,8},{3,12},{4,1},{5,5},{6,9},{7,13},{8,2},{9,6},{10,... | collective-permute-start | bytes 1544 | tf_op jit(solution)/shard_map/ppermute | solution.py:39
  51.6 10.0 %collective-permute-start.6 = (f32[128,1024]{1,0:T(8,128)}, f32[128,1024]{1,0:T(8,128)S(1)}, u32[]{:S(2)}, u32[]{:S(2)}) collective-permute-start(f32[128,1024]{1,0:T(8,128)} %get-tuple-element.29), channel_id=1, source_target_pairs={{0,3},{1,0},{2,1},{3,2},{4,7},{5,4},{6,5},{7,6},{8,11},{9,8},{10,9... | collective-permute-start | bytes 1572872 | tf_op jit(solution)/shard_map/ppermute | solution.py:23
  53.1 11.5 %collective-permute-start.8 = (f32[128,1024]{1,0:T(8,128)}, f32[128,1024]{1,0:T(8,128)S(1)}, u32[]{:S(2)}, u32[]{:S(2)}) collective-permute-start(f32[128,1024]{1,0:T(8,128)} %get-tuple-element.30), channel_id=1, source_target_pairs={{0,1},{1,2},{2,3},{3,0},{4,5},{5,6},{6,7},{7,4},{8,9},{9,10},{10,1... | collective-permute-start | bytes 1572872 | tf_op jit(solution)/shard_map/ppermute | solution.py:23

commit v9 on v8

--- a/solution.py
+++ b/solution.py
@@ -52,16 +52,20 @@
     part_right = partial(from_right)
     part_far = partial(jnp.concatenate([far_a, far_b], axis=0))
     parts = jnp.stack([part_own, part_right, part_far, part_left])
+    near = jnp.stack([part_own, part_right, part_own, part_left])
 
     def block(w):
         return lax.dynamic_index_in_dim(parts, (w - x) % nx, 0, keepdims=False)
 
-    far_part = block(y + 2)
-    via_right = shift(far_part[:half], "wy", ny, -1)
-    via_left = shift(far_part[half:], "wy", ny, 1)
+    opposite = lax.dynamic_index_in_dim(near, (y + 2 - x) % nx, 0, keepdims=False)
+    via_right = shift(opposite[:half], "wy", ny, -1)
+    via_left = shift(opposite[half:], "wy", ny, 1)
+    via_right = jnp.where((y + 1 - x) % ny == 0, jnp.zeros_like(via_right), via_right)
+    via_left = jnp.where((y - 1 - x) % ny == 0, jnp.zeros_like(via_left), via_left)
+    across = lax.ppermute(part_far, ("wx", "wy"), [(w * ny + w, w * ny + (w + 2) % ny) for w in range(nx)])
     to_left = block(y - 1).at[:half].add(via_right)
     to_right = block(y + 1).at[half:].add(via_left)
-    total = block(y) + shift(to_left, "wy", ny, -1) + shift(to_right, "wy", ny, 1)
+    total = block(y) + shift(to_left, "wy", ny, -1) + shift(to_right, "wy", ny, 1) + across
     gate_sum, up_sum = total[:, :hid], total[:, hid:]
     hidden = (jax.nn.silu(gate_sum) * up_sum).astype(jnp.bfloat16)
     placed = place_rows(hidden, group_of, slots, groups_total)

time: 90 us -> 92.3 us (1.026)
  starting transfers between devices: 13.5 us -> 20.3 us
  waiting for transfers between devices: 39 us -> 34.1 us
  other arithmetic: 1.67 us -> 3.19 us
  blocking collectives: 24.1 us -> 23 us
    ppermute x8, waiting for transfers between devices: 39 us -> 29.1 us  [shift(): lax.ppermute(value, axis, [(i, (i + step) % count) for i in range(count)])]
    ppermute x0 -> x1, starting transfers between devices: none -> 6.75 us  [per_device(): lax.ppermute(part_far, ('wx', 'wy'), [(w * ny + w, w * ny + (w + 2) % ny)...]
    ppermute x0 -> x1, waiting for transfers between devices: none -> 5.02 us  [per_device(): lax.ppermute(part_far, ('wx', 'wy'), [(w * ny + w, w * ny + (w + 2) % ny)...]
    add x1, other arithmetic: 0.09 us -> 1.34 us  [per_device(): block(y) + shift(to_left, 'wy', ny, -1) + shift(to_right, 'wy', ny, 1)]
    all_to_all x1, blocking collectives: 24.1 us -> 23 us  [per_device(): lax.all_to_all(placed, 'batch', split_axis=0, concat_axis=0, tiled=True)]
  transfers between devices with their start and end apart: 9 -> 10, of which waited for: 7 -> 6; matrix products, arithmetic and copies ran while one was open for 11% -> 13% of each run, Pallas kernels for 0% -> 0%
where the time goes in v9:
time: 92.3 us; the launch traced here: 92 us
  waiting for transfers between devices  34.1 us (37%)
  blocking collectives  23 us (25%)
  starting transfers between devices  20.3 us (22%)
  matrix products  9 us (10%)
  other arithmetic  3.19 us (3%)
  local copies, waits for them, and re-layouts  2.31 us (3%)
    ppermute x8, waiting for transfers between devices, shift(): lax.ppermute(value, axis, [(i, (i + step) % count) for i in range(count)])  29.1 us
    all_to_all x1, blocking collectives, per_device(): lax.all_to_all(placed, 'batch', split_axis=0, concat_axis=0, tiled=True)  23 us
    ppermute x8, starting transfers between devices, shift(): lax.ppermute(value, axis, [(i, (i + step) % count) for i in range(count)])  12.2 us
    ppermute x1, starting transfers between devices, per_device(): lax.ppermute(part_far, ('wx', 'wy'), [(w * ny + w, w * ny + (w + 2) % ny)...  6.75 us
    dot_general x4, matrix products, partial(): up = jnp.dot(rows, up_weight, preferred_element_type=jnp.float32)  5.62 us
    ppermute x1, waiting for transfers between devices, per_device(): lax.ppermute(part_far, ('wx', 'wy'), [(w * ny + w, w * ny + (w + 2) % ny)...  5.02 us
    dot_general x4, matrix products, partial(): gate = jnp.dot(rows, gate_weight, preferred_element_type=jnp.float32)  3.04 us
  transfers between devices with their start and end apart: 10, of which 6 were waited for; matrix products, arithmetic and copies ran while one was open for 13% of the time, Pallas kernels for 0%

profile of v9, /device:TPU:1, one launch (start us, length us, event | category | flops | bytes accessed | tf_op | source)
XLA Modules:
  0.0 92.0 jit_solution(1236871806946413104)
XLA Ops:
  0.0 2.1 %collective-permute-start.2 = (bf16[128,4096]{1,0:T(8,128)(2,1)}, bf16[128,4096]{1,0:T(8,128)(2,1)S(1)}, u32[]{:S(2)}, u32[]{:S(2)}) collective-permute-start(bf16[128,4096]{1,0:T(8,128)(2,1)} %param.8), channel_id=1, source_target_pairs={{0,4},{4,8},{8,12},{12,0},{1,5},{5,9},{9,13},{13,1},{2,6},{6,10},{... | collective-permute-start | bytes 3145736 | tf_op jit(solution)/shard_map/ppermute | solution.py:23
  2.1 1.5 %collective-permute-start.1 = (bf16[128,4096]{1,0:T(8,128)(2,1)}, bf16[128,4096]{1,0:T(8,128)(2,1)S(1)}, u32[]{:S(2)}, u32[]{:S(2)}) collective-permute-start(bf16[128,4096]{1,0:T(8,128)(2,1)} %param.8), channel_id=1, source_target_pairs={{0,12},{4,0},{8,4},{12,8},{1,13},{5,1},{9,5},{13,9},{2,14},{6,2},{... | collective-permute-start | bytes 3145736 | tf_op jit(solution)/shard_map/ppermute | solution.py:23
  3.6 1.3 %collective-permute-start = (s32[128,1]{0,1:T(1,128)}, s32[128,1]{0,1:T(1,128)S(1)}, u32[]{:S(2)}, u32[]{:S(2)}) collective-permute-start(s32[128,1]{0,1:T(1,128)} %param.9), channel_id=1, source_target_pairs={{0,0},{1,4},{2,8},{3,12},{4,1},{5,5},{6,9},{7,13},{8,2},{9,6},{10,... | collective-permute-start | bytes 1544 | tf_op jit(solution)/shard_map/ppermute | solution.py:39
  4.9 3.4 %fusion.16 = f32[128,512]{1,0:T(8,128)S(1)} fusion(bf16[128,4096]{1,0:T(8,128)(2,1)} %param.8, bf16[4096,512]{1,0:T(8,128)(2,1)} %param.11), kind=kOutput, calls=%fused_computation.40 | convolution fusion | flops 536870912 | bytes 5505024 | tf_op jit(solution)/shard_map/dot_general | solution.py:43
  8.7 0.8 fusion.15
  9.5 15.3 %collective-permute-done.2 = bf16[128,4096]{1,0:T(8,128)(2,1)S(1)} collective-permute-done((bf16[128,4096]{1,0:T(8,128)(2,1)}, bf16[128,4096]{1,0:T(8,128)(2,1)S(1)}, u32[]{:S(2)}, u32[]{:S(2)}) %collective-permute-start.2) | collective-permute-done | bytes 1048608 | tf_op jit(solution)/shard_map/ppermute | solution.py:23
  24.9 1.4 %collective-permute-start.3 = (bf16[64,4096]{1,0:T(8,128)(2,1)S(1)}, bf16[64,4096]{1,0:T(8,128)(2,1)S(1)}, u32[]{:S(2)}, u32[]{:S(2)}) collective-permute-start(bf16[64,4096]{1,0:T(8,128)(2,1)S(1)} %slice.64), channel_id=1, source_target_pairs={{0,4},{4,8},{8,12},{12,0},{1,5},{5,9},{9,13},{13,1},{2,6},{6,10},{... | collective-permute-start | bytes 1572872 | tf_op jit(solution)/shard_map/ppermute | solution.py:23
  26.3 1.7 %collective-permute-start.4 = (bf16[64,4096]{1,0:T(8,128)(2,1)S(1)}, bf16[64,4096]{1,0:T(8,128)(2,1)S(1)}, u32[]{:S(2)}, u32[]{:S(2)}) collective-permute-start(bf16[64,4096]{1,0:T(8,128)(2,1)S(1)} %slice.65), channel_id=1, source_target_pairs={{0,12},{4,0},{8,4},{12,8},{1,13},{5,1},{9,5},{13,9},{2,14},{6,2},{... | collective-permute-start | bytes 1572872 | tf_op jit(solution)/shard_map/ppermute | solution.py:23
  28.1 0.8 fusion.22
  28.9 0.8 fusion.21
  29.6 0.8 fusion.18
  30.4 0.8 fusion.17
  31.6 4.0 %collective-permute-start.5 = (f32[64,1024]{1,0:T(8,128)S(1)}, f32[64,1024]{1,0:T(8,128)S(1)}, u32[]{:S(2)}, u32[]{:S(2)}) collective-permute-start(f32[64,1024]{1,0:T(8,128)S(1)} %get-tuple-element.33), channel_id=1, source_target_pairs={{0,3},{1,0},{2,1},{3,2},{4,7},{5,4},{6,5},{7,6},{8,11},{9,8},{10,9... | collective-permute-start | bytes 786440 | tf_op jit(solution)/shard_map/ppermute | solution.py:23
  35.5 1.6 %collective-permute-done.3 = bf16[64,4096]{1,0:T(8,128)(2,1)S(1)} collective-permute-done((bf16[64,4096]{1,0:T(8,128)(2,1)S(1)}, bf16[64,4096]{1,0:T(8,128)(2,1)S(1)}, u32[]{:S(2)}, u32[]{:S(2)}) %collective-permute-start.3) | collective-permute-done | bytes 524320 | tf_op jit(solution)/shard_map/ppermute | solution.py:23
  37.2 0.8 collective-permute-done.4
  39.5 6.8 %collective-permute-start.9 = (f32[128,1024]{1,0:T(8,128)S(1)}, f32[128,1024]{1,0:T(8,128)S(1)}, u32[]{:S(2)}, u32[]{:S(2)}) collective-permute-start(f32[128,1024]{1,0:T(8,128)S(1)} %get-tuple-element.36), channel_id=1, source_target_pairs={{0,2},{5,7},{10,8},{15,13},{16,18},{21,23},{26,24},{31,29},{32,34}... | collective-permute-start | bytes 1572872 | tf_op jit(solution)/shard_map/ppermute | solution.py:65
  46.4 1.1 %dynamic-slice_bitcast_fusion.1 = (f32[128,1024]{1,0:T(8,128)}, f32[128,1024]{1,0:T(8,128)}) fusion(f32[4,128,1024]{2,1,0:T(8,128)S(1)} %pad_maximum_fusion, s32[]{:T(128)S(6)} %select_n.57, s32[]{:T(128)S(6)} %select_n.64), kind=kLoop, calls=%fused_computation.19 | loop fusion | bytes 2097160 | tf_op jit(solution)/shard_map/jit(dynamic_index_in_dim)/squeeze | solution.py:58
  47.5 0.9 fusion.8
  48.4 1.5 %collective-permute-start.8 = (f32[128,1024]{1,0:T(8,128)}, f32[128,1024]{1,0:T(8,128)}, u32[]{:S(2)}, u32[]{:S(2)}) collective-permute-start(f32[128,1024]{1,0:T(8,128)} %get-tuple-element.30), channel_id=1, source_target_pairs={{0,1},{1,2},{2,3},{3,0},{4,5},{5,6},{6,7},{7,4},{8,9},{9,10},{10,1... | collective-permute-start | bytes 1572872 | tf_op jit(solution)/shard_map/ppermute | solution.py:23
  50.3 5.0 %collective-permute-done.9 = f32[128,1024]{1,0:T(8,128)S(1)} collective-permute-done((f32[128,1024]{1,0:T(8,128)S(1)}, f32[128,1024]{1,0:T(8,128)S(1)}, u32[]{:S(2)}, u32[]{:S(2)}) %collective-permute-start.9) | collective-permute-done | bytes 524320 | tf_op jit(solution)/shard_map/ppermute | solution.py:65
  55.3 4.3 %collective-permute-done.6 = f32[128,1024]{1,0:T(8,128)} collective-permute-done((f32[128,1024]{1,0:T(8,128)}, f32[128,1024]{1,0:T(8,128)}, u32[]{:S(2)}, u32[]{:S(2)}) %collective-permute-start.6) | collective-permute-done | bytes 524320 | tf_op jit(solution)/shard_map/ppermute | solution.py:23
  59.6 7.0 %collective-permute-done.8 = f32[128,1024]{1,0:T(8,128)} collective-permute-done((f32[128,1024]{1,0:T(8,128)}, f32[128,1024]{1,0:T(8,128)}, u32[]{:S(2)}, u32[]{:S(2)}) %collective-permute-start.8) | collective-permute-done | bytes 524320 | tf_op jit(solution)/shard_map/ppermute | solution.py:23
  66.6 1.3 %fusion.5 = f32[128,1024]{1,0:T(8,128)S(1)} fusion(f32[128,1024]{1,0:T(8,128)S(1)} %collective-permute-done.9, f32[128,1024]{1,0:T(8,128)} %collective-permute-done.8, f32[128,1024]{1,0:T(8,128)} %collective-permute-done.6, f32[4,128,1024]{2,1,0:T(8,128)S(1)} %pad_maximum_fusion, s32[]{:T(128)S(6)} %select_n.55), kind=kLoop, calls=%fused_computation.17 | loop fusion | flops 393216 | bytes 2621444 | tf_op jit(solution)/shard_map/add | solution.py:68
  68.3 23.0 %all_to_all.5 = bf16[16,16,512]{2,1,0:T(8,128)(2,1)S(1)} all-to-all(bf16[16,16,512]{2,1,0:T(8,128)(2,1)S(1)} %bitcast.56), channel_id=1, replica_groups=mesh['batch'=16,'wx'=4,'wy'=4] {'batch'}, dimensions={0} | all-to-all | bytes 524288 | tf_op jit(solution)/shard_map/all_to_all | solution.py:73
  (31 shorter events, 4.0 us)
Async XLA Ops:
  0.0 8.3 %copy-start.2 = (bf16[128,4096]{1,0:T(8,128)(2,1)S(1)}, bf16[128,4096]{1,0:T(8,128)(2,1)}, u32[]{:S(2)}) copy-start(bf16[128,4096]{1,0:T(8,128)(2,1)} %param.8) | copy-start | bytes 3145732
  0.0 24.8 %collective-permute-start.2 = (bf16[128,4096]{1,0:T(8,128)(2,1)}, bf16[128,4096]{1,0:T(8,128)(2,1)S(1)}, u32[]{:S(2)}, u32[]{:S(2)}) collective-permute-start(bf16[128,4096]{1,0:T(8,128)(2,1)} %param.8), channel_id=1, source_target_pairs={{0,4},{4,8},{8,12},{12,0},{1,5},{5,9},{9,13},{13,1},{2,6},{6,10},{... | collective-permute-start | bytes 3145736 | tf_op jit(solution)/shard_map/ppermute | solution.py:23
  2.1 24.2 %collective-permute-start.1 = (bf16[128,4096]{1,0:T(8,128)(2,1)}, bf16[128,4096]{1,0:T(8,128)(2,1)S(1)}, u32[]{:S(2)}, u32[]{:S(2)}) collective-permute-start(bf16[128,4096]{1,0:T(8,128)(2,1)} %param.8), channel_id=1, source_target_pairs={{0,12},{4,0},{8,4},{12,8},{1,13},{5,1},{9,5},{13,9},{2,14},{6,2},{... | collective-permute-start | bytes 3145736 | tf_op jit(solution)/shard_map/ppermute | solution.py:23
  3.6 46.2 %collective-permute-start = (s32[128,1]{0,1:T(1,128)}, s32[128,1]{0,1:T(1,128)S(1)}, u32[]{:S(2)}, u32[]{:S(2)}) collective-permute-start(s32[128,1]{0,1:T(1,128)} %param.9), channel_id=1, source_target_pairs={{0,0},{1,4},{2,8},{3,12},{4,1},{5,5},{6,9},{7,13},{8,2},{9,6},{10,... | collective-permute-start | bytes 1544 | tf_op jit(solution)/shard_map/ppermute | solution.py:39
  4.9 3.7 %copy-start.1 = (bf16[4096,512]{1,0:T(8,128)(2,1)S(1)}, bf16[4096,512]{1,0:T(8,128)(2,1)}, u32[]{:S(2)}) copy-start(bf16[4096,512]{1,0:T(8,128)(2,1)} %param.10) | copy-start | bytes 12582916
  8.7 19.4 %copy-start = (bf16[4096,512]{1,0:T(8,128)(2,1)S(1)}, bf16[4096,512]{1,0:T(8,128)(2,1)}, u32[]{:S(2)}) copy-start(bf16[4096,512]{1,0:T(8,128)(2,1)} %param.11) | copy-start | bytes 12582916
  24.9 12.3 %collective-permute-start.3 = (bf16[64,4096]{1,0:T(8,128)(2,1)S(1)}, bf16[64,4096]{1,0:T(8,128)(2,1)S(1)}, u32[]{:S(2)}, u32[]{:S(2)}) collective-permute-start(bf16[64,4096]{1,0:T(8,128)(2,1)S(1)} %slice.64), channel_id=1, source_target_pairs={{0,4},{4,8},{8,12},{12,0},{1,5},{5,9},{9,13},{13,1},{2,6},{6,10},{... | collective-permute-start | bytes 1572872 | tf_op jit(solution)/shard_map/ppermute | solution.py:23
  26.3 11.6 %collective-permute-start.4 = (bf16[64,4096]{1,0:T(8,128)(2,1)S(1)}, bf16[64,4096]{1,0:T(8,128)(2,1)S(1)}, u32[]{:S(2)}, u32[]{:S(2)}) collective-permute-start(bf16[64,4096]{1,0:T(8,128)(2,1)S(1)} %slice.65), channel_id=1, source_target_pairs={{0,12},{4,0},{8,4},{12,8},{1,13},{5,1},{9,5},{13,9},{2,14},{6,2},{... | collective-permute-start | bytes 1572872 | tf_op jit(solution)/shard_map/ppermute | solution.py:23
  31.6 15.9 %collective-permute-start.5 = (f32[64,1024]{1,0:T(8,128)S(1)}, f32[64,1024]{1,0:T(8,128)S(1)}, u32[]{:S(2)}, u32[]{:S(2)}) collective-permute-start(f32[64,1024]{1,0:T(8,128)S(1)} %get-tuple-element.33), channel_id=1, source_target_pairs={{0,3},{1,0},{2,1},{3,2},{4,7},{5,4},{6,5},{7,6},{8,11},{9,8},{10,9... | collective-permute-start | bytes 786440 | tf_op jit(solution)/shard_map/ppermute | solution.py:23
  35.5 12.0 %collective-permute-start.7 = (f32[64,1024]{1,0:T(8,128)S(1)}, f32[64,1024]{1,0:T(8,128)S(1)}, u32[]{:S(2)}, u32[]{:S(2)}) collective-permute-start(f32[64,1024]{1,0:T(8,128)S(1)} %get-tuple-element.34), channel_id=1, source_target_pairs={{0,1},{1,2},{2,3},{3,0},{4,5},{5,6},{6,7},{7,4},{8,9},{9,10},{10,1... | collective-permute-start | bytes 786440 | tf_op jit(solution)/shard_map/ppermute | solution.py:23
  39.5 15.8 %collective-permute-start.9 = (f32[128,1024]{1,0:T(8,128)S(1)}, f32[128,1024]{1,0:T(8,128)S(1)}, u32[]{:S(2)}, u32[]{:S(2)}) collective-permute-start(f32[128,1024]{1,0:T(8,128)S(1)} %get-tuple-element.36), channel_id=1, source_target_pairs={{0,2},{5,7},{10,8},{15,13},{16,18},{21,23},{26,24},{31,29},{32,34}... | collective-permute-start | bytes 1572872 | tf_op jit(solution)/shard_map/ppermute | solution.py:65
  48.4 11.3 %collective-permute-start.6 = (f32[128,1024]{1,0:T(8,128)}, f32[128,1024]{1,0:T(8,128)}, u32[]{:S(2)}, u32[]{:S(2)}) collective-permute-start(f32[128,1024]{1,0:T(8,128)} %get-tuple-element.29), channel_id=1, source_target_pairs={{0,3},{1,0},{2,1},{3,2},{4,7},{5,4},{6,5},{7,6},{8,11},{9,8},{10,9... | collective-permute-start | bytes 1572872 | tf_op jit(solution)/shard_map/ppermute | solution.py:23
  48.4 18.3 %collective-permute-start.8 = (f32[128,1024]{1,0:T(8,128)}, f32[128,1024]{1,0:T(8,128)}, u32[]{:S(2)}, u32[]{:S(2)}) collective-permute-start(f32[128,1024]{1,0:T(8,128)} %get-tuple-element.30), channel_id=1, source_target_pairs={{0,1},{1,2},{2,3},{3,0},{4,5},{5,6},{6,7},{7,4},{8,9},{9,10},{10,1... | collective-permute-start | bytes 1572872 | tf_op jit(solution)/shard_map/ppermute | solution.py:23

commit v10 on v8

--- a/solution.py
+++ b/solution.py
@@ -59,8 +59,9 @@
     far_part = block(y + 2)
     via_right = shift(far_part[:half], "wy", ny, -1)
     via_left = shift(far_part[half:], "wy", ny, 1)
-    to_left = block(y - 1).at[:half].add(via_right)
-    to_right = block(y + 1).at[half:].add(via_left)
+    base_left, base_right = lax.optimization_barrier((block(y - 1), block(y + 1)))
+    to_left = base_left.at[:half].add(via_right)
+    to_right = base_right.at[half:].add(via_left)
     total = block(y) + shift(to_left, "wy", ny, -1) + shift(to_right, "wy", ny, 1)
     gate_sum, up_sum = total[:, :hid], total[:, hid:]
     hidden = (jax.nn.silu(gate_sum) * up_sum).astype(jnp.bfloat16)

time: 90 us -> 92.1 us (1.023)
  waiting for transfers between devices: 39 us -> 31.9 us
  starting transfers between devices: 13.5 us -> 20.2 us
  other arithmetic: 1.67 us -> 3.09 us
    ppermute x8, waiting for transfers between devices: 39 us -> 31.9 us  [shift(): lax.ppermute(value, axis, [(i, (i + step) % count) for i in range(count)])]
    ppermute x8, starting transfers between devices: 12.9 us -> 19.5 us  [shift(): lax.ppermute(value, axis, [(i, (i + step) % count) for i in range(count)])]
    add x1, other arithmetic: 0.09 us -> 1.29 us  [per_device(): block(y) + shift(to_left, 'wy', ny, -1) + shift(to_right, 'wy', ny, 1)]
    squeeze x1, local copies, waits for them, and re-layouts: 1.05 us -> 0.1 us  [block(): return lax.dynamic_index_in_dim(parts, (w - x) % nx, 0, keepdims=False)]
  transfers between devices with their start and end apart: 9 -> 9, of which waited for: 7 -> 6; matrix products, arithmetic and copies ran while one was open for 11% -> 10% of each run, Pallas kernels for 0% -> 0%
where the time goes in v10:
time: 92.1 us; the launch traced here: 91.5 us
  waiting for transfers between devices  31.9 us (35%)
  blocking collectives  25 us (27%)
  starting transfers between devices  20.2 us (22%)
  matrix products  9 us (10%)
  other arithmetic  3.09 us (3%)
  local copies, waits for them, and re-layouts  2.07 us (2%)
    ppermute x8, waiting for transfers between devices, shift(): lax.ppermute(value, axis, [(i, (i + step) % count) for i in range(count)])  31.9 us
    all_to_all x1, blocking collectives, per_device(): lax.all_to_all(placed, 'batch', split_axis=0, concat_axis=0, tiled=True)  25 us
    ppermute x8, starting transfers between devices, shift(): lax.ppermute(value, axis, [(i, (i + step) % count) for i in range(count)])  19.5 us
    dot_general x4, matrix products, partial(): up = jnp.dot(rows, up_weight, preferred_element_type=jnp.float32)  5.63 us
    dot_general x4, matrix products, partial(): gate = jnp.dot(rows, gate_weight, preferred_element_type=jnp.float32)  3.03 us
  transfers between devices with their start and end apart: 9, of which 6 were waited for; matrix products, arithmetic and copies ran while one was open for 10% of the time, Pallas kernels for 0%

profile of v10, /device:TPU:1, one launch (start us, length us, event | category | flops | bytes accessed | tf_op | source)
XLA Modules:
  0.0 91.5 jit_solution(336533867138275812)
XLA Ops:
  0.0 2.1 %collective-permute-start.2 = (bf16[128,4096]{1,0:T(8,128)(2,1)}, bf16[128,4096]{1,0:T(8,128)(2,1)S(1)}, u32[]{:S(2)}, u32[]{:S(2)}) collective-permute-start(bf16[128,4096]{1,0:T(8,128)(2,1)} %param.8), channel_id=1, source_target_pairs={{0,4},{4,8},{8,12},{12,0},{1,5},{5,9},{9,13},{13,1},{2,6},{6,10},{... | collective-permute-start | bytes 3145736 | tf_op jit(solution)/shard_map/ppermute | solution.py:23
  2.1 1.5 %collective-permute-start.1 = (bf16[128,4096]{1,0:T(8,128)(2,1)}, bf16[128,4096]{1,0:T(8,128)(2,1)S(1)}, u32[]{:S(2)}, u32[]{:S(2)}) collective-permute-start(bf16[128,4096]{1,0:T(8,128)(2,1)} %param.8), channel_id=1, source_target_pairs={{0,12},{4,0},{8,4},{12,8},{1,13},{5,1},{9,5},{13,9},{2,14},{6,2},{... | collective-permute-start | bytes 3145736 | tf_op jit(solution)/shard_map/ppermute | solution.py:23
  3.6 3.4 %fusion.8 = f32[128,512]{1,0:T(8,128)S(1)} fusion(bf16[128,4096]{1,0:T(8,128)(2,1)} %param.8, bf16[4096,512]{1,0:T(8,128)(2,1)} %param.11), kind=kOutput, calls=%fused_computation.27 | convolution fusion | flops 536870912 | bytes 5505024 | tf_op jit(solution)/shard_map/dot_general | solution.py:43
  7.4 0.8 fusion.7
  8.2 16.6 %collective-permute-done.2 = bf16[128,4096]{1,0:T(8,128)(2,1)S(1)} collective-permute-done((bf16[128,4096]{1,0:T(8,128)(2,1)}, bf16[128,4096]{1,0:T(8,128)(2,1)S(1)}, u32[]{:S(2)}, u32[]{:S(2)}) %collective-permute-start.2) | collective-permute-done | bytes 1048608 | tf_op jit(solution)/shard_map/ppermute | solution.py:23
  24.9 1.4 %collective-permute-start.3 = (bf16[64,4096]{1,0:T(8,128)(2,1)S(1)}, bf16[64,4096]{1,0:T(8,128)(2,1)S(1)}, u32[]{:S(2)}, u32[]{:S(2)}) collective-permute-start(bf16[64,4096]{1,0:T(8,128)(2,1)S(1)} %slice.72), channel_id=1, source_target_pairs={{0,4},{4,8},{8,12},{12,0},{1,5},{5,9},{9,13},{13,1},{2,6},{6,10},{... | collective-permute-start | bytes 1572872 | tf_op jit(solution)/shard_map/ppermute | solution.py:23
  26.3 1.7 %collective-permute-start.4 = (bf16[64,4096]{1,0:T(8,128)(2,1)S(1)}, bf16[64,4096]{1,0:T(8,128)(2,1)S(1)}, u32[]{:S(2)}, u32[]{:S(2)}) collective-permute-start(bf16[64,4096]{1,0:T(8,128)(2,1)S(1)} %slice.73), channel_id=1, source_target_pairs={{0,12},{4,0},{8,4},{12,8},{1,13},{5,1},{9,5},{13,9},{2,14},{6,2},{... | collective-permute-start | bytes 1572872 | tf_op jit(solution)/shard_map/ppermute | solution.py:23
  28.1 0.8 fusion.14
  28.9 0.8 fusion.13
  29.6 0.8 fusion.10
  30.5 0.8 fusion.9
  31.3 5.9 %collective-permute-done.3 = bf16[64,4096]{1,0:T(8,128)(2,1)S(1)} collective-permute-done((bf16[64,4096]{1,0:T(8,128)(2,1)S(1)}, bf16[64,4096]{1,0:T(8,128)(2,1)S(1)}, u32[]{:S(2)}, u32[]{:S(2)}) %collective-permute-start.3) | collective-permute-done | bytes 524320 | tf_op jit(solution)/shard_map/ppermute | solution.py:23
  37.2 0.8 collective-permute-done.4
  38.7 0.7 fusion.11
  39.7 0.8 dynamic-slice_bitcast_fusion.3
  40.4 3.3 %collective-permute-start.7 = (f32[64,1024]{1,0:T(8,128)}, f32[64,1024]{1,0:T(8,128)}, u32[]{:S(2)}, u32[]{:S(2)}) collective-permute-start(f32[64,1024]{1,0:T(8,128)} %get-tuple-element.34), channel_id=1, source_target_pairs={{0,1},{1,2},{2,3},{3,0},{4,5},{5,6},{6,7},{7,4},{8,9},{9,10},{10,1... | collective-permute-start | bytes 786440 | tf_op jit(solution)/shard_map/ppermute | solution.py:23
  44.4 6.2 %collective-permute-start.5 = (f32[64,1024]{1,0:T(8,128)S(1)}, f32[64,1024]{1,0:T(8,128)S(1)}, u32[]{:S(2)}, u32[]{:S(2)}) collective-permute-start(f32[64,1024]{1,0:T(8,128)S(1)} %get-tuple-element.33), channel_id=1, source_target_pairs={{0,3},{1,0},{2,1},{3,2},{4,7},{5,4},{6,5},{7,6},{8,11},{9,8},{10,9... | collective-permute-start | bytes 786440 | tf_op jit(solution)/shard_map/ppermute | solution.py:23
  50.7 1.0 %add_dynamic-update-slice_fusion = f32[128,1024]{1,0:T(8,128)S(1)} fusion(f32[128,1024]{1,0:T(8,128)S(1)} %get-tuple-element.32, f32[64,1024]{1,0:T(8,128)} %collective-permute-done.7), kind=kLoop, calls=%fused_computation.14 | loop fusion | flops 65536 | bytes 786432 | tf_op jit(solution)/shard_map/scatter-add | solution.py:64
  51.8 2.1 %collective-permute-done.5 = f32[64,1024]{1,0:T(8,128)S(1)} collective-permute-done((f32[64,1024]{1,0:T(8,128)S(1)}, f32[64,1024]{1,0:T(8,128)S(1)}, u32[]{:S(2)}, u32[]{:S(2)}) %collective-permute-start.5) | collective-permute-done | bytes 262176 | tf_op jit(solution)/shard_map/ppermute | solution.py:23
  54.0 3.2 %collective-permute-start.6 = (f32[128,1024]{1,0:T(8,128)S(1)}, f32[128,1024]{1,0:T(8,128)}, u32[]{:S(2)}, u32[]{:S(2)}) collective-permute-start(f32[128,1024]{1,0:T(8,128)S(1)} %add_dynamic-update-slice_fusion.1), channel_id=1, source_target_pairs={{0,3},{1,0},{2,1},{3,2},{4,7},{5,4},{6,5},{7,6},{8,11},{9,8},{10,9... | collective-permute-start | bytes 1572872 | tf_op jit(solution)/shard_map/ppermute | solution.py:23
  57.6 5.6 %collective-permute-done.8 = f32[128,1024]{1,0:T(8,128)} collective-permute-done((f32[128,1024]{1,0:T(8,128)S(1)}, f32[128,1024]{1,0:T(8,128)}, u32[]{:S(2)}, u32[]{:S(2)}) %collective-permute-start.8) | collective-permute-done | bytes 524320 | tf_op jit(solution)/shard_map/ppermute | solution.py:23
  63.2 1.0 %collective-permute-done.6 = f32[128,1024]{1,0:T(8,128)} collective-permute-done((f32[128,1024]{1,0:T(8,128)S(1)}, f32[128,1024]{1,0:T(8,128)}, u32[]{:S(2)}, u32[]{:S(2)}) %collective-permute-start.6) | collective-permute-done | bytes 524320 | tf_op jit(solution)/shard_map/ppermute | solution.py:23
  64.2 1.3 %fusion = f32[128,1024]{1,0:T(8,128)S(1)} fusion(f32[128,1024]{1,0:T(8,128)} %collective-permute-done.8, f32[128,1024]{1,0:T(8,128)} %collective-permute-done.6, f32[4,128,1024]{2,1,0:T(8,128)S(1)} %pad_maximum_fusion, s32[]{:T(128)S(6)} %select_n.33), kind=kLoop, calls=%fused_computation.7 | loop fusion | flops 262144 | bytes 2097156 | tf_op jit(solution)/shard_map/add | solution.py:65
  65.8 25.0 %all_to_all.5 = bf16[16,16,512]{2,1,0:T(8,128)(2,1)S(1)} all-to-all(bf16[16,16,512]{2,1,0:T(8,128)(2,1)S(1)} %bitcast.46), channel_id=1, replica_groups=mesh['batch'=16,'wx'=4,'wy'=4] {'batch'}, dimensions={0} | all-to-all | bytes 524288 | tf_op jit(solution)/shard_map/all_to_all | solution.py:70
  (31 shorter events, 3.9 us)
Async XLA Ops:
  0.0 7.0 %copy-start.2 = (bf16[128,4096]{1,0:T(8,128)(2,1)S(1)}, bf16[128,4096]{1,0:T(8,128)(2,1)}, u32[]{:S(2)}) copy-start(bf16[128,4096]{1,0:T(8,128)(2,1)} %param.8) | copy-start | bytes 3145732
  0.0 24.8 %collective-permute-start.2 = (bf16[128,4096]{1,0:T(8,128)(2,1)}, bf16[128,4096]{1,0:T(8,128)(2,1)S(1)}, u32[]{:S(2)}, u32[]{:S(2)}) collective-permute-start(bf16[128,4096]{1,0:T(8,128)(2,1)} %param.8), channel_id=1, source_target_pairs={{0,4},{4,8},{8,12},{12,0},{1,5},{5,9},{9,13},{13,1},{2,6},{6,10},{... | collective-permute-start | bytes 3145736 | tf_op jit(solution)/shard_map/ppermute | solution.py:23
  2.1 24.2 %collective-permute-start.1 = (bf16[128,4096]{1,0:T(8,128)(2,1)}, bf16[128,4096]{1,0:T(8,128)(2,1)S(1)}, u32[]{:S(2)}, u32[]{:S(2)}) collective-permute-start(bf16[128,4096]{1,0:T(8,128)(2,1)} %param.8), channel_id=1, source_target_pairs={{0,12},{4,0},{8,4},{12,8},{1,13},{5,1},{9,5},{13,9},{2,14},{6,2},{... | collective-permute-start | bytes 3145736 | tf_op jit(solution)/shard_map/ppermute | solution.py:23
  3.6 3.7 %copy-start.1 = (bf16[4096,512]{1,0:T(8,128)(2,1)S(1)}, bf16[4096,512]{1,0:T(8,128)(2,1)}, u32[]{:S(2)}) copy-start(bf16[4096,512]{1,0:T(8,128)(2,1)} %param.10) | copy-start | bytes 12582916
  7.4 20.7 %copy-start = (bf16[4096,512]{1,0:T(8,128)(2,1)S(1)}, bf16[4096,512]{1,0:T(8,128)(2,1)}, u32[]{:S(2)}) copy-start(bf16[4096,512]{1,0:T(8,128)(2,1)} %param.11) | copy-start | bytes 12582916
  24.9 12.3 %collective-permute-start.3 = (bf16[64,4096]{1,0:T(8,128)(2,1)S(1)}, bf16[64,4096]{1,0:T(8,128)(2,1)S(1)}, u32[]{:S(2)}, u32[]{:S(2)}) collective-permute-start(bf16[64,4096]{1,0:T(8,128)(2,1)S(1)} %slice.72), channel_id=1, source_target_pairs={{0,4},{4,8},{8,12},{12,0},{1,5},{5,9},{9,13},{13,1},{2,6},{6,10},{... | collective-permute-start | bytes 1572872 | tf_op jit(solution)/shard_map/ppermute | solution.py:23
  26.3 11.6 %collective-permute-start.4 = (bf16[64,4096]{1,0:T(8,128)(2,1)S(1)}, bf16[64,4096]{1,0:T(8,128)(2,1)S(1)}, u32[]{:S(2)}, u32[]{:S(2)}) collective-permute-start(bf16[64,4096]{1,0:T(8,128)(2,1)S(1)} %slice.73), channel_id=1, source_target_pairs={{0,12},{4,0},{8,4},{12,8},{1,13},{5,1},{9,5},{13,9},{2,14},{6,2},{... | collective-permute-start | bytes 1572872 | tf_op jit(solution)/shard_map/ppermute | solution.py:23
  39.4 4.2 %copy-start.3 = (s32[128,1]{0,1:T(1,128)S(1)}, s32[128,1]{0,1:T(1,128)}, u32[]{:S(2)}) copy-start(s32[128,1]{0,1:T(1,128)} %param.9) | copy-start | bytes 1540
  40.4 10.3 %collective-permute-start.7 = (f32[64,1024]{1,0:T(8,128)}, f32[64,1024]{1,0:T(8,128)}, u32[]{:S(2)}, u32[]{:S(2)}) collective-permute-start(f32[64,1024]{1,0:T(8,128)} %get-tuple-element.34), channel_id=1, source_target_pairs={{0,1},{1,2},{2,3},{3,0},{4,5},{5,6},{6,7},{7,4},{8,9},{9,10},{10,1... | collective-permute-start | bytes 786440 | tf_op jit(solution)/shard_map/ppermute | solution.py:23
  43.7 13.5 %collective-permute-start = (s32[128,1]{0,1:T(1,128)S(1)}, s32[128,1]{0,1:T(1,128)S(1)}, u32[]{:S(2)}, u32[]{:S(2)}) collective-permute-start(s32[128,1]{0,1:T(1,128)S(1)} %copy-done.3), channel_id=1, source_target_pairs={{0,0},{1,4},{2,8},{3,12},{4,1},{5,5},{6,9},{7,13},{8,2},{9,6},{10,... | collective-permute-start | bytes 1544 | tf_op jit(solution)/shard_map/ppermute | solution.py:39
  44.4 9.5 %collective-permute-start.5 = (f32[64,1024]{1,0:T(8,128)S(1)}, f32[64,1024]{1,0:T(8,128)S(1)}, u32[]{:S(2)}, u32[]{:S(2)}) collective-permute-start(f32[64,1024]{1,0:T(8,128)S(1)} %get-tuple-element.33), channel_id=1, source_target_pairs={{0,3},{1,0},{2,1},{3,2},{4,7},{5,4},{6,5},{7,6},{8,11},{9,8},{10,9... | collective-permute-start | bytes 786440 | tf_op jit(solution)/shard_map/ppermute | solution.py:23
  51.7 11.5 %collective-permute-start.8 = (f32[128,1024]{1,0:T(8,128)S(1)}, f32[128,1024]{1,0:T(8,128)}, u32[]{:S(2)}, u32[]{:S(2)}) collective-permute-start(f32[128,1024]{1,0:T(8,128)S(1)} %add_dynamic-update-slice_fusion), channel_id=1, source_target_pairs={{0,1},{1,2},{2,3},{3,0},{4,5},{5,6},{6,7},{7,4},{8,9},{9,10},{10,1... | collective-permute-start | bytes 1572872 | tf_op jit(solution)/shard_map/ppermute | solution.py:23
  54.0 10.2 %collective-permute-start.6 = (f32[128,1024]{1,0:T(8,128)S(1)}, f32[128,1024]{1,0:T(8,128)}, u32[]{:S(2)}, u32[]{:S(2)}) collective-permute-start(f32[128,1024]{1,0:T(8,128)S(1)} %add_dynamic-update-slice_fusion.1), channel_id=1, source_target_pairs={{0,3},{1,0},{2,1},{3,2},{4,7},{5,4},{6,5},{7,6},{8,11},{9,8},{10,9... | collective-permute-start | bytes 1572872 | tf_op jit(solution)/shard_map/ppermute | solution.py:23

commit v11 on v8

--- a/solution.py
+++ b/solution.py
@@ -43,11 +43,16 @@
         up = jnp.dot(rows, up_weight, preferred_element_type=jnp.float32)
         return jnp.concatenate([gate, up], axis=1)
 
-    from_left = shift(tokens, "wx", nx, 1)
-    from_right = shift(tokens, "wx", nx, -1)
+    left_a = shift(tokens[:half], "wx", nx, 1)
+    right_b = shift(tokens[half:], "wx", nx, -1)
     part_own = partial(tokens)
-    far_a = shift(from_left[:half], "wx", nx, 1)
-    far_b = shift(from_right[half:], "wx", nx, -1)
+    later, _ = lax.optimization_barrier((tokens, (left_a, right_b)))
+    far_a = shift(left_a, "wx", nx, 1)
+    far_b = shift(right_b, "wx", nx, -1)
+    left_b = shift(later[half:], "wx", nx, 1)
+    right_a = shift(later[:half], "wx", nx, -1)
+    from_left = jnp.concatenate([left_a, left_b], axis=0)
+    from_right = jnp.concatenate([right_a, right_b], axis=0)
     part_left = partial(from_left)
     part_right = partial(from_right)
     part_far = partial(jnp.concatenate([far_a, far_b], axis=0))

time: 90 us -> 93.5 us (1.039)
  waiting for transfers between devices: 39 us -> 35.2 us
  starting transfers between devices: 13.5 us -> 16.8 us
  matrix products: 9 us -> 10.8 us
  local copies, waits for them, and re-layouts: 2.32 us -> 3.47 us
    ppermute x8 -> x10, waiting for transfers between devices: 39 us -> 35.2 us  [shift(): lax.ppermute(value, axis, [(i, (i + step) % count) for i in range(count)])]
    ppermute x8 -> x10, starting transfers between devices: 12.9 us -> 16.2 us  [shift(): lax.ppermute(value, axis, [(i, (i + step) % count) for i in range(count)])]
    dot_general x4, matrix products: 3.03 us -> 5.37 us  [partial(): gate = jnp.dot(rows, gate_weight, preferred_element_type=jnp.float32)]
    slice x2, local copies, waits for them, and re-layouts: 0.07 us -> 1.42 us  [the longest x1 1.36 us: per_device(): right_b = shift(tokens[half:], 'wx', nx, -1)]
  transfers between devices with their start and end apart: 9 -> 11, of which waited for: 7 -> 7; matrix products, arithmetic and copies ran while one was open for 11% -> 12% of each run, Pallas kernels for 0% -> 0%
where the time goes in v11:
time: 93.5 us; the launch traced here: 93.3 us
  waiting for transfers between devices  35.2 us (38%)
  blocking collectives  24.9 us (27%)
  starting transfers between devices  16.8 us (18%)
  matrix products  10.8 us (12%)
  local copies, waits for them, and re-layouts  3.47 us (4%)
  other arithmetic  1.75 us (2%)
    ppermute x10, waiting for transfers between devices, shift(): lax.ppermute(value, axis, [(i, (i + step) % count) for i in range(count)])  35.2 us
    all_to_all x1, blocking collectives, per_device(): lax.all_to_all(placed, 'batch', split_axis=0, concat_axis=0, tiled=True)  24.9 us
    ppermute x10, starting transfers between devices, shift(): lax.ppermute(value, axis, [(i, (i + step) % count) for i in range(count)])  16.2 us
    dot_general x4, matrix products, partial(): gate = jnp.dot(rows, gate_weight, preferred_element_type=jnp.float32)  5.37 us
    dot_general x4, matrix products, partial(): up = jnp.dot(rows, up_weight, preferred_element_type=jnp.float32)  5.05 us
  transfers between devices with their start and end apart: 11, of which 7 were waited for; matrix products, arithmetic and copies ran while one was open for 12% of the time, Pallas kernels for 0%

profile of v11, /device:TPU:1, one launch (start us, length us, event | category | flops | bytes accessed | tf_op | source)
XLA Modules:
  0.0 93.3 jit_solution(12188426597597001453)
XLA Ops:
  0.0 1.4 %fusion.10 = (bf16[64,4096]{1,0:T(8,128)(2,1)S(1)}, bf16[64,4096]{1,0:T(8,128)(2,1)S(1)}) fusion(bf16[128,4096]{1,0:T(8,128)(2,1)} %param.8), kind=kLoop, calls=%fused_computation.33 | loop fusion | bytes 2097152 | tf_op jit(solution)/shard_map/slice | solution.py:47
  1.4 2.2 %collective-permute-start.1 = (bf16[64,4096]{1,0:T(8,128)(2,1)S(1)}, bf16[64,4096]{1,0:T(8,128)(2,1)S(1)}, u32[]{:S(2)}, u32[]{:S(2)}) collective-permute-start(bf16[64,4096]{1,0:T(8,128)(2,1)S(1)} %get-tuple-element.40), channel_id=1, source_target_pairs={{0,4},{4,8},{8,12},{12,0},{1,5},{5,9},{9,13},{13,1},{2,6},{6,10},{... | collective-permute-start | bytes 1572872 | tf_op jit(solution)/shard_map/ppermute | solution.py:23
  3.6 1.5 %collective-permute-start.2 = (bf16[64,4096]{1,0:T(8,128)(2,1)S(1)}, bf16[64,4096]{1,0:T(8,128)(2,1)S(1)}, u32[]{:S(2)}, u32[]{:S(2)}) collective-permute-start(bf16[64,4096]{1,0:T(8,128)(2,1)S(1)} %get-tuple-element.39), channel_id=1, source_target_pairs={{0,12},{4,0},{8,4},{12,8},{1,13},{5,1},{9,5},{13,9},{2,14},{6,2},{... | collective-permute-start | bytes 1572872 | tf_op jit(solution)/shard_map/ppermute | solution.py:23
  5.1 3.2 %fusion.11 = f32[128,512]{1,0:T(8,128)S(1)} fusion(bf16[128,4096]{1,0:T(8,128)(2,1)} %param.8, bf16[4096,512]{1,0:T(8,128)(2,1)} %param.10), kind=kOutput, calls=%fused_computation.34 | convolution fusion | flops 536870912 | bytes 5505024 | tf_op jit(solution)/shard_map/dot_general | solution.py:42
  8.4 2.9 %fusion.12 = f32[128,512]{1,0:T(8,128)S(1)} fusion(bf16[128,4096]{1,0:T(8,128)(2,1)S(1)} %copy-done.2, bf16[4096,512]{1,0:T(8,128)(2,1)} %param.11), kind=kOutput, calls=%fused_computation.35 | convolution fusion | flops 536870912 | bytes 5505024 | tf_op jit(solution)/shard_map/dot_general | solution.py:43
  11.3 3.4 %collective-permute-done.1 = bf16[64,4096]{1,0:T(8,128)(2,1)S(1)} collective-permute-done((bf16[64,4096]{1,0:T(8,128)(2,1)S(1)}, bf16[64,4096]{1,0:T(8,128)(2,1)S(1)}, u32[]{:S(2)}, u32[]{:S(2)}) %collective-permute-start.1) | collective-permute-done | bytes 524320 | tf_op jit(solution)/shard_map/ppermute | solution.py:23
  14.7 1.2 %collective-permute-done.2 = bf16[64,4096]{1,0:T(8,128)(2,1)S(1)} collective-permute-done((bf16[64,4096]{1,0:T(8,128)(2,1)S(1)}, bf16[64,4096]{1,0:T(8,128)(2,1)S(1)}, u32[]{:S(2)}, u32[]{:S(2)}) %collective-permute-start.2) | collective-permute-done | bytes 524320 | tf_op jit(solution)/shard_map/ppermute | solution.py:23
  15.9 2.0 %collective-permute-start.3 = (bf16[64,4096]{1,0:T(8,128)(2,1)S(1)}, bf16[64,4096]{1,0:T(8,128)(2,1)S(1)}, u32[]{:S(2)}, u32[]{:S(2)}) collective-permute-start(bf16[64,4096]{1,0:T(8,128)(2,1)S(1)} %get-tuple-element.37), channel_id=1, source_target_pairs={{0,12},{4,0},{8,4},{12,8},{1,13},{5,1},{9,5},{13,9},{2,14},{6,2},{... | collective-permute-start | bytes 1572872 | tf_op jit(solution)/shard_map/ppermute | solution.py:23
  18.1 1.0 %collective-permute-start.4 = (bf16[64,4096]{1,0:T(8,128)(2,1)S(1)}, bf16[64,4096]{1,0:T(8,128)(2,1)S(1)}, u32[]{:S(2)}, u32[]{:S(2)}) collective-permute-start(bf16[64,4096]{1,0:T(8,128)(2,1)S(1)} %collective-permute-done.1), channel_id=1, source_target_pairs={{0,4},{4,8},{8,12},{12,0},{1,5},{5,9},{9,13},{13,1},{2,6},{6,10},{... | collective-permute-start | bytes 1572872 | tf_op jit(solution)/shard_map/ppermute | solution.py:23
  19.1 1.7 %collective-permute-start.5 = (bf16[64,4096]{1,0:T(8,128)(2,1)S(1)}, bf16[64,4096]{1,0:T(8,128)(2,1)S(1)}, u32[]{:S(2)}, u32[]{:S(2)}) collective-permute-start(bf16[64,4096]{1,0:T(8,128)(2,1)S(1)} %collective-permute-done.2), channel_id=1, source_target_pairs={{0,12},{4,0},{8,4},{12,8},{1,13},{5,1},{9,5},{13,9},{2,14},{6,2},{... | collective-permute-start | bytes 1572872 | tf_op jit(solution)/shard_map/ppermute | solution.py:23
  20.9 6.7 %collective-permute-done.3 = bf16[64,4096]{1,0:T(8,128)(2,1)S(1)} collective-permute-done((bf16[64,4096]{1,0:T(8,128)(2,1)S(1)}, bf16[64,4096]{1,0:T(8,128)(2,1)S(1)}, u32[]{:S(2)}, u32[]{:S(2)}) %collective-permute-start.3) | collective-permute-done | bytes 524320 | tf_op jit(solution)/shard_map/ppermute | solution.py:23
  27.7 0.7 fusion.13
  28.4 0.7 fusion.14
  29.1 11.8 %collective-permute-done.4 = bf16[64,4096]{1,0:T(8,128)(2,1)S(1)} collective-permute-done((bf16[64,4096]{1,0:T(8,128)(2,1)S(1)}, bf16[64,4096]{1,0:T(8,128)(2,1)S(1)}, u32[]{:S(2)}, u32[]{:S(2)}) %collective-permute-start.4) | collective-permute-done | bytes 524320 | tf_op jit(solution)/shard_map/ppermute | solution.py:23
  41.7 0.7 fusion.16
  43.2 0.7 fusion.18
  44.4 4.9 %collective-permute-start.7 = (f32[64,1024]{1,0:T(8,128)S(1)}, f32[64,1024]{1,0:T(8,128)S(1)}, u32[]{:S(2)}, u32[]{:S(2)}) collective-permute-start(f32[64,1024]{1,0:T(8,128)S(1)} %get-tuple-element.33), channel_id=1, source_target_pairs={{0,3},{1,0},{2,1},{3,2},{4,7},{5,4},{6,5},{7,6},{8,11},{9,8},{10,9... | collective-permute-start | bytes 786440 | tf_op jit(solution)/shard_map/ppermute | solution.py:23
  50.0 1.1 %dynamic-slice_bitcast_fusion.1 = (f32[128,1024]{1,0:T(8,128)}, f32[128,1024]{1,0:T(8,128)}) fusion(f32[4,128,1024]{2,1,0:T(8,128)S(1)} %pad_maximum_fusion, s32[]{:T(128)S(6)} %select_n.39, s32[]{:T(128)S(6)} %select_n.44), kind=kLoop, calls=%fused_computation.9 | loop fusion | bytes 2097160 | tf_op jit(solution)/shard_map/jit(dynamic_index_in_dim)/squeeze | solution.py:62
  51.1 1.5 %collective-permute-done.7 = f32[64,1024]{1,0:T(8,128)S(1)} collective-permute-done((f32[64,1024]{1,0:T(8,128)S(1)}, f32[64,1024]{1,0:T(8,128)S(1)}, u32[]{:S(2)}, u32[]{:S(2)}) %collective-permute-start.7) | collective-permute-done | bytes 262176 | tf_op jit(solution)/shard_map/ppermute | solution.py:23
  52.6 3.1 %collective-permute-done.9 = f32[64,1024]{1,0:T(8,128)S(1)} collective-permute-done((f32[64,1024]{1,0:T(8,128)S(1)}, f32[64,1024]{1,0:T(8,128)S(1)}, u32[]{:S(2)}, u32[]{:S(2)}) %collective-permute-start.9) | collective-permute-done | bytes 262176 | tf_op jit(solution)/shard_map/ppermute | solution.py:23
  55.7 0.9 fusion.3
  56.6 2.7 %collective-permute-start.8 = (f32[128,1024]{1,0:T(8,128)}, f32[128,1024]{1,0:T(8,128)S(1)}, u32[]{:S(2)}, u32[]{:S(2)}) collective-permute-start(f32[128,1024]{1,0:T(8,128)} %get-tuple-element.31), channel_id=1, source_target_pairs={{0,3},{1,0},{2,1},{3,2},{4,7},{5,4},{6,5},{7,6},{8,11},{9,8},{10,9... | collective-permute-start | bytes 1572872 | tf_op jit(solution)/shard_map/ppermute | solution.py:23
  59.7 7.5 %collective-permute-done.10 = f32[128,1024]{1,0:T(8,128)S(1)} collective-permute-done((f32[128,1024]{1,0:T(8,128)}, f32[128,1024]{1,0:T(8,128)S(1)}, u32[]{:S(2)}, u32[]{:S(2)}) %collective-permute-start.10) | collective-permute-done | bytes 524320 | tf_op jit(solution)/shard_map/ppermute | solution.py:23
  67.7 24.9 %all_to_all.5 = bf16[16,16,512]{2,1,0:T(8,128)(2,1)S(1)} all-to-all(bf16[16,16,512]{2,1,0:T(8,128)(2,1)S(1)} %bitcast.54), channel_id=1, replica_groups=mesh['batch'=16,'wx'=4,'wy'=4] {'batch'}, dimensions={0} | all-to-all | bytes 524288 | tf_op jit(solution)/shard_map/all_to_all | solution.py:74
  (37 shorter events, 4.5 us)
Async XLA Ops:
  0.0 8.3 %copy-start.2 = (bf16[128,4096]{1,0:T(8,128)(2,1)S(1)}, bf16[128,4096]{1,0:T(8,128)(2,1)}, u32[]{:S(2)}) copy-start(bf16[128,4096]{1,0:T(8,128)(2,1)} %param.8) | copy-start | bytes 3145732
  1.4 13.3 %collective-permute-start.1 = (bf16[64,4096]{1,0:T(8,128)(2,1)S(1)}, bf16[64,4096]{1,0:T(8,128)(2,1)S(1)}, u32[]{:S(2)}, u32[]{:S(2)}) collective-permute-start(bf16[64,4096]{1,0:T(8,128)(2,1)S(1)} %get-tuple-element.40), channel_id=1, source_target_pairs={{0,4},{4,8},{8,12},{12,0},{1,5},{5,9},{9,13},{13,1},{2,6},{6,10},{... | collective-permute-start | bytes 1572872 | tf_op jit(solution)/shard_map/ppermute | solution.py:23
  3.6 12.3 %collective-permute-start.2 = (bf16[64,4096]{1,0:T(8,128)(2,1)S(1)}, bf16[64,4096]{1,0:T(8,128)(2,1)S(1)}, u32[]{:S(2)}, u32[]{:S(2)}) collective-permute-start(bf16[64,4096]{1,0:T(8,128)(2,1)S(1)} %get-tuple-element.39), channel_id=1, source_target_pairs={{0,12},{4,0},{8,4},{12,8},{1,13},{5,1},{9,5},{13,9},{2,14},{6,2},{... | collective-permute-start | bytes 1572872 | tf_op jit(solution)/shard_map/ppermute | solution.py:23
  11.3 16.4 %copy-start = (bf16[4096,512]{1,0:T(8,128)(2,1)S(1)}, bf16[4096,512]{1,0:T(8,128)(2,1)}, u32[]{:S(2)}) copy-start(bf16[4096,512]{1,0:T(8,128)(2,1)} %param.10) | copy-start | bytes 12582916
  15.9 11.6 %collective-permute-start.3 = (bf16[64,4096]{1,0:T(8,128)(2,1)S(1)}, bf16[64,4096]{1,0:T(8,128)(2,1)S(1)}, u32[]{:S(2)}, u32[]{:S(2)}) collective-permute-start(bf16[64,4096]{1,0:T(8,128)(2,1)S(1)} %get-tuple-element.37), channel_id=1, source_target_pairs={{0,12},{4,0},{8,4},{12,8},{1,13},{5,1},{9,5},{13,9},{2,14},{6,2},{... | collective-permute-start | bytes 1572872 | tf_op jit(solution)/shard_map/ppermute | solution.py:23
  18.0 10.4 %copy-start.1 = (bf16[4096,512]{1,0:T(8,128)(2,1)S(1)}, bf16[4096,512]{1,0:T(8,128)(2,1)}, u32[]{:S(2)}) copy-start(bf16[4096,512]{1,0:T(8,128)(2,1)} %param.11) | copy-start | bytes 12582916
  18.0 24.4 %collective-permute-start.6 = (bf16[64,4096]{1,0:T(8,128)(2,1)S(1)}, bf16[64,4096]{1,0:T(8,128)(2,1)S(1)}, u32[]{:S(2)}, u32[]{:S(2)}) collective-permute-start(bf16[64,4096]{1,0:T(8,128)(2,1)S(1)} %get-tuple-element.38), channel_id=1, source_target_pairs={{0,4},{4,8},{8,12},{12,0},{1,5},{5,9},{9,13},{13,1},{2,6},{6,10},{... | collective-permute-start | bytes 1572872 | tf_op jit(solution)/shard_map/ppermute | solution.py:23
  18.1 22.8 %collective-permute-start.4 = (bf16[64,4096]{1,0:T(8,128)(2,1)S(1)}, bf16[64,4096]{1,0:T(8,128)(2,1)S(1)}, u32[]{:S(2)}, u32[]{:S(2)}) collective-permute-start(bf16[64,4096]{1,0:T(8,128)(2,1)S(1)} %collective-permute-done.1), channel_id=1, source_target_pairs={{0,4},{4,8},{8,12},{12,0},{1,5},{5,9},{9,13},{13,1},{2,6},{6,10},{... | collective-permute-start | bytes 1572872 | tf_op jit(solution)/shard_map/ppermute | solution.py:23
  19.1 21.8 %collective-permute-start.5 = (bf16[64,4096]{1,0:T(8,128)(2,1)S(1)}, bf16[64,4096]{1,0:T(8,128)(2,1)S(1)}, u32[]{:S(2)}, u32[]{:S(2)}) collective-permute-start(bf16[64,4096]{1,0:T(8,128)(2,1)S(1)} %collective-permute-done.2), channel_id=1, source_target_pairs={{0,12},{4,0},{8,4},{12,8},{1,13},{5,1},{9,5},{13,9},{2,14},{6,2},{... | collective-permute-start | bytes 1572872 | tf_op jit(solution)/shard_map/ppermute | solution.py:23
  43.9 5.3 %copy-start.3 = (s32[128,1]{0,1:T(1,128)S(1)}, s32[128,1]{0,1:T(1,128)}, u32[]{:S(2)}) copy-start(s32[128,1]{0,1:T(1,128)} %param.9) | copy-start | bytes 1540
  44.4 8.2 %collective-permute-start.7 = (f32[64,1024]{1,0:T(8,128)S(1)}, f32[64,1024]{1,0:T(8,128)S(1)}, u32[]{:S(2)}, u32[]{:S(2)}) collective-permute-start(f32[64,1024]{1,0:T(8,128)S(1)} %get-tuple-element.33), channel_id=1, source_target_pairs={{0,3},{1,0},{2,1},{3,2},{4,7},{5,4},{6,5},{7,6},{8,11},{9,8},{10,9... | collective-permute-start | bytes 786440 | tf_op jit(solution)/shard_map/ppermute | solution.py:23
  49.3 6.4 %collective-permute-start.9 = (f32[64,1024]{1,0:T(8,128)S(1)}, f32[64,1024]{1,0:T(8,128)S(1)}, u32[]{:S(2)}, u32[]{:S(2)}) collective-permute-start(f32[64,1024]{1,0:T(8,128)S(1)} %get-tuple-element.34), channel_id=1, source_target_pairs={{0,1},{1,2},{2,3},{3,0},{4,5},{5,6},{6,7},{7,4},{8,9},{9,10},{10,1... | collective-permute-start | bytes 786440 | tf_op jit(solution)/shard_map/ppermute | solution.py:23
  49.3 10.0 %collective-permute-start = (s32[128,1]{0,1:T(1,128)S(1)}, s32[128,1]{0,1:T(1,128)S(1)}, u32[]{:S(2)}, u32[]{:S(2)}) collective-permute-start(s32[128,1]{0,1:T(1,128)S(1)} %copy-done.3), channel_id=1, source_target_pairs={{0,0},{1,4},{2,8},{3,12},{4,1},{5,5},{6,9},{7,13},{8,2},{9,6},{10,... | collective-permute-start | bytes 1544 | tf_op jit(solution)/shard_map/ppermute | solution.py:39
  56.6 10.7 %collective-permute-start.10 = (f32[128,1024]{1,0:T(8,128)}, f32[128,1024]{1,0:T(8,128)S(1)}, u32[]{:S(2)}, u32[]{:S(2)}) collective-permute-start(f32[128,1024]{1,0:T(8,128)} %get-tuple-element.32), channel_id=1, source_target_pairs={{0,1},{1,2},{2,3},{3,0},{4,5},{5,6},{6,7},{7,4},{8,9},{9,10},{10,1... | collective-permute-start | bytes 1572872 | tf_op jit(solution)/shard_map/ppermute | solution.py:23
  56.6 10.7 %collective-permute-start.8 = (f32[128,1024]{1,0:T(8,128)}, f32[128,1024]{1,0:T(8,128)S(1)}, u32[]{:S(2)}, u32[]{:S(2)}) collective-permute-start(f32[128,1024]{1,0:T(8,128)} %get-tuple-element.31), channel_id=1, source_target_pairs={{0,3},{1,0},{2,1},{3,2},{4,7},{5,4},{6,5},{7,6},{8,11},{9,8},{10,9... | collective-permute-start | bytes 1572872 | tf_op jit(solution)/shard_map/ppermute | solution.py:23

commit v12 on v8

--- a/solution.py
+++ b/solution.py
@@ -38,10 +38,10 @@
     pairs = [(w * ny + v, v * ny + w) for w in range(nx) for v in range(ny)]
     group_of = lax.ppermute(routes, ("wx", "wy"), pairs)[:, 0]
 
+    both = jnp.concatenate([gate_weight, up_weight], axis=1)
+
     def partial(rows):
-        gate = jnp.dot(rows, gate_weight, preferred_element_type=jnp.float32)
-        up = jnp.dot(rows, up_weight, preferred_element_type=jnp.float32)
-        return jnp.concatenate([gate, up], axis=1)
+        return jnp.dot(rows, both, preferred_element_type=jnp.float32)
 
     from_left = shift(tokens, "wx", nx, 1)
     from_right = shift(tokens, "wx", nx, -1)

time: 90 us -> 89.5 us (level)
  waiting for transfers between devices: 39 us -> 30 us
  local copies, waits for them, and re-layouts: 2.32 us -> 11.1 us
    ppermute x8, waiting for transfers between devices: 39 us -> 30 us  [shift(): lax.ppermute(value, axis, [(i, (i + step) % count) for i in range(count)])]
    concatenate x1, local copies, waits for them, and re-layouts: 0.03 us -> 4.6 us  [per_device(): both = jnp.concatenate([gate_weight, up_weight], axis=1)]
    unnamed x10 -> x8, local copies, waits for them, and re-layouts: 1.11 us -> 5.28 us
    dot_general x8 -> x4, matrix products: 8.66 us -> 8.7 us  [partial(): return jnp.dot(rows, both, preferred_element_type=jnp.float32)]
  transfers between devices with their start and end apart: 9 -> 9, of which waited for: 7 -> 7; matrix products, arithmetic and copies ran while one was open for 11% -> 21% of each run, Pallas kernels for 0% -> 0%
where the time goes in v12:
time: 89.5 us; the launch traced here: 89.4 us
  waiting for transfers between devices  30 us (34%)
  blocking collectives  24.2 us (27%)
  starting transfers between devices  13.3 us (15%)
  local copies, waits for them, and re-layouts  11.1 us (12%)
  matrix products  9.03 us (10%)
  other arithmetic  1.5 us (2%)
    ppermute x8, waiting for transfers between devices, shift(): lax.ppermute(value, axis, [(i, (i + step) % count) for i in range(count)])  30 us
    all_to_all x1, blocking collectives, per_device(): lax.all_to_all(placed, 'batch', split_axis=0, concat_axis=0, tiled=True)  24.2 us
    ppermute x8, starting transfers between devices, shift(): lax.ppermute(value, axis, [(i, (i + step) % count) for i in range(count)])  12.7 us
    dot_general x4, matrix products, partial(): return jnp.dot(rows, both, preferred_element_type=jnp.float32)  8.7 us
    unnamed x8, local copies, waits for them, and re-layouts  5.28 us
    concatenate x1, local copies, waits for them, and re-layouts, per_device(): both = jnp.concatenate([gate_weight, up_weight], axis=1)  4.6 us
  transfers between devices with their start and end apart: 9, of which 7 were waited for; matrix products, arithmetic and copies ran while one was open for 21% of the time, Pallas kernels for 0%

profile of v12, /device:TPU:1, one launch (start us, length us, event | category | flops | bytes accessed | tf_op | source)
XLA Modules:
  0.0 89.4 jit_solution(14319717440085089282)
XLA Ops:
  0.0 2.1 %collective-permute-start.2 = (bf16[128,4096]{1,0:T(8,128)(2,1)}, bf16[128,4096]{1,0:T(8,128)(2,1)S(1)}, u32[]{:S(2)}, u32[]{:S(2)}) collective-permute-start(bf16[128,4096]{1,0:T(8,128)(2,1)} %param.8), channel_id=1, source_target_pairs={{0,4},{4,8},{8,12},{12,0},{1,5},{5,9},{9,13},{13,1},{2,6},{6,10},{... | collective-permute-start | bytes 3145736 | tf_op jit(solution)/shard_map/ppermute | solution.py:23
  2.1 1.4 %collective-permute-start.1 = (bf16[128,4096]{1,0:T(8,128)(2,1)}, bf16[128,4096]{1,0:T(8,128)(2,1)S(1)}, u32[]{:S(2)}, u32[]{:S(2)}) collective-permute-start(bf16[128,4096]{1,0:T(8,128)(2,1)} %param.8), channel_id=1, source_target_pairs={{0,12},{4,0},{8,4},{12,8},{1,13},{5,1},{9,5},{13,9},{2,14},{6,2},{... | collective-permute-start | bytes 3145736 | tf_op jit(solution)/shard_map/ppermute | solution.py:23
  3.6 4.6 %constant_dynamic-update-slice_fusion.1 = bf16[4096,1024]{1,0:T(8,128)(2,1)} fusion(bf16[4096,512]{1,0:T(8,128)(2,1)} %param.10), kind=kLoop, calls=%fused_computation.27 | loop fusion | bytes 8388608
  8.1 4.6 %constant_dynamic-update-slice_fusion = bf16[4096,1024]{1,0:T(8,128)(2,1)} fusion(bf16[4096,1024]{1,0:T(8,128)(2,1)} %constant_dynamic-update-slice_fusion.1, bf16[4096,512]{1,0:T(8,128)(2,1)} %param.11), kind=kLoop, calls=%fused_computation.26 | loop fusion | bytes 8388608 | tf_op jit(solution)/shard_map/concatenate | solution.py:41
  12.7 4.9 %convolution_bitcast_fusion.2 = f32[1,128,1024]{2,1,0:T(8,128)S(1)} fusion(bf16[128,4096]{1,0:T(8,128)(2,1)S(1)} %copy-done.1, bf16[4096,1024]{1,0:T(8,128)(2,1)} %constant_dynamic-update-slice_fusion), kind=kOutput, calls=%fused_computation.3 | convolution fusion | flops 1073741824 | bytes 9961472 | tf_op jit(solution)/shard_map/dot_general | solution.py:44
  17.6 7.1 %collective-permute-done.2 = bf16[128,4096]{1,0:T(8,128)(2,1)S(1)} collective-permute-done((bf16[128,4096]{1,0:T(8,128)(2,1)}, bf16[128,4096]{1,0:T(8,128)(2,1)S(1)}, u32[]{:S(2)}, u32[]{:S(2)}) %collective-permute-start.2) | collective-permute-done | bytes 1048608 | tf_op jit(solution)/shard_map/ppermute | solution.py:23
  24.7 1.6 %collective-permute-start.3 = (bf16[64,4096]{1,0:T(8,128)(2,1)S(1)}, bf16[64,4096]{1,0:T(8,128)(2,1)S(1)}, u32[]{:S(2)}, u32[]{:S(2)}) collective-permute-start(bf16[64,4096]{1,0:T(8,128)(2,1)S(1)} %slice.64), channel_id=1, source_target_pairs={{0,4},{4,8},{8,12},{12,0},{1,5},{5,9},{9,13},{13,1},{2,6},{6,10},{... | collective-permute-start | bytes 1572872 | tf_op jit(solution)/shard_map/ppermute | solution.py:23
  26.4 1.7 %collective-permute-start.4 = (bf16[64,4096]{1,0:T(8,128)(2,1)S(1)}, bf16[64,4096]{1,0:T(8,128)(2,1)S(1)}, u32[]{:S(2)}, u32[]{:S(2)}) collective-permute-start(bf16[64,4096]{1,0:T(8,128)(2,1)S(1)} %slice.65), channel_id=1, source_target_pairs={{0,12},{4,0},{8,4},{12,8},{1,13},{5,1},{9,5},{13,9},{2,14},{6,2},{... | collective-permute-start | bytes 1572872 | tf_op jit(solution)/shard_map/ppermute | solution.py:23
  28.1 1.3 %convolution_bitcast_fusion = f32[1,128,1024]{2,1,0:T(8,128)S(1)} fusion(bf16[128,4096]{1,0:T(8,128)(2,1)S(1)} %collective-permute-done.2, bf16[4096,1024]{1,0:T(8,128)(2,1)S(1)} %copy-done), kind=kOutput, calls=%fused_computation.1 | convolution fusion | flops 1073741824 | bytes 9961472 | tf_op jit(solution)/shard_map/dot_general | solution.py:44
  29.4 1.3 %convolution_bitcast_fusion.1 = f32[1,128,1024]{2,1,0:T(8,128)S(1)} fusion(bf16[128,4096]{1,0:T(8,128)(2,1)S(1)} %collective-permute-done.1, bf16[4096,1024]{1,0:T(8,128)(2,1)S(1)} %copy-done), kind=kOutput, calls=%fused_computation.2 | convolution fusion | flops 1073741824 | bytes 9961472 | tf_op jit(solution)/shard_map/dot_general | solution.py:44
  30.7 6.5 %collective-permute-done.3 = bf16[64,4096]{1,0:T(8,128)(2,1)S(1)} collective-permute-done((bf16[64,4096]{1,0:T(8,128)(2,1)S(1)}, bf16[64,4096]{1,0:T(8,128)(2,1)S(1)}, u32[]{:S(2)}, u32[]{:S(2)}) %collective-permute-start.3) | collective-permute-done | bytes 524320 | tf_op jit(solution)/shard_map/ppermute | solution.py:23
  37.2 0.8 collective-permute-done.4
  38.0 1.3 %convolution_bitcast_fusion.3 = f32[1,128,1024]{2,1,0:T(8,128)S(1)} fusion(bf16[4096,1024]{1,0:T(8,128)(2,1)S(1)} %copy-done, bf16[64,4096]{1,0:T(8,128)(2,1)S(1)} %collective-permute-done.4, bf16[64,4096]{1,0:T(8,128)(2,1)S(1)} %collective-permute-done.3), kind=kOutput, calls=%fused_computation.4 | convolution fusion | flops 1075838976 | bytes 9961472 | tf_op jit(solution)/shard_map/dot_general | solution.py:44
  39.5 4.3 %collective-permute-start.5 = (f32[64,1024]{1,0:T(8,128)S(1)}, f32[64,1024]{1,0:T(8,128)S(1)}, u32[]{:S(2)}, u32[]{:S(2)}) collective-permute-start(f32[64,1024]{1,0:T(8,128)S(1)} %get-tuple-element.31), channel_id=1, source_target_pairs={{0,3},{1,0},{2,1},{3,2},{4,7},{5,4},{6,5},{7,6},{8,11},{9,8},{10,9... | collective-permute-start | bytes 786440 | tf_op jit(solution)/shard_map/ppermute | solution.py:23
  43.8 0.7 collective-permute-start
  44.5 1.1 %dynamic-slice_bitcast_fusion.1 = (f32[128,1024]{1,0:T(8,128)}, f32[128,1024]{1,0:T(8,128)}) fusion(f32[4,128,1024]{2,1,0:T(8,128)S(1)} %pad_maximum_fusion, s32[]{:T(128)S(6)} %select_n.39, s32[]{:T(128)S(6)} %select_n.44), kind=kLoop, calls=%fused_computation.12 | loop fusion | bytes 2097160 | tf_op jit(solution)/shard_map/jit(dynamic_index_in_dim)/squeeze | solution.py:57
  45.6 1.5 %collective-permute-done.5 = f32[64,1024]{1,0:T(8,128)S(1)} collective-permute-done((f32[64,1024]{1,0:T(8,128)S(1)}, f32[64,1024]{1,0:T(8,128)S(1)}, u32[]{:S(2)}, u32[]{:S(2)}) %collective-permute-start.5) | collective-permute-done | bytes 262176 | tf_op jit(solution)/shard_map/ppermute | solution.py:23
  47.1 3.1 %collective-permute-done.7 = f32[64,1024]{1,0:T(8,128)S(1)} collective-permute-done((f32[64,1024]{1,0:T(8,128)S(1)}, f32[64,1024]{1,0:T(8,128)S(1)}, u32[]{:S(2)}, u32[]{:S(2)}) %collective-permute-start.7) | collective-permute-done | bytes 262176 | tf_op jit(solution)/shard_map/ppermute | solution.py:23
  50.2 0.8 fusion.6
  51.1 1.5 %collective-permute-start.6 = (f32[128,1024]{1,0:T(8,128)}, f32[128,1024]{1,0:T(8,128)S(1)}, u32[]{:S(2)}, u32[]{:S(2)}) collective-permute-start(f32[128,1024]{1,0:T(8,128)} %get-tuple-element.29), channel_id=1, source_target_pairs={{0,3},{1,0},{2,1},{3,2},{4,7},{5,4},{6,5},{7,6},{8,11},{9,8},{10,9... | collective-permute-start | bytes 1572872 | tf_op jit(solution)/shard_map/ppermute | solution.py:23
  53.1 8.0 %collective-permute-done.6 = f32[128,1024]{1,0:T(8,128)S(1)} collective-permute-done((f32[128,1024]{1,0:T(8,128)}, f32[128,1024]{1,0:T(8,128)S(1)}, u32[]{:S(2)}, u32[]{:S(2)}) %collective-permute-start.6) | collective-permute-done | bytes 524320 | tf_op jit(solution)/shard_map/ppermute | solution.py:23
  61.0 3.0 %collective-permute-done.8 = f32[128,1024]{1,0:T(8,128)S(1)} collective-permute-done((f32[128,1024]{1,0:T(8,128)}, f32[128,1024]{1,0:T(8,128)S(1)}, u32[]{:S(2)}, u32[]{:S(2)}) %collective-permute-start.8) | collective-permute-done | bytes 524320 | tf_op jit(solution)/shard_map/ppermute | solution.py:23
  64.5 24.2 %all_to_all.5 = bf16[16,16,512]{2,1,0:T(8,128)(2,1)S(1)} all-to-all(bf16[16,16,512]{2,1,0:T(8,128)(2,1)S(1)} %bitcast.51), channel_id=1, replica_groups=mesh['batch'=16,'wx'=4,'wy'=4] {'batch'}, dimensions={0} | all-to-all | bytes 524288 | tf_op jit(solution)/shard_map/all_to_all | solution.py:69
  88.7 0.7 copy.9
  (20 shorter events, 1.1 us)
Async XLA Ops:
  0.0 24.7 %collective-permute-start.2 = (bf16[128,4096]{1,0:T(8,128)(2,1)}, bf16[128,4096]{1,0:T(8,128)(2,1)S(1)}, u32[]{:S(2)}, u32[]{:S(2)}) collective-permute-start(bf16[128,4096]{1,0:T(8,128)(2,1)} %param.8), channel_id=1, source_target_pairs={{0,4},{4,8},{8,12},{12,0},{1,5},{5,9},{9,13},{13,1},{2,6},{6,10},{... | collective-permute-start | bytes 3145736 | tf_op jit(solution)/shard_map/ppermute | solution.py:23
  2.1 24.2 %collective-permute-start.1 = (bf16[128,4096]{1,0:T(8,128)(2,1)}, bf16[128,4096]{1,0:T(8,128)(2,1)S(1)}, u32[]{:S(2)}, u32[]{:S(2)}) collective-permute-start(bf16[128,4096]{1,0:T(8,128)(2,1)} %param.8), channel_id=1, source_target_pairs={{0,12},{4,0},{8,4},{12,8},{1,13},{5,1},{9,5},{13,9},{2,14},{6,2},{... | collective-permute-start | bytes 3145736 | tf_op jit(solution)/shard_map/ppermute | solution.py:23
  8.1 4.6 %copy-start.1 = (bf16[128,4096]{1,0:T(8,128)(2,1)S(1)}, bf16[128,4096]{1,0:T(8,128)(2,1)}, u32[]{:S(2)}) copy-start(bf16[128,4096]{1,0:T(8,128)(2,1)} %param.8) | copy-start | bytes 3145732
  12.7 15.3 %copy-start = (bf16[4096,1024]{1,0:T(8,128)(2,1)S(1)}, bf16[4096,1024]{1,0:T(8,128)(2,1)}, u32[]{:S(2)}) copy-start(bf16[4096,1024]{1,0:T(8,128)(2,1)} %constant_dynamic-update-slice_fusion) | copy-start | bytes 25165828
  24.7 12.5 %collective-permute-start.3 = (bf16[64,4096]{1,0:T(8,128)(2,1)S(1)}, bf16[64,4096]{1,0:T(8,128)(2,1)S(1)}, u32[]{:S(2)}, u32[]{:S(2)}) collective-permute-start(bf16[64,4096]{1,0:T(8,128)(2,1)S(1)} %slice.64), channel_id=1, source_target_pairs={{0,4},{4,8},{8,12},{12,0},{1,5},{5,9},{9,13},{13,1},{2,6},{6,10},{... | collective-permute-start | bytes 1572872 | tf_op jit(solution)/shard_map/ppermute | solution.py:23
  26.4 11.6 %collective-permute-start.4 = (bf16[64,4096]{1,0:T(8,128)(2,1)S(1)}, bf16[64,4096]{1,0:T(8,128)(2,1)S(1)}, u32[]{:S(2)}, u32[]{:S(2)}) collective-permute-start(bf16[64,4096]{1,0:T(8,128)(2,1)S(1)} %slice.65), channel_id=1, source_target_pairs={{0,12},{4,0},{8,4},{12,8},{1,13},{5,1},{9,5},{13,9},{2,14},{6,2},{... | collective-permute-start | bytes 1572872 | tf_op jit(solution)/shard_map/ppermute | solution.py:23
  39.3 4.5 %copy-start.2 = (s32[128,1]{0,1:T(1,128)S(1)}, s32[128,1]{0,1:T(1,128)}, u32[]{:S(2)}) copy-start(s32[128,1]{0,1:T(1,128)} %param.9) | copy-start | bytes 1540
  39.5 7.6 %collective-permute-start.5 = (f32[64,1024]{1,0:T(8,128)S(1)}, f32[64,1024]{1,0:T(8,128)S(1)}, u32[]{:S(2)}, u32[]{:S(2)}) collective-permute-start(f32[64,1024]{1,0:T(8,128)S(1)} %get-tuple-element.31), channel_id=1, source_target_pairs={{0,3},{1,0},{2,1},{3,2},{4,7},{5,4},{6,5},{7,6},{8,11},{9,8},{10,9... | collective-permute-start | bytes 786440 | tf_op jit(solution)/shard_map/ppermute | solution.py:23
  43.8 6.4 %collective-permute-start.7 = (f32[64,1024]{1,0:T(8,128)S(1)}, f32[64,1024]{1,0:T(8,128)S(1)}, u32[]{:S(2)}, u32[]{:S(2)}) collective-permute-start(f32[64,1024]{1,0:T(8,128)S(1)} %get-tuple-element.32), channel_id=1, source_target_pairs={{0,1},{1,2},{2,3},{3,0},{4,5},{5,6},{6,7},{7,4},{8,9},{9,10},{10,1... | collective-permute-start | bytes 786440 | tf_op jit(solution)/shard_map/ppermute | solution.py:23
  43.8 8.8 %collective-permute-start = (s32[128,1]{0,1:T(1,128)S(1)}, s32[128,1]{0,1:T(1,128)S(1)}, u32[]{:S(2)}, u32[]{:S(2)}) collective-permute-start(s32[128,1]{0,1:T(1,128)S(1)} %copy-done.2), channel_id=1, source_target_pairs={{0,0},{1,4},{2,8},{3,12},{4,1},{5,5},{6,9},{7,13},{8,2},{9,6},{10,... | collective-permute-start | bytes 1544 | tf_op jit(solution)/shard_map/ppermute | solution.py:39
  51.1 10.0 %collective-permute-start.6 = (f32[128,1024]{1,0:T(8,128)}, f32[128,1024]{1,0:T(8,128)S(1)}, u32[]{:S(2)}, u32[]{:S(2)}) collective-permute-start(f32[128,1024]{1,0:T(8,128)} %get-tuple-element.29), channel_id=1, source_target_pairs={{0,3},{1,0},{2,1},{3,2},{4,7},{5,4},{6,5},{7,6},{8,11},{9,8},{10,9... | collective-permute-start | bytes 1572872 | tf_op jit(solution)/shard_map/ppermute | solution.py:23
  52.6 11.5 %collective-permute-start.8 = (f32[128,1024]{1,0:T(8,128)}, f32[128,1024]{1,0:T(8,128)S(1)}, u32[]{:S(2)}, u32[]{:S(2)}) collective-permute-start(f32[128,1024]{1,0:T(8,128)} %get-tuple-element.30), channel_id=1, source_target_pairs={{0,1},{1,2},{2,3},{3,0},{4,5},{5,6},{6,7},{7,4},{8,9},{9,10},{10,1... | collective-permute-start | bytes 1572872 | tf_op jit(solution)/shard_map/ppermute | solution.py:23
